TPU v7x, 256 devices: a whole 4x4x8 slice. The times are simulated.
256 devices in a mesh: dp: 8 (over x, core), seq: 32 (over z, y).
Axes of the slice: x: 4, y: 4, z: 8, core: 2. Of those that a mesh axis runs over, the one named last changes fastest.
Arguments:
- tokens: bfloat16 [32768, 2048], P(('dp', 'seq')), parts along dimension 0, may hold values from -6 to 6
- expert_ids: int32 [32768, 2], P(('dp', 'seq')), parts along dimension 0, may hold values from 0 to 31, all different within a row; in each aligned block of 128 rows (0 to 127, 128 to 255, ...) at most 16 rows name the same one
- router: bfloat16 [2048, 32], replicated, may hold values from -0.125 to 0.125
- w_gate: bfloat16 [32, 2048, 768], P('seq'), may hold values from -0.125 to 0.125
- w_up: bfloat16 [32, 2048, 768], P('seq'), may hold values from -0.125 to 0.125
- w_down: bfloat16 [32, 768, 2048], P('seq'), may hold values from -0.21875 to 0.21875
- spike_level: int32 [32, 768], P('seq'), may hold values from 1 to 8
- queries: bfloat16 [32768, 2048], P(('dp', 'seq')), parts along dimension 0, may hold values from -6 to 6
- key_vectors: bfloat16 [32768, 2048], P(('dp', 'seq')), parts along dimension 0, may hold values from -0.59765625 to 0.59765625
- log_decay: float32 [16, 32768], P(None, ('dp', 'seq')), parts along dimension 1, may hold values from -1 to 0
Outputs:
- expert_mix: bfloat16 [32768, 2048], P(('dp', 'seq')), parts along dimension 0
- attended: bfloat16 [32768, 2048], P(('dp', 'seq')), parts along dimension 0
There are 8 independent parts, one for each index of `dp`. A program takes and returns all parts, laid end to end along the dimension named above; an argument that names none is the same for every part. Nothing has to cross between parts.
Inputs may be any that keep to these rules, and one draw needn't show every extreme that they name: `expert_ids`: each row names two different experts; among the rows of one device no expert is named more than 16 times.
All inputs are finite; a program needn't handle non-finite values.
Results may differ from a plain program's by a relative error of at most 0.0066.
Values may be sent and summed in bfloat16 or wider, within the bound.
No kernel may reach another device: no remote copies, remote signals or barrier semaphores. Data moves between devices by JAX's collectives and lax.ppermute only.
A program may use at most 128 MiB of HBM per device.

v0:
```python
from functools import partial

import jax
import jax.numpy as jnp
from jax import lax
from jax.sharding import PartitionSpec as P


def entering(part, axis, combine, identity):
    place = lax.axis_index(axis)
    gathered = jax.tree.map(lambda a: lax.all_gather(a, axis), part)
    state = jax.tree.map(lambda a, e: jnp.zeros_like(a) + jnp.asarray(e, a.dtype), part, identity)

    def one(hop, state):
        return combine(
            state, jax.tree.map(lambda a: lax.dynamic_index_in_dim(a, hop, 0, False), gathered)
        )

    return lax.fori_loop(0, place, one, state)


def slot_ranks(id_rows, expert_total):
    flat_ids = id_rows.reshape(-1)
    one_hot = (flat_ids[:, None] == jnp.arange(expert_total, dtype=jnp.int32)[None, :]).astype(
        jnp.int32
    )
    running = jnp.cumsum(one_hot, axis=0)
    return jnp.sum(one_hot * running, axis=1) - 1


def expert_apply(token_rows, gate_matrix, up_matrix, down_matrix, levels):
    gate_values = jnp.dot(token_rows, gate_matrix, preferred_element_type=jnp.float32)
    up_values = jnp.dot(token_rows, up_matrix, preferred_element_type=jnp.float32)
    hidden = jax.nn.silu(gate_values) * up_values
    threshold = 0.125 * levels.astype(jnp.float32)
    spikes = (threshold * jnp.tanh(hidden / threshold)).astype(jnp.bfloat16)
    return jnp.dot(spikes, down_matrix, preferred_element_type=jnp.float32).astype(jnp.bfloat16)


def decayed_weights(query_heads, key_heads, decay_rows):
    cumulative = jnp.cumsum(decay_rows, axis=1)
    length = decay_rows.shape[1]
    scores = jnp.einsum("thd,shd->hts", query_heads, key_heads, preferred_element_type=jnp.float32)
    causal = jnp.arange(length)[:, None] >= jnp.arange(length)[None, :]
    spread = cumulative[:, :, None] - cumulative[:, None, :]
    decay = jnp.where(causal[None], jnp.exp(jnp.minimum(spread, 0.0)), 0.0)
    return ((scores * decay).astype(jnp.bfloat16), cumulative)


def combine_states(earlier, later):
    return (earlier[0] * later[0], later[0][:, None, None] * earlier[1] + later[1])


def body(
    tokens, expert_ids, router, w_gate, w_up, w_down, spike_level, queries, key_vectors, log_decay
):
    highest = lax.Precision.HIGHEST
    token_count = tokens.shape[0]
    width = tokens.shape[1]
    local_count = w_gate.shape[0]
    n_devices = lax.axis_size("seq")
    n_experts = router.shape[1]
    expert_quota = max(2, 4 * token_count // n_experts)
    heads = log_decay.shape[0]
    channel_width_per_group = queries.shape[1] // heads
    query_heads = queries.reshape(token_count, heads, channel_width_per_group)
    key_heads = key_vectors.reshape(token_count, heads, channel_width_per_group)
    logits = jnp.dot(tokens, router, preferred_element_type=jnp.float32)
    matches = (
        expert_ids[:, :, None] == jnp.arange(n_experts, dtype=jnp.int32)[None, None, :]
    ).astype(jnp.float32)
    picked = jnp.sum(logits[:, None, :] * matches, axis=2)
    gate_first = jax.nn.sigmoid(picked[:, 0] - picked[:, 1])
    gate_second = jax.nn.sigmoid(picked[:, 1] - picked[:, 0])
    slots = slot_ranks(expert_ids, n_experts)
    flat_ids = expert_ids.reshape(-1)
    position = flat_ids * expert_quota + slots
    all_tokens, all_ids = (
        lax.all_gather(tokens, "seq", axis=0, tiled=True),
        lax.all_gather(expert_ids, "seq", axis=0, tiled=True),
    )
    id_blocks = all_ids.reshape(n_devices, token_count, 2)
    block_slots = jax.vmap(partial(slot_ranks, expert_total=n_experts))(id_blocks)
    flat_all = id_blocks.reshape(n_devices, 2 * token_count)
    my_first = lax.axis_index("seq") * local_count
    local_ids = flat_all - my_first
    owned = (local_ids >= 0) & (local_ids < local_count)
    target = jnp.where(owned, local_ids * expert_quota + block_slots, local_count * expert_quota)
    entry_rows = (
        jnp.arange(n_devices, dtype=jnp.int32)[:, None] * token_count
        + jnp.arange(2 * token_count, dtype=jnp.int32)[None, :] // 2
        + 1
    )
    table = jnp.zeros((n_devices, local_count * expert_quota + 1), jnp.int32)
    table = table.at[jnp.arange(n_devices, dtype=jnp.int32)[:, None], target].set(entry_rows)
    table = table[:, : local_count * expert_quota]
    padded = jnp.concatenate([jnp.zeros((1, width), jnp.bfloat16), all_tokens], axis=0)
    receive_buffer = padded[table].reshape(n_devices, local_count, expert_quota, width)
    segment_piece = receive_buffer[:, 0]
    flat_rows = segment_piece.reshape(-1, width)
    computed = expert_apply(flat_rows, w_gate[0], w_up[0], w_down[0], spike_level[0])
    results = [computed.reshape(segment_piece.shape)]
    expert_out = jnp.stack(results, axis=1)
    returned = lax.all_to_all(expert_out, "seq", split_axis=0, concat_axis=0, tiled=True)
    returned = returned.reshape(n_experts * expert_quota, width)
    picked_rows = returned[position].reshape(token_count, 2, width).astype(jnp.float32)
    expert_mix = (
        gate_first[:, None] * picked_rows[:, 0] + gate_second[:, None] * picked_rows[:, 1]
    ).astype(jnp.bfloat16)
    weights_intra, cumulative = decayed_weights(query_heads, key_heads, log_decay)
    value_heads = expert_mix.reshape(token_count, heads, channel_width_per_group)
    intra = jnp.einsum(
        "hts,shd->thd", weights_intra, value_heads, preferred_element_type=jnp.float32
    )
    tail = jnp.exp(cumulative[:, -1:] - cumulative)
    local_state = jnp.einsum(
        "shd,she->hde",
        key_heads.astype(jnp.float32) * tail.T[:, :, None],
        value_heads.astype(jnp.float32),
        precision=highest,
    )
    total_decay = jnp.exp(cumulative[:, -1])
    identity = (
        jnp.ones((heads,), jnp.float32),
        jnp.zeros((heads, channel_width_per_group, channel_width_per_group), jnp.float32),
    )
    prefix_decay, carried = entering((total_decay, local_state), "seq", combine_states, identity)
    inter = jnp.exp(cumulative).T[:, :, None] * jnp.einsum(
        "thd,hde->the", query_heads.astype(jnp.float32), carried, precision=highest
    )
    total_out = intra + inter
    normed = total_out * lax.rsqrt(jnp.mean(total_out * total_out, axis=2, keepdims=True) + 1e-06)
    attended = normed.astype(jnp.bfloat16).reshape(token_count, heads * channel_width_per_group)
    return (expert_mix, attended)


def solution(mesh):
    in_specs = (
        P(("dp", "seq"), None),
        P(("dp", "seq"), None),
        P(),
        P("seq", None, None),
        P("seq", None, None),
        P("seq", None, None),
        P("seq", None),
        P(("dp", "seq"), None),
        P(("dp", "seq"), None),
        P(None, ("dp", "seq")),
    )
    out_specs = (P(("dp", "seq"), None), P(("dp", "seq"), None))
    return jax.shard_map(body, mesh=mesh, in_specs=in_specs, out_specs=out_specs, check_vma=False)
```

profile of v0, /device:TPU:248, one launch (start us, length us, event | category | flops | bytes accessed | tf_op | source)
XLA Modules:
  0.0 548.6 jit_solution(7808513849987049464)
XLA Ops:
  7.9 40.8 %all_gather.17 = s32[4096,2]{0,1:T(2,128)S(1)} all-gather(s32[128,2]{0,1:T(2,128)} %param.13), channel_id=1, replica_groups=mesh['dp'=8,'seq'=32] {'seq'}, dimensions={0}, use_global_device_ids=true | all-gather | bytes 33792 | tf_op jit(solution)/shard_map/all_gather | solution.py:80
  48.8 2.0 copy.98
  50.8 2.7 eq.66
  53.5 2.8 eq.70
  57.9 2.6 and.30
  60.5 2.0 copy.97
  62.5 2.8 mul.168
  66.5 35.2 %reduce-window.14 = s32[32,32,2,128]{3,1,2,0:T(8,128)} reduce-window(s32[32,32,2,128]{3,1,2,0:T(8,128)} %fusion.29, s32[]{:T(128)} %constant.77.clone.1), window={size=1x1x1x128 pad=0_0x0_0x0_0x127_0}, to_apply=%region_1.0 | reduce-window | flops 33292288 | bytes 2097156 | tf_op jit(solution)/shard_map/reduce-window
  101.7 2.7 slice.47
  104.4 1.7 copy.100
  106.1 1.5 fusion.15
  108.0 30.6 %scatter_custom_fusion = s32[544]{0:T(1024)S(1)} fusion(s32[8192]{0:T(1024)S(1)} %bitcast.144, s32[8192]{0:T(1024)S(1)} %bitcast.145, s32[]{:T(128)} %constant.77.clone.1), kind=kCustom, calls=%fused_computation.89 | custom fusion | bytes 2180
  138.9 7.7 %all-gather.5.cloned.1.call-done = bf16[4096,2048]{1,0:T(8,128)(2,1)} async-done(((bf16[128,2048]{1,0:T(8,128)(2,1)}), bf16[4096,2048]{1,0:T(8,128)(2,1)}) %all-gather.5.cloned.1.call-update) | async-done | bytes 16777232 | tf_op jit(solution)/shard_map/all_gather | solution.py:79
  146.6 15.1 %concatenate.6 = bf16[4097,2048]{1,0:T(8,128)(2,1)} pad(bf16[4096,2048]{1,0:T(8,128)(2,1)} %all-gather.5.cloned.1.call-done, bf16[]{:T(256)} %constant.76.clone.1), padding=1_0x0_0 | pad | bytes 33558528 | tf_op jit(solution)/shard_map/concatenate | solution.py:97
  161.7 13.2 %gather_fusion = bf16[512,2048]{1,0:T(8,128)(2,1)} fusion(bf16[4097,2048]{1,0:T(8,128)(2,1)} %concatenate.6, s32[1024]{0:T(1024)S(1)} %pad_clamp_fusion.1), kind=kCustom, calls=%fused_computation | custom fusion | bytes 4196352 | tf_op jit(solution)/shard_map/gather | solution.py:98
  174.9 5.5 fusion.4
  180.4 8.3 %fusion.6 = bf16[512,2048]{1,0:T(8,128)(2,1)} fusion(bf16[1,768,2048]{2,1,0:T(8,128)(2,1)S(1)} %copy-done, f32[512,768]{1,0:T(8,128)} %fusion.4, bf16[512,2048]{1,0:T(8,128)(2,1)} %gather_fusion, bf16[1,2048,768]{2,1,0:T(8,128)(2,1)} %param.16, f32[768]{0:T(1024)S(1)} %multiply_reduce_fusion.2), kind=kOutput, calls=%fused_computation.11 | convolution fusion | flops 3225419776 | bytes 12061696 | tf_op jit(solution)/shard_map/dot_general | solution.py:37
  188.7 9.3 %all-to-all-start = ((bf16[32,1,16,2048]{3,2,1,0:T(8,128)(2,1)}), bf16[32,1,16,2048]{3,2,1,0:T(8,128)(2,1)S(1)}, u32[]{:S(2)}, u32[]{:S(2)}) async-start(bf16[32,1,16,2048]{3,2,1,0:T(8,128)(2,1)} %bitcast.139), calls=%async_computation | async-start | bytes 4194304 | tf_op jit(solution)/shard_map/all_to_all | solution.py:104
  199.9 2.1 copy.124
  202.9 40.9 %all-to-all-done = bf16[32,1,16,2048]{3,2,1,0:T(8,128)(2,1)S(1)} async-done(((bf16[32,1,16,2048]{3,2,1,0:T(8,128)(2,1)}), bf16[32,1,16,2048]{3,2,1,0:T(8,128)(2,1)S(1)}, u32[]{:S(2)}, u32[]{:S(2)}) %all-to-all-start) | async-done | bytes 2097184 | tf_op jit(solution)/shard_map/all_to_all | solution.py:104
  245.2 2.4 reshape.243
  247.6 4.4 fusion.55
  253.0 1.6 fusion.22
  256.2 72.0 %all-reduce.1 = f32[512]{0:T(512)S(1)} all-reduce(f32[512]{0:T(512)S(1)} %dynamic-update-slice), channel_id=2, replica_groups=mesh['dp'=8,'seq'=32] {'seq'}, use_global_device_ids=true, to_apply=%add.1 | all-reduce | flops 512 | bytes 4096
  328.3 1.8 fusion.18
  330.1 155.4 %all-gather.7.cloned.1.call-done = f32[512,128,128]{2,1,0:T(8,128)} async-done(((f32[16,128,128]{2,1,0:T(8,128)}), f32[512,128,128]{2,1,0:T(8,128)}) %all-gather.7.cloned.1.call-update) | async-done | bytes 33554448 | tf_op jit(solution)/shard_map/all_gather | solution.py:11
  485.7 46.3 %while.12 = (s32[]{:T(128)}, f32[16,128,128]{2,1,0:T(8,128)S(1)}, s32[]{:T(128)}, f32[32,16]{1,0:T(8,128)S(1)}, f32[32,16,128,128]{3,2,1,0:T(8,128)}, /*index=5*/s32[]{:T(128)}, s32[]{:T(128)}, s32[]{:T(128)}) while((s32[]{:T(128)}, f32[16,128,128]{2,1,0:T(8,128)S(1)}, s32[]{:T(128)}, f32[32,16]{1,0:T(8,128)S(1)}, ...), condition=%wide.region_10.11_spmd, body=%wide.region_9.10_spmd.sunk | while | flops 524293 | bytes 3146055 | solution.py:19
  485.7 1.5 bitcast_add_fusion.3
  532.0 2.0 fusion.12
  534.0 3.6 multiply_reduce_fusion
  537.6 2.2 multiply_convert_fusion.1
  539.8 2.0 copy.119
  (144 shorter events, 54.0 us)
Async XLA Ops:
  7.2 173.2 %copy-start = (bf16[1,768,2048]{2,1,0:T(8,128)(2,1)S(1)}, bf16[1,768,2048]{2,1,0:T(8,128)(2,1)}, u32[]{:S(2)}) copy-start(bf16[1,768,2048]{2,1,0:T(8,128)(2,1)} %param.17) | copy-start | bytes 9437188
  7.2 139.5 %all-gather.5.cloned.1.call-start = ((), (), s32[]{:S(2)}) async-start(), calls=%async_computation.1 | async-start | bytes 17301504 | tf_op jit(solution)/shard_map/all_gather | solution.py:79
  101.7 6.0 %copy-start.11 = (s32[2]{0:T(128)S(1)}, s32[2]{0:T(128)}, u32[]{:S(2)}) copy-start(s32[2]{0:T(128)} %constant.99) | copy-start | bytes 28
  101.7 6.1 %copy-start.10 = (s32[2]{0:T(128)S(1)}, s32[2]{0:T(128)}, u32[]{:S(2)}) copy-start(s32[2]{0:T(128)} %constant.102) | copy-start | bytes 28
  101.7 37.2 %copy-start.9 = (s32[1,768]{1,0:T(1,128)S(1)}, s32[1,768]{1,0:T(1,128)}, u32[]{:S(2)}) copy-start(s32[1,768]{1,0:T(1,128)} %param.18) | copy-start | bytes 9220
  188.7 9.6 %copy-start.7 = (s32[128,2]{0,1:T(2,128)S(1)}, s32[128,2]{0,1:T(2,128)}, u32[]{:S(2)}) copy-start(s32[128,2]{0,1:T(2,128)} %param.13) | copy-start | bytes 3076
  188.7 13.2 %copy-start.8 = (f32[16,128]{1,0:T(8,128)S(1)}, f32[16,128]{1,0:T(8,128)}, u32[]{:S(2)}) copy-start(f32[16,128]{1,0:T(8,128)} %param.21) | copy-start | bytes 24580
  188.7 13.8 %copy-start.2 = (bf16[128,2048]{1,0:T(8,128)(2,1)S(1)}, bf16[128,2048]{1,0:T(8,128)(2,1)}, u32[]{:S(2)}) copy-start(bf16[128,2048]{1,0:T(8,128)(2,1)} %param.12) | copy-start | bytes 1572868
  188.7 13.8 %copy-start.6 = (bf16[2048,32]{0,1:T(8,128)(2,1)S(1)}, bf16[2048,32]{0,1:T(8,128)(2,1)}, u32[]{:S(2)}) copy-start(bf16[2048,32]{0,1:T(8,128)(2,1)} %param.14) | copy-start | bytes 393220
  188.7 55.1 %all-to-all-start = ((bf16[32,1,16,2048]{3,2,1,0:T(8,128)(2,1)}), bf16[32,1,16,2048]{3,2,1,0:T(8,128)(2,1)S(1)}, u32[]{:S(2)}, u32[]{:S(2)}) async-start(bf16[32,1,16,2048]{3,2,1,0:T(8,128)(2,1)} %bitcast.139), calls=%async_computation | async-start | bytes 4194304 | tf_op jit(solution)/shard_map/all_to_all | solution.py:104
  198.1 287.5 %all-gather.7.cloned.1.call-start = ((), (), s32[]{:S(2)}) async-start(), calls=%async_computation.2 | async-start | bytes 34603008 | tf_op jit(solution)/shard_map/all_gather | solution.py:11
  252.0 1.0 copy-start.4
  252.6 77.5 %copy-start.3 = (bf16[128,16,128]{2,0,1:T(8,128)(2,1)}, bf16[128,16,128]{2,0,1:T(8,128)(2,1)S(1)}, u32[]{:S(2)}) copy-start(bf16[128,16,128]{2,0,1:T(8,128)(2,1)S(1)} %fusion.21) | copy-start | bytes 1572868
  252.6 2.0 copy-start.12
  485.6 46.3 %copy-start.5 = (bf16[128,2048]{1,0:T(8,128)(2,1)S(1)}, bf16[128,2048]{1,0:T(8,128)(2,1)}, u32[]{:S(2)}) copy-start(bf16[128,2048]{1,0:T(8,128)(2,1)} %param.19) | copy-start | bytes 1572868
  534.0 7.8 %copy-start.1 = (bf16[1,768,2048]{2,1,0:T(8,128)(2,1)S(1)}, bf16[1,768,2048]{2,1,0:T(8,128)(2,1)}, u32[]{:S(2)}) copy-start(bf16[1,768,2048]{2,1,0:T(8,128)(2,1)} %param.17) | copy-start | bytes 9437188
Sparse Core Ops, SparseCore 0:
  10.6 136.0 all-gather.4
  254.8 230.6 all-gather.6
where the time goes:
time: 554 us; the launch traced here: 549 us
  waiting for transfers between devices  205 us (37%)
  blocking collectives  113 us (20%)
  local copies, waits for them, and re-layouts  95 us (17%)
  other arithmetic  89 us (16%)
  matrix products  21.3 us (4%)
  between operations  15.1 us (3%)
  starting transfers between devices  9.64 us (2%)
    all_gather x1, waiting for transfers between devices, entering(): gathered = jax.tree.map(lambda a: lax.all_gather(a, axis), part)  155 us
    unnamed x1, blocking collectives  72 us
    add x31, other arithmetic, combine_states(): later[0][:, None, None] * earlier[1] + later[1]  44.9 us
    all_to_all x1, waiting for transfers between devices, body(): lax.all_to_all(expert_out, 'seq', split_axis=0, concat_axis=0, tiled=True)  40.9 us
    all_gather x1, blocking collectives, body(): lax.all_gather(expert_ids, 'seq', axis=0, tiled=True)  40.8 us
    another operation x4, other arithmetic  35.9 us
    unnamed x35, local copies, waits for them, and re-layouts  34.1 us
    concatenate x1, local copies, waits for them, and re-layouts, body(): jnp.concatenate([jnp.zeros((1, width), jnp.bfloat16), all_tokens], axis=0)  15.1 us
  transfers between devices with their start and end apart: 3, of which 3 were waited for; matrix products, arithmetic and copies ran while one was open for 18% of the time, Pallas kernels for 0%

commit v1 on v0

v1 whole, which is shorter than its diff:
```python
import jax
import jax.numpy as jnp
from jax import lax
from jax.sharding import Mesh
from jax.sharding import PartitionSpec as P

SLOTS = 16
GROUP = 4


def expert_apply(token_rows, gate_matrix, up_matrix, down_matrix, levels):
    gate_values = jnp.dot(token_rows, gate_matrix, preferred_element_type=jnp.float32)
    up_values = jnp.dot(token_rows, up_matrix, preferred_element_type=jnp.float32)
    hidden = jax.nn.silu(gate_values) * up_values
    threshold = 0.125 * levels.astype(jnp.float32)
    spikes = (threshold * jnp.tanh(hidden / threshold)).astype(jnp.bfloat16)
    return jnp.dot(spikes, down_matrix, preferred_element_type=jnp.float32).astype(jnp.bfloat16)


def body(
    tokens, expert_ids, router, w_gate, w_up, w_down, spike_level, queries, key_vectors, log_decay
):
    highest = lax.Precision.HIGHEST
    seq_axes = ("sz", "sy")
    count, width = tokens.shape
    n_experts = router.shape[1]
    heads = log_decay.shape[0]
    hd = queries.shape[1] // heads
    n_sz = lax.axis_size("sz")
    n_sy = lax.axis_size("sy")
    zi = lax.axis_index("sz")
    yi = lax.axis_index("sy")
    quarter = heads // n_sy

    all_decay = lax.all_gather(log_decay, seq_axes, axis=0)
    group_keys = lax.all_gather(key_vectors, "sy", axis=0)

    logits = jnp.dot(tokens, router, preferred_element_type=jnp.float32)
    matches = (
        expert_ids[:, :, None] == jnp.arange(n_experts, dtype=jnp.int32)[None, None, :]
    ).astype(jnp.float32)
    picked = jnp.sum(logits[:, None, :] * matches, axis=2)
    gate_first = jax.nn.sigmoid(picked[:, 0] - picked[:, 1])
    gate_second = jax.nn.sigmoid(picked[:, 1] - picked[:, 0])

    flat_ids = expert_ids.reshape(-1)
    entries = flat_ids.shape[0]
    one_hot = (flat_ids[:, None] == jnp.arange(n_experts, dtype=jnp.int32)[None, :]).astype(
        jnp.bfloat16
    )
    lower = (
        jnp.arange(entries)[:, None] >= jnp.arange(entries)[None, :]
    ).astype(jnp.bfloat16)
    running = jnp.dot(lower, one_hot, preferred_element_type=jnp.float32)
    slots = (jnp.sum(running * one_hot.astype(jnp.float32), axis=1) - 1.0).astype(jnp.int32)
    dest = flat_ids * SLOTS + slots
    n_rows = n_experts * SLOTS
    select = (jnp.arange(n_rows, dtype=jnp.int32)[:, None] == dest[None, :]).astype(jnp.bfloat16)
    select_tok = select.reshape(n_rows, count, 2).sum(axis=2)
    send = jnp.dot(select_tok, tokens, preferred_element_type=jnp.float32).astype(jnp.bfloat16)

    recv = lax.all_to_all(send.reshape(n_experts, SLOTS, width), seq_axes, 0, 0, tiled=True)
    computed = expert_apply(
        recv.reshape(n_rows, width), w_gate[0], w_up[0], w_down[0], spike_level[0]
    )
    back = lax.all_to_all(computed.reshape(n_experts, SLOTS, width), seq_axes, 0, 0, tiled=True)
    back = back.reshape(n_rows, width)

    dest2 = dest.reshape(count, 2)
    pick0 = (dest2[:, 0:1] == jnp.arange(n_rows, dtype=jnp.int32)[None, :]).astype(jnp.bfloat16)
    pick1 = (dest2[:, 1:2] == jnp.arange(n_rows, dtype=jnp.int32)[None, :]).astype(jnp.bfloat16)
    first_out = jnp.dot(pick0, back, preferred_element_type=jnp.float32)
    second_out = jnp.dot(pick1, back, preferred_element_type=jnp.float32)
    expert_mix = (gate_first[:, None] * first_out + gate_second[:, None] * second_out).astype(
        jnp.bfloat16
    )

    query_heads = queries.reshape(count, heads, hd)
    key_heads = key_vectors.reshape(count, heads, hd)
    value_heads = expert_mix.reshape(count, heads, hd)
    cumulative = jnp.cumsum(log_decay, axis=1)
    scores = jnp.einsum("thd,shd->hts", query_heads, key_heads, preferred_element_type=jnp.float32)
    causal = jnp.arange(count)[:, None] >= jnp.arange(count)[None, :]
    spread = cumulative[:, :, None] - cumulative[:, None, :]
    decay = jnp.where(causal[None], jnp.exp(jnp.minimum(spread, 0.0)), 0.0)
    weights = (scores * decay).astype(jnp.bfloat16)
    intra = jnp.einsum("hts,shd->thd", weights, value_heads, preferred_element_type=jnp.float32)

    group_values = lax.all_gather(expert_mix, "sy", axis=0)
    all_cum = jnp.cumsum(all_decay, axis=2)
    all_total = jnp.exp(all_cum[:, :, -1])
    group_cum = lax.dynamic_slice_in_dim(all_cum, zi * n_sy, n_sy, axis=0)
    group_tail = jnp.exp(group_cum[:, :, -1:] - group_cum)
    gk = group_keys.reshape(n_sy, count, heads, hd).astype(jnp.float32)
    gk = gk * jnp.transpose(group_tail, (0, 2, 1))[:, :, :, None]
    gv = group_values.reshape(n_sy, count, heads, hd).astype(jnp.float32)
    local_states = jnp.einsum("gshd,gshe->ghde", gk, gv, precision=highest)
    group_total = lax.dynamic_slice_in_dim(all_total, zi * n_sy, n_sy, axis=0)

    run = jnp.zeros((heads, hd, hd), jnp.float32)
    prefixes = [run]
    for g in range(n_sy):
        run = group_total[g][:, None, None] * run + local_states[g]
        prefixes.append(run)
    prefixes = jnp.stack(prefixes)
    inside = lax.dynamic_index_in_dim(prefixes, yi, 0, False)
    group_state = prefixes[n_sy]

    piece = lax.dynamic_slice_in_dim(group_state, yi * quarter, quarter, axis=0)
    pieces = lax.all_gather(piece, "sz", axis=0)
    group_decay = jnp.prod(all_total.reshape(n_sz, n_sy, heads), axis=1)
    quarter_decay = lax.dynamic_slice_in_dim(group_decay, yi * quarter, quarter, axis=1)
    run = jnp.zeros((quarter, hd, hd), jnp.float32)
    entering = [run]
    for g in range(n_sz - 1):
        run = quarter_decay[g][:, None, None] * run + pieces[g]
        entering.append(run)
    entering = jnp.stack(entering)
    mine = lax.dynamic_index_in_dim(entering, zi, 0, False)
    carried_groups = lax.all_gather(mine, "sy", axis=0).reshape(heads, hd, hd)

    lead = [jnp.ones((heads,), jnp.float32)]
    for g in range(n_sy - 1):
        lead.append(lead[-1] * group_total[g])
    lead = lax.dynamic_index_in_dim(jnp.stack(lead), yi, 0, False)
    carried = lead[:, None, None] * carried_groups + inside

    inter = jnp.exp(cumulative).T[:, :, None] * jnp.einsum(
        "thd,hde->the", query_heads.astype(jnp.float32), carried, precision=highest
    )
    total_out = intra + inter
    normed = total_out * lax.rsqrt(jnp.mean(total_out * total_out, axis=2, keepdims=True) + 1e-06)
    attended = normed.astype(jnp.bfloat16).reshape(count, heads * hd)
    return (expert_mix, attended)


def solution(mesh):
    n_dp = mesh.shape["dp"]
    n_seq = mesh.shape["seq"]
    inner = Mesh(mesh.devices.reshape(n_dp, n_seq // GROUP, GROUP), ("dp", "sz", "sy"))
    rows = ("dp", "sz", "sy")
    in_specs = (
        P(rows, None),
        P(rows, None),
        P(),
        P(("sz", "sy"), None, None),
        P(("sz", "sy"), None, None),
        P(("sz", "sy"), None, None),
        P(("sz", "sy"), None),
        P(rows, None),
        P(rows, None),
        P(None, rows),
    )
    out_specs = (P(rows, None), P(rows, None))
    return jax.shard_map(body, mesh=inner, in_specs=in_specs, out_specs=out_specs, check_vma=False)
```

time: 554 us -> 319 us (0.58)
  the two profiles are of different devices: /device:TPU:248 before, /device:TPU:36 now
where the time goes in v1:
time: 319 us; the launch traced here: 318 us
  waiting for transfers between devices  160 us (50%)
  blocking collectives  47.9 us (15%)
  matrix products  28.6 us (9%)
  other arithmetic  26.9 us (8%)
  local copies, waits for them, and re-layouts  22.3 us (7%)
  starting transfers between devices  18.3 us (6%)
  between operations  14.1 us (4%)
    all_to_all x1, waiting for transfers between devices, body(): lax.all_to_all(send.reshape(n_experts, SLOTS, width), seq_axes, 0, 0, til...  49.7 us
    all_gather x1, blocking collectives, body(): all_decay = lax.all_gather(log_decay, seq_axes, axis=0)  47.9 us
    all_to_all x1, waiting for transfers between devices, body(): lax.all_to_all(computed.reshape(n_experts, SLOTS, width), seq_axes, 0, 0,...  47.5 us
    all_gather x1, waiting for transfers between devices, body(): pieces = lax.all_gather(piece, 'sz', axis=0)  37.9 us
    all_gather x1, waiting for transfers between devices, body(): carried_groups = lax.all_gather(mine, 'sy', axis=0).reshape(heads, hd, hd)  24.2 us
    unnamed x34, local copies, waits for them, and re-layouts  12.9 us
    all_to_all x1, starting transfers between devices, body(): lax.all_to_all(send.reshape(n_experts, SLOTS, width), seq_axes, 0, 0, til...  11.5 us
    unnamed x11, other arithmetic  10.8 us
  transfers between devices with their start and end apart: 6, of which 4 were waited for; matrix products, arithmetic and copies ran while one was open for 8% of the time, Pallas kernels for 0%

profile of v1, /device:TPU:36, one launch (start us, length us, event | category | flops | bytes accessed | tf_op | source)
XLA Modules:
  0.0 318.3 jit_solution(4407985878649111779)
XLA Ops:
  7.2 0.9 copy.70
  9.5 3.0 convolution_convert_fusion
  12.5 11.5 %all-to-all-start = ((bf16[32,16,2048]{2,1,0:T(8,128)(2,1)}), bf16[32,16,2048]{2,1,0:T(8,128)(2,1)}, u32[]{:S(2)}, u32[]{:S(2)}) async-start(bf16[32,16,2048]{2,1,0:T(8,128)(2,1)} %bitcast.186), calls=%async_computation | async-start | bytes 4194304 | tf_op jit(solution)/shard_map/all_to_all | solution.py:62
  24.1 49.7 %all-to-all-done = bf16[32,16,2048]{2,1,0:T(8,128)(2,1)} async-done(((bf16[32,16,2048]{2,1,0:T(8,128)(2,1)}), bf16[32,16,2048]{2,1,0:T(8,128)(2,1)}, u32[]{:S(2)}, u32[]{:S(2)}) %all-to-all-start) | async-done | bytes 2097184 | tf_op jit(solution)/shard_map/all_to_all | solution.py:62
  73.8 5.5 %fusion.6 = f32[512,768]{1,0:T(8,128)} fusion(bf16[512,2048]{1,0:T(8,128)(2,1)} %bitcast.3, bf16[1,2048,768]{2,1,0:T(8,128)(2,1)} %param.13), kind=kOutput, calls=%fused_computation.7 | convolution fusion | flops 1610612736 | bytes 6815744 | tf_op jit(solution)/shard_map/dot_general | solution.py:12
  79.2 8.3 %fusion.8 = bf16[512,2048]{1,0:T(8,128)(2,1)} fusion(bf16[1,768,2048]{2,1,0:T(8,128)(2,1)S(1)} %copy-done, f32[512,768]{1,0:T(8,128)} %fusion.6, bf16[512,2048]{1,0:T(8,128)(2,1)} %bitcast.3, bf16[1,2048,768]{2,1,0:T(8,128)(2,1)} %param.14, f32[768]{0:T(1024)S(1)} %multiply_reduce_fusion.1), kind=kOutput, calls=%fused_computation.10 | convolution fusion | flops 3225419776 | bytes 12061696 | tf_op jit(solution)/shard_map/dot_general | solution.py:17
  87.5 6.6 %all-to-all-start.1 = ((bf16[32,16,2048]{2,1,0:T(8,128)(2,1)}), bf16[32,16,2048]{2,1,0:T(8,128)(2,1)S(1)}, u32[]{:S(2)}, u32[]{:S(2)}) async-start(bf16[32,16,2048]{2,1,0:T(8,128)(2,1)} %bitcast.189), calls=%async_computation.1 | async-start | bytes 4194304 | tf_op jit(solution)/shard_map/all_to_all | solution.py:66
  95.3 47.5 %all-to-all-done.1 = bf16[32,16,2048]{2,1,0:T(8,128)(2,1)S(1)} async-done(((bf16[32,16,2048]{2,1,0:T(8,128)(2,1)}), bf16[32,16,2048]{2,1,0:T(8,128)(2,1)S(1)}, u32[]{:S(2)}, u32[]{:S(2)}) %all-to-all-start.1) | async-done | bytes 2097184 | tf_op jit(solution)/shard_map/all_to_all | solution.py:66
  143.3 1.3 fusion.12
  144.7 47.9 %all-gather = f32[512,128]{1,0:T(8,128)S(1)} all-gather(f32[16,128]{1,0:T(8,128)S(1)} %copy-done.9), channel_id=2, replica_groups=mesh['dp'=8,'sz'=8,'sy'=4] {'sz','sy'}, dimensions={0}, use_global_device_ids=true | all-gather | bytes 270336 | tf_op jit(solution)/shard_map/all_gather | solution.py:35
  192.7 9.1 %reduce_window_sum.23 = f32[32,16,128]{2,1,0:T(8,128)S(1)} reduce-window(f32[32,16,128]{2,1,0:T(8,128)S(1)} %bitcast.190, f32[]{:T(128)} %constant.20.clone.1), window={size=1x1x128 pad=0_0x0_0x127_0}, to_apply=%region_4.5 | reduce-window | flops 8323072 | bytes 524292 | tf_op jit(solution)/shard_map/jit(cumsum)/reduce_window_sum | solution.py:90
  202.6 1.1 broadcast_dynamic-update-slice_fusion
  203.8 2.1 convert_bitcast_fusion
  205.9 3.0 copy.84
  208.9 5.4 %copy.75 = f32[4,128,16,128]{1,3,2,0:T(8,128)} copy(f32[4,128,16,128]{3,2,1,0:T(8,128)} %bitcast.184) | data formatting | bytes 8388608 | tf_op jit(solution)/shard_map/convert_element_type | solution.py:94
  214.2 2.4 copy.85
  217.0 2.6 fusion
  220.9 2.3 copy-done.6
  223.2 0.8 dynamic-slice_add_fusion
  225.0 37.9 %all-gather.15.cloned.1.call-done = f32[32,128,128]{2,1,0:T(8,128)} async-done(((f32[4,128,128]{2,1,0:T(8,128)}), f32[32,128,128]{2,1,0:T(8,128)}) %all-gather.15.cloned.1.call-update) | async-done | bytes 2097168 | tf_op jit(solution)/shard_map/all_gather | solution.py:110
  262.9 1.9 fusion.57
  264.7 1.8 fusion.61
  266.6 1.9 constant_dynamic-update-slice_fusion.3
  271.0 0.8 fusion.48
  271.8 1.7 constant_dynamic-slice_fusion
  274.0 1.0 copy.81
  275.0 24.2 %all-gather.9.cloned.1.call-done = f32[4,4,128,128]{3,2,1,0:T(8,128)} async-done(((f32[1,4,128,128]{3,2,1,0:T(8,128)}), f32[4,4,128,128]{3,2,1,0:T(8,128)}) %all-gather.9.cloned.1.call-update) | async-done | bytes 1048592 | tf_op jit(solution)/shard_map/all_gather | solution.py:120
  299.2 1.4 bitcast_multiply_fusion
  300.6 3.2 %fusion.18 = f32[128,16,128]{0,2,1:T(8,128)} fusion(f32[16,128,128]{2,1,0:T(8,128)S(1)} %bitcast_multiply_fusion, f32[5,16,128,128]{3,2,1,0:T(8,128)} %copy-done.6, s32[]{:T(128)S(6)} %select_n.29, f32[128,16]{0,1:T(8,128)S(1)} %exponential_bitcast_fusion.1, bf16[128,2048]{1,0:T(8,128)(2,1)S(1)} %copy-done.7), kind=kOutput, calls=%fused_computation.22 | convolution fusion | flops 403177472 | bytes 3678212 | tf_op jit(solution)/shard_map/thd,hde->the/dot_general | solution.py:128
  303.8 3.7 %multiply_reduce_fusion = (f32[128,16]{0,1:T(8,128)S(1)}, f32[128,16,128]{0,2,1:T(8,128)}) fusion(f32[128,16,128]{0,2,1:T(8,128)} %fusion.18, bf16[128,16,128]{0,2,1:T(8,128)(2,1)} %bitcast.193, f32[16,128]{1,0:T(8,128)S(1)} %reduce_window_sum.22, pred[128,128]{1,0:T(8,128)(4,1)S(1)} %iota_compare_fusion.7, bf16[128,2048]{1,0:T(8,128)(2,1)} %param.18, ...), kind=kOutput, calls=%fused_computation.30 | convolution fusion | flops 136312832 | bytes 3702784 | tf_op jit(solution)/shard_map/hts,shd->thd/dot_general | solution.py:87
  307.5 2.1 multiply_convert_fusion.1
  309.7 2.0 copy.79
  (78 shorter events, 9.3 us)
Async XLA Ops:
  7.2 72.1 %copy-start = (bf16[1,768,2048]{2,1,0:T(8,128)(2,1)S(1)}, bf16[1,768,2048]{2,1,0:T(8,128)(2,1)}, u32[]{:S(2)}) copy-start(bf16[1,768,2048]{2,1,0:T(8,128)(2,1)} %param.15) | copy-start | bytes 9437188
  12.5 11.6 %copy-start.11 = (s32[1,768]{1,0:T(1,128)S(1)}, s32[1,768]{1,0:T(1,128)}, u32[]{:S(2)}) copy-start(s32[1,768]{1,0:T(1,128)} %param.16) | copy-start | bytes 9220
  12.5 61.3 %all-to-all-start = ((bf16[32,16,2048]{2,1,0:T(8,128)(2,1)}), bf16[32,16,2048]{2,1,0:T(8,128)(2,1)}, u32[]{:S(2)}, u32[]{:S(2)}) async-start(bf16[32,16,2048]{2,1,0:T(8,128)(2,1)} %bitcast.186), calls=%async_computation | async-start | bytes 4194304 | tf_op jit(solution)/shard_map/all_to_all | solution.py:62
  87.5 7.4 %copy-start.5 = (bf16[128,2048]{1,0:T(8,128)(2,1)S(1)}, bf16[128,2048]{1,0:T(8,128)(2,1)}, u32[]{:S(2)}) copy-start(bf16[128,2048]{1,0:T(8,128)(2,1)} %param.10) | copy-start | bytes 1572868
  87.5 7.4 %copy-start.8 = (bf16[2048,32]{0,1:T(8,128)(2,1)S(1)}, bf16[2048,32]{0,1:T(8,128)(2,1)}, u32[]{:S(2)}) copy-start(bf16[2048,32]{0,1:T(8,128)(2,1)} %param.12) | copy-start | bytes 393220
  87.5 7.7 %copy-start.10 = (s32[128,2]{0,1:T(2,128)S(1)}, s32[128,2]{0,1:T(2,128)}, u32[]{:S(2)}) copy-start(s32[128,2]{0,1:T(2,128)} %param.11) | copy-start | bytes 3076
  87.5 55.3 %all-to-all-start.1 = ((bf16[32,16,2048]{2,1,0:T(8,128)(2,1)}), bf16[32,16,2048]{2,1,0:T(8,128)(2,1)S(1)}, u32[]{:S(2)}, u32[]{:S(2)}) async-start(bf16[32,16,2048]{2,1,0:T(8,128)(2,1)} %bitcast.189), calls=%async_computation.1 | async-start | bytes 4194304 | tf_op jit(solution)/shard_map/all_to_all | solution.py:66
  94.1 109.6 %all-gather.11.cloned.1.call-start = ((), (), s32[]{:S(2)}) async-start(), calls=%async_computation.3 | async-start | bytes 2621440 | tf_op jit(solution)/shard_map/all_gather | solution.py:36
  94.9 119.4 %all-gather.13.cloned.1.call-start = ((), (), s32[]{:S(2)}) async-start(), calls=%async_computation.4 | async-start | bytes 2621440 | tf_op jit(solution)/shard_map/all_gather | solution.py:89
  143.3 1.4 copy-start.9
  144.7 118.2 %all-gather.15.cloned.1.call-start = ((), (), s32[]{:S(2)}) async-start(), calls=%async_computation.5 | async-start | bytes 2359296 | tf_op jit(solution)/shard_map/all_gather | solution.py:110
  214.2 2.8 copy-start.2
  214.2 5.5 %slice-start = ((s8[5242880]{0:T(1024)(128)(4,1)}), s8[4194304]{0:T(1024)(128)(4,1)S(1)}, s32[]{:S(2)}) async-start(s8[5242880]{0:T(1024)(128)(4,1)} %bitcast.191), calls=%async_computation.6 | async-start | bytes 8388608
  217.0 2.7 slice-start.1
  220.9 2.3 copy-start.6
  224.1 75.1 %all-gather.9.cloned.1.call-start = ((), (), s32[]{:S(2)}) async-start(), calls=%async_computation.2 | async-start | bytes 1310720 | tf_op jit(solution)/shard_map/all_gather | solution.py:120
  262.9 5.7 %copy-start.3 = (f32[32,128,128]{2,1,0:T(8,128)S(1)}, f32[32,128,128]{2,1,0:T(8,128)}, u32[]{:S(2)}) copy-start(f32[32,128,128]{2,1,0:T(8,128)} %all-gather.15.cloned.1.call-done) | copy-start | bytes 6291460
  269.3 4.6 %copy-start.4 = (bf16[128,2048]{1,0:T(8,128)(2,1)S(1)}, bf16[128,2048]{1,0:T(8,128)(2,1)}, u32[]{:S(2)}) copy-start(bf16[128,2048]{1,0:T(8,128)(2,1)} %fusion.12) | copy-start | bytes 1572868
  271.8 28.8 %copy-start.7 = (bf16[128,2048]{1,0:T(8,128)(2,1)S(1)}, bf16[128,2048]{1,0:T(8,128)(2,1)}, u32[]{:S(2)}) copy-start(bf16[128,2048]{1,0:T(8,128)(2,1)} %param.17) | copy-start | bytes 1572868
  303.8 7.9 %copy-start.1 = (bf16[1,768,2048]{2,1,0:T(8,128)(2,1)S(1)}, bf16[1,768,2048]{2,1,0:T(8,128)(2,1)}, u32[]{:S(2)}) copy-start(bf16[1,768,2048]{2,1,0:T(8,128)(2,1)} %param.15) | copy-start | bytes 9437188
Sparse Core Ops, SparseCore 0:
  96.8 47.1 all-gather.10
  146.4 32.4 all-gather.12
  224.2 38.6 all-gather.14
  273.7 25.4 all-gather.8

commit v2 on v1

--- a/solution.py
+++ b/solution.py
@@ -32,8 +32,24 @@
     yi = lax.axis_index("sy")
     quarter = heads // n_sy
 
-    all_decay = lax.all_gather(log_decay, seq_axes, axis=0)
-    group_keys = lax.all_gather(key_vectors, "sy", axis=0)
+    qw = quarter * hd
+    flat_decay = log_decay.reshape(n_sy, 1, quarter * count)
+    decay_hi = lax.reduce_precision(flat_decay, exponent_bits=8, mantissa_bits=7)
+    rest = flat_decay - decay_hi
+    decay_mid = lax.reduce_precision(rest, exponent_bits=8, mantissa_bits=7)
+    decay_lo = rest - decay_mid
+    decay_parts = jnp.concatenate([decay_hi, decay_mid, decay_lo], axis=1).astype(jnp.bfloat16)
+    q_split = queries.reshape(count, n_sy, qw).transpose(1, 0, 2)
+    k_split = key_vectors.reshape(count, n_sy, qw).transpose(1, 0, 2)
+    pad_rows = (-(2 * count + 3)) % 16
+    packed = jnp.concatenate(
+        [q_split, k_split, decay_parts, jnp.zeros((n_sy, pad_rows, qw), jnp.bfloat16)], axis=1
+    )
+    got = lax.all_to_all(packed, "sy", 0, 0, tiled=True)
+    group_q = got[:, :count].reshape(n_sy, count, quarter, hd)
+    group_k = got[:, count : 2 * count].reshape(n_sy, count, quarter, hd)
+    parts = got[:, 2 * count : 2 * count + 3].astype(jnp.float32)
+    group_decay = (parts[:, 0] + parts[:, 1] + parts[:, 2]).reshape(n_sy, quarter, count)
 
     logits = jnp.dot(tokens, router, preferred_element_type=jnp.float32)
     matches = (
@@ -75,62 +91,56 @@
         jnp.bfloat16
     )
 
-    query_heads = queries.reshape(count, heads, hd)
-    key_heads = key_vectors.reshape(count, heads, hd)
-    value_heads = expert_mix.reshape(count, heads, hd)
-    cumulative = jnp.cumsum(log_decay, axis=1)
-    scores = jnp.einsum("thd,shd->hts", query_heads, key_heads, preferred_element_type=jnp.float32)
+    v_split = expert_mix.reshape(count, n_sy, qw).transpose(1, 0, 2)
+    group_v = lax.all_to_all(v_split, "sy", 0, 0, tiled=True).reshape(n_sy, count, quarter, hd)
+    cumulative = jnp.cumsum(group_decay, axis=2)
+    scores = jnp.einsum(
+        "bthd,bshd->bhts", group_q, group_k, preferred_element_type=jnp.float32
+    )
     causal = jnp.arange(count)[:, None] >= jnp.arange(count)[None, :]
-    spread = cumulative[:, :, None] - cumulative[:, None, :]
-    decay = jnp.where(causal[None], jnp.exp(jnp.minimum(spread, 0.0)), 0.0)
+    spread = cumulative[:, :, :, None] - cumulative[:, :, None, :]
+    decay = jnp.where(causal[None, None], jnp.exp(jnp.minimum(spread, 0.0)), 0.0)
     weights = (scores * decay).astype(jnp.bfloat16)
-    intra = jnp.einsum("hts,shd->thd", weights, value_heads, preferred_element_type=jnp.float32)
+    intra = jnp.einsum("bhts,bshd->bthd", weights, group_v, preferred_element_type=jnp.float32)
 
-    group_values = lax.all_gather(expert_mix, "sy", axis=0)
-    all_cum = jnp.cumsum(all_decay, axis=2)
-    all_total = jnp.exp(all_cum[:, :, -1])
-    group_cum = lax.dynamic_slice_in_dim(all_cum, zi * n_sy, n_sy, axis=0)
-    group_tail = jnp.exp(group_cum[:, :, -1:] - group_cum)
-    gk = group_keys.reshape(n_sy, count, heads, hd).astype(jnp.float32)
-    gk = gk * jnp.transpose(group_tail, (0, 2, 1))[:, :, :, None]
-    gv = group_values.reshape(n_sy, count, heads, hd).astype(jnp.float32)
-    local_states = jnp.einsum("gshd,gshe->ghde", gk, gv, precision=highest)
-    group_total = lax.dynamic_slice_in_dim(all_total, zi * n_sy, n_sy, axis=0)
+    tail = jnp.exp(cumulative[:, :, -1:] - cumulative)
+    scaled_k = group_k.astype(jnp.float32) * jnp.transpose(tail, (0, 2, 1))[:, :, :, None]
+    local_states = jnp.einsum(
+        "bshd,bshe->bhde", scaled_k, group_v.astype(jnp.float32), precision=highest
+    )
+    block_total = jnp.exp(cumulative[:, :, -1])
 
-    run = jnp.zeros((heads, hd, hd), jnp.float32)
-    prefixes = [run]
-    for g in range(n_sy):
-        run = group_total[g][:, None, None] * run + local_states[g]
-        prefixes.append(run)
-    prefixes = jnp.stack(prefixes)
-    inside = lax.dynamic_index_in_dim(prefixes, yi, 0, False)
-    group_state = prefixes[n_sy]
+    run = jnp.zeros((quarter, hd, hd), jnp.float32)
+    lead = jnp.ones((quarter,), jnp.float32)
+    inside, leads = [], []
+    for b in range(n_sy):
+        inside.append(run)
+        leads.append(lead)
+        run = block_total[b][:, None, None] * run + local_states[b]
+        lead = lead * block_total[b]
+    group_state, group_span = run, lead
 
-    piece = lax.dynamic_slice_in_dim(group_state, yi * quarter, quarter, axis=0)
-    pieces = lax.all_gather(piece, "sz", axis=0)
-    group_decay = jnp.prod(all_total.reshape(n_sz, n_sy, heads), axis=1)
-    quarter_decay = lax.dynamic_slice_in_dim(group_decay, yi * quarter, quarter, axis=1)
+    decay_row = jnp.zeros((8, hd), jnp.float32).at[0, :quarter].set(group_span)
+    piece_packed = jnp.concatenate([group_state.reshape(quarter * hd, hd), decay_row], axis=0)
+    pieces_packed = lax.all_gather(piece_packed, "sz", axis=0)
+    pieces = pieces_packed[:, : quarter * hd].reshape(n_sz, quarter, hd, hd)
+    spans = pieces_packed[:, quarter * hd, :quarter]
     run = jnp.zeros((quarter, hd, hd), jnp.float32)
     entering = [run]
     for g in range(n_sz - 1):
-        run = quarter_decay[g][:, None, None] * run + pieces[g]
+        run = spans[g][:, None, None] * run + pieces[g]
         entering.append(run)
-    entering = jnp.stack(entering)
-    mine = lax.dynamic_index_in_dim(entering, zi, 0, False)
-    carried_groups = lax.all_gather(mine, "sy", axis=0).reshape(heads, hd, hd)
+    before = lax.dynamic_index_in_dim(jnp.stack(entering), zi, 0, False)
 
-    lead = [jnp.ones((heads,), jnp.float32)]
-    for g in range(n_sy - 1):
-        lead.append(lead[-1] * group_total[g])
-    lead = lax.dynamic_index_in_dim(jnp.stack(lead), yi, 0, False)
-    carried = lead[:, None, None] * carried_groups + inside
-
-    inter = jnp.exp(cumulative).T[:, :, None] * jnp.einsum(
-        "thd,hde->the", query_heads.astype(jnp.float32), carried, precision=highest
+    carried = jnp.stack(leads)[:, :, None, None] * before[None] + jnp.stack(inside)
+    inter = jnp.transpose(jnp.exp(cumulative), (0, 2, 1))[:, :, :, None] * jnp.einsum(
+        "bthd,bhde->bthe", group_q.astype(jnp.float32), carried, precision=highest
     )
     total_out = intra + inter
-    normed = total_out * lax.rsqrt(jnp.mean(total_out * total_out, axis=2, keepdims=True) + 1e-06)
-    attended = normed.astype(jnp.bfloat16).reshape(count, heads * hd)
+    normed = total_out * lax.rsqrt(jnp.mean(total_out * total_out, axis=3, keepdims=True) + 1e-06)
+    pieces_out = normed.astype(jnp.bfloat16).reshape(n_sy, count, qw)
+    mine = lax.all_to_all(pieces_out, "sy", 0, 0, tiled=True)
+    attended = mine.transpose(1, 0, 2).reshape(count, heads * hd)
     return (expert_mix, attended)
 
 

time: 319 us -> 244 us (0.76)
  waiting for transfers between devices: 160 us -> 117 us
  blocking collectives: 47.9 us -> 12.3 us
  other arithmetic: 26.9 us -> 7.86 us
  local copies, waits for them, and re-layouts: 22.3 us -> 32.5 us
  starting transfers between devices: 18.3 us -> 27.2 us
    all_gather x1 -> x0, blocking collectives: 47.9 us -> none  [body(): all_decay = lax.all_gather(log_decay, seq_axes, axis=0)]
    all_gather x4 -> x1, waiting for transfers between devices: 62.2 us -> 34.3 us  [body(): pieces_packed = lax.all_gather(piece_packed, 'sz', axis=0)]
    all_to_all x1, waiting for transfers between devices: 49.7 us -> 34 us  [body(): lax.all_to_all(send.reshape(n_experts, SLOTS, width), seq_axes, 0, 0, til...]
    all_to_all x0 -> x1, blocking collectives: none -> 12.3 us  [body(): mine = lax.all_to_all(pieces_out, 'sy', 0, 0, tiled=True)]
    unnamed x11 -> x6, other arithmetic: 10.8 us -> 0.64 us
    another operation x5 -> x4, other arithmetic: 10.8 us -> 1.41 us  [the longest x1 1.23 us: body(): cumulative = jnp.cumsum(group_decay, axis=2)]
    all_to_all x0 -> x2, waiting for transfers between devices: none -> 8.92 us  [the longest x1 7.89 us: body(): lax.all_to_all(v_split, 'sy', 0, 0, tiled=True)]
    all_to_all x0 -> x2, starting transfers between devices: none -> 8.53 us  [the longest x1 4.28 us: body(): got = lax.all_to_all(packed, 'sy', 0, 0, tiled=True)]
  transfers between devices with their start and end apart: 6 -> 5, of which waited for: 4 -> 5; matrix products, arithmetic and copies ran while one was open for 8% -> 17% of each run, Pallas kernels for 0% -> 0%
where the time goes in v2:
time: 244 us; the launch traced here: 242 us
  waiting for transfers between devices  117 us (48%)
  local copies, waits for them, and re-layouts  32.5 us (13%)
  matrix products  30.5 us (12%)
  starting transfers between devices  27.2 us (11%)
  between operations  14.3 us (6%)
  blocking collectives  12.3 us (5%)
  other arithmetic  7.86 us (3%)
    all_to_all x1, waiting for transfers between devices, body(): lax.all_to_all(computed.reshape(n_experts, SLOTS, width), seq_axes, 0, 0,...  40.3 us
    all_gather x1, waiting for transfers between devices, body(): pieces_packed = lax.all_gather(piece_packed, 'sz', axis=0)  34.3 us
    all_to_all x1, waiting for transfers between devices, body(): lax.all_to_all(send.reshape(n_experts, SLOTS, width), seq_axes, 0, 0, til...  34 us
    all_to_all x1, blocking collectives, body(): mine = lax.all_to_all(pieces_out, 'sy', 0, 0, tiled=True)  12.3 us
    all_to_all x1, starting transfers between devices, body(): lax.all_to_all(send.reshape(n_experts, SLOTS, width), seq_axes, 0, 0, til...  11.5 us
    unnamed x26, local copies, waits for them, and re-layouts  11.4 us
    dot_general x1, matrix products, expert_apply(): jnp.dot(spikes, down_matrix, preferred_element_type=jnp.float32)  8.3 us
    all_to_all x1, waiting for transfers between devices, body(): lax.all_to_all(v_split, 'sy', 0, 0, tiled=True)  7.89 us
  transfers between devices with their start and end apart: 5, of which 5 were waited for; matrix products, arithmetic and copies ran while one was open for 17% of the time, Pallas kernels for 0%

profile of v2, /device:TPU:36, one launch (start us, length us, event | category | flops | bytes accessed | tf_op | source)
XLA Modules:
  0.0 242.1 jit_solution(4830420917282225969)
XLA Ops:
  9.5 3.1 %convolution_convert_fusion = bf16[512,2048]{1,0:T(8,128)(2,1)} fusion(bf16[512,128]{1,0:T(8,128)(2,1)S(1)} %fusion.43, bf16[128,2048]{1,0:T(8,128)(2,1)} %param.12), kind=kOutput, calls=%fused_computation.6 | convolution fusion | flops 269484032 | bytes 2752512 | tf_op jit(solution)/shard_map/dot_general | solution.py:76
  12.5 11.5 %all-to-all-start = ((bf16[32,16,2048]{2,1,0:T(8,128)(2,1)}), bf16[32,16,2048]{2,1,0:T(8,128)(2,1)}, u32[]{:S(2)}, u32[]{:S(2)}) async-start(bf16[32,16,2048]{2,1,0:T(8,128)(2,1)} %bitcast.134), calls=%async_computation | async-start | bytes 4194304 | tf_op jit(solution)/shard_map/all_to_all | solution.py:78
  24.1 1.1 copy.129
  25.2 1.1 copy.130
  27.3 2.0 copy.127
  29.3 2.0 copy.128
  32.2 5.0 %concatenate.11 = bf16[4,272,512]{1,2,0:T(8,128)(2,1)} concatenate(bf16[4,128,512]{1,2,0:T(8,128)(2,1)} %bitcast.147, bf16[4,128,512]{1,2,0:T(8,128)(2,1)} %bitcast.148, bf16[4,1,512]{1,2,0:T(8,128)(2,1)} %copy.129, bf16[4,1,512]{1,2,0:T(8,128)(2,1)} %copy.130, bf16[4,1,512]{1,2,0:T(8,128)(2,1)} %copy.131, bf16[4,13,512]{1,2,0:T(8,128)(2,1)} %broadcast_in_dim.8), dimensions={1} | concatenate | bytes 2228224 | tf_op jit(solution)/shard_map/concatenate | solution.py:45
  37.3 2.5 %copy.132 = bf16[4,272,512]{2,1,0:T(8,128)(2,1)} copy(bf16[4,272,512]{1,2,0:T(8,128)(2,1)} %concatenate.11) | data formatting | bytes 2228224 | tf_op jit(solution)/shard_map/concatenate | solution.py:45
  39.8 34.0 %all-to-all-done = bf16[32,16,2048]{2,1,0:T(8,128)(2,1)} async-done(((bf16[32,16,2048]{2,1,0:T(8,128)(2,1)}), bf16[32,16,2048]{2,1,0:T(8,128)(2,1)}, u32[]{:S(2)}, u32[]{:S(2)}) %all-to-all-start) | async-done | bytes 2097184 | tf_op jit(solution)/shard_map/all_to_all | solution.py:78
  73.8 4.3 %all-to-all-start.3 = ((bf16[4,272,512]{2,1,0:T(8,128)(2,1)}), bf16[4,272,512]{2,1,0:T(8,128)(2,1)}, u32[]{:S(2)}, u32[]{:S(2)}) async-start(bf16[4,272,512]{2,1,0:T(8,128)(2,1)} %copy.132), calls=%async_computation.3 | async-start | bytes 2228224 | tf_op jit(solution)/shard_map/all_to_all | solution.py:48
  78.1 5.5 %fusion.4 = f32[512,768]{1,0:T(8,128)} fusion(bf16[512,2048]{1,0:T(8,128)(2,1)} %bitcast.3, bf16[1,2048,768]{2,1,0:T(8,128)(2,1)} %param.15), kind=kOutput, calls=%fused_computation.4 | convolution fusion | flops 1610612736 | bytes 6815744 | tf_op jit(solution)/shard_map/dot_general | solution.py:12
  83.6 8.3 %fusion.6 = bf16[512,2048]{1,0:T(8,128)(2,1)} fusion(bf16[1,768,2048]{2,1,0:T(8,128)(2,1)S(1)} %copy-done, f32[512,768]{1,0:T(8,128)} %fusion.4, bf16[512,2048]{1,0:T(8,128)(2,1)} %bitcast.3, bf16[1,2048,768]{2,1,0:T(8,128)(2,1)} %param.16, f32[768]{0:T(1024)S(1)} %multiply_reduce_fusion.1), kind=kOutput, calls=%fused_computation.7 | convolution fusion | flops 3225419776 | bytes 12061696 | tf_op jit(solution)/shard_map/dot_general | solution.py:17
  92.9 7.0 %all-to-all-start.1 = ((bf16[32,16,2048]{2,1,0:T(8,128)(2,1)}), bf16[32,16,2048]{2,1,0:T(8,128)(2,1)}, u32[]{:S(2)}, u32[]{:S(2)}) async-start(bf16[32,16,2048]{2,1,0:T(8,128)(2,1)} %bitcast.150), calls=%async_computation.1 | async-start | bytes 4194304 | tf_op jit(solution)/shard_map/all_to_all | solution.py:82
  99.9 1.3 fusion.61
  101.3 2.2 fusion.59
  103.5 2.0 copy.148
  106.4 1.2 reduce_window_sum.11
  107.8 40.3 %all-to-all-done.1 = bf16[32,16,2048]{2,1,0:T(8,128)(2,1)} async-done(((bf16[32,16,2048]{2,1,0:T(8,128)(2,1)}), bf16[32,16,2048]{2,1,0:T(8,128)(2,1)}, u32[]{:S(2)}, u32[]{:S(2)}) %all-to-all-start.1) | async-done | bytes 2097184 | tf_op jit(solution)/shard_map/all_to_all | solution.py:82
  148.1 2.1 convolution_multiply_fusion.1
  150.2 2.1 fusion.10
  153.9 4.3 %all-to-all-start.2 = ((bf16[4,128,512]{2,1,0:T(8,128)(2,1)}), bf16[4,128,512]{2,1,0:T(8,128)(2,1)}, u32[]{:S(2)}, u32[]{:S(2)}) async-start(bf16[4,128,512]{2,1,0:T(8,128)(2,1)} %bitcast.151), calls=%async_computation.2 | async-start | bytes 1048576 | tf_op jit(solution)/shard_map/all_to_all | solution.py:95
  158.5 7.9 %all-to-all-done.2 = bf16[4,128,512]{2,1,0:T(8,128)(2,1)} async-done(((bf16[4,128,512]{2,1,0:T(8,128)(2,1)}), bf16[4,128,512]{2,1,0:T(8,128)(2,1)}, u32[]{:S(2)}, u32[]{:S(2)}) %all-to-all-start.2) | async-done | bytes 524320 | tf_op jit(solution)/shard_map/all_to_all | solution.py:95
  166.4 2.1 copy.126
  168.4 2.4 fusion.24
  173.6 2.0 copy.147
  175.7 34.3 %all-gather.3.cloned.1.call-done = f32[4160,128]{1,0:T(8,128)} async-done(((f32[520,128]{1,0:T(8,128)}), f32[4160,128]{1,0:T(8,128)}) %all-gather.3.cloned.1.call-update) | async-done | bytes 2129936 | tf_op jit(solution)/shard_map/all_gather | solution.py:125
  210.0 1.7 fusion.58
  214.1 2.1 fusion.14
  216.1 3.5 %multiply_reduce_fusion = (f32[4,128,4]{1,2,0:T(4,128)S(1)}, f32[4,128,4,128]{1,3,2,0:T(8,128)}) fusion(f32[4,128,4,128]{1,3,2,0:T(8,128)} %fusion.14, bf16[4,128,4,128]{1,3,2,0:T(8,128)(2,1)} %bitcast.138, bf16[4,128,4,128]{1,3,2,0:T(8,128)(2,1)} %bitcast.145, bf16[4,128,4,128]{1,3,2,0:T(8,128)(2,1)} %bitcast.136, f32[4,4,128]{2,1,0:T(4,128)S(1)} %reduce_window_sum.11, ...), kind=kOutput, calls=%fused_computation.29 | convolution fusion | flops 136312832 | bytes 3702784 | tf_op jit(solution)/shard_map/bhts,bshd->bthd/dot_general | solution.py:104
  219.6 1.3 multiply_convert_fusion.1
  221.0 12.3 %all_to_all.25 = bf16[4,128,512]{1,2,0:T(8,128)(2,1)} all-to-all(bf16[4,128,512]{1,2,0:T(8,128)(2,1)S(1)} %bitcast.149), channel_id=1, replica_groups=mesh['dp'=8,'sz'=8,'sy'=4] {'sy'}, dimensions={0} | all-to-all | bytes 1048576 | tf_op jit(solution)/shard_map/all_to_all | solution.py:142
  233.3 2.0 copy.146
  (66 shorter events, 13.4 us)
Async XLA Ops:
  7.2 76.4 %copy-start = (bf16[1,768,2048]{2,1,0:T(8,128)(2,1)S(1)}, bf16[1,768,2048]{2,1,0:T(8,128)(2,1)}, u32[]{:S(2)}) copy-start(bf16[1,768,2048]{2,1,0:T(8,128)(2,1)} %param.17) | copy-start | bytes 9437188
  12.5 11.6 %copy-start.8 = (f32[16,128]{1,0:T(8,128)S(1)}, f32[16,128]{1,0:T(8,128)}, u32[]{:S(2)}) copy-start(f32[16,128]{1,0:T(8,128)} %param.21) | copy-start | bytes 24580
  12.5 61.3 %all-to-all-start = ((bf16[32,16,2048]{2,1,0:T(8,128)(2,1)}), bf16[32,16,2048]{2,1,0:T(8,128)(2,1)}, u32[]{:S(2)}, u32[]{:S(2)}) async-start(bf16[32,16,2048]{2,1,0:T(8,128)(2,1)} %bitcast.134), calls=%async_computation | async-start | bytes 4194304 | tf_op jit(solution)/shard_map/all_to_all | solution.py:78
  37.3 2.5 %copy-start.9 = (s32[1,768]{1,0:T(1,128)S(1)}, s32[1,768]{1,0:T(1,128)}, u32[]{:S(2)}) copy-start(s32[1,768]{1,0:T(1,128)} %param.18) | copy-start | bytes 9220
  73.8 19.1 %all-to-all-start.3 = ((bf16[4,272,512]{2,1,0:T(8,128)(2,1)}), bf16[4,272,512]{2,1,0:T(8,128)(2,1)}, u32[]{:S(2)}, u32[]{:S(2)}) async-start(bf16[4,272,512]{2,1,0:T(8,128)(2,1)} %copy.132), calls=%async_computation.3 | async-start | bytes 2228224 | tf_op jit(solution)/shard_map/all_to_all | solution.py:48
  92.9 7.0 %copy-start.6 = (bf16[2048,32]{0,1:T(8,128)(2,1)S(1)}, bf16[2048,32]{0,1:T(8,128)(2,1)}, u32[]{:S(2)}) copy-start(bf16[2048,32]{0,1:T(8,128)(2,1)} %param.14) | copy-start | bytes 393220
  92.9 8.4 %copy-start.7 = (s32[128,2]{0,1:T(2,128)S(1)}, s32[128,2]{0,1:T(2,128)}, u32[]{:S(2)}) copy-start(s32[128,2]{0,1:T(2,128)} %param.13) | copy-start | bytes 3076
  92.9 55.2 %all-to-all-start.1 = ((bf16[32,16,2048]{2,1,0:T(8,128)(2,1)}), bf16[32,16,2048]{2,1,0:T(8,128)(2,1)}, u32[]{:S(2)}, u32[]{:S(2)}) async-start(bf16[32,16,2048]{2,1,0:T(8,128)(2,1)} %bitcast.150), calls=%async_computation.1 | async-start | bytes 4194304 | tf_op jit(solution)/shard_map/all_to_all | solution.py:82
  152.3 0.8 copy-start.2
  153.9 12.4 %all-to-all-start.2 = ((bf16[4,128,512]{2,1,0:T(8,128)(2,1)}), bf16[4,128,512]{2,1,0:T(8,128)(2,1)}, u32[]{:S(2)}, u32[]{:S(2)}) async-start(bf16[4,128,512]{2,1,0:T(8,128)(2,1)} %bitcast.151), calls=%async_computation.2 | async-start | bytes 1048576 | tf_op jit(solution)/shard_map/all_to_all | solution.py:95
  158.2 51.8 %all-gather.3.cloned.1.call-start = ((), (), s32[]{:S(2)}) async-start(), calls=%async_computation.5 | async-start | bytes 2396160 | tf_op jit(solution)/shard_map/all_gather | solution.py:125
  210.0 2.4 %copy-start.5 = (f32[8,4,128,128]{3,2,1,0:T(8,128)S(1)}, f32[8,4,128,128]{3,2,1,0:T(8,128)}, u32[]{:S(2)}) copy-start(f32[8,4,128,128]{3,2,1,0:T(8,128)} %broadcast_dynamic-update-slice_fusion) | copy-start | bytes 6291460
  212.9 1.0 copy-start.1
  212.9 1.1 copy-start.3
  212.9 1.2 copy-start.4
Sparse Core Ops, SparseCore 0:
  173.0 36.9 all-gather.2

commit v3 on v2

--- a/solution.py
+++ b/solution.py
@@ -17,6 +17,13 @@
     return jnp.dot(spikes, down_matrix, preferred_element_type=jnp.float32).astype(jnp.bfloat16)
 
 
+def split3(values):
+    hi = lax.reduce_precision(values, exponent_bits=8, mantissa_bits=7)
+    rest = values - hi
+    mid = lax.reduce_precision(rest, exponent_bits=8, mantissa_bits=7)
+    return [hi, mid, rest - mid]
+
+
 def body(
     tokens, expert_ids, router, w_gate, w_up, w_down, spike_level, queries, key_vectors, log_decay
 ):
@@ -29,27 +36,8 @@
     n_sz = lax.axis_size("sz")
     n_sy = lax.axis_size("sy")
     zi = lax.axis_index("sz")
-    yi = lax.axis_index("sy")
     quarter = heads // n_sy
-
     qw = quarter * hd
-    flat_decay = log_decay.reshape(n_sy, 1, quarter * count)
-    decay_hi = lax.reduce_precision(flat_decay, exponent_bits=8, mantissa_bits=7)
-    rest = flat_decay - decay_hi
-    decay_mid = lax.reduce_precision(rest, exponent_bits=8, mantissa_bits=7)
-    decay_lo = rest - decay_mid
-    decay_parts = jnp.concatenate([decay_hi, decay_mid, decay_lo], axis=1).astype(jnp.bfloat16)
-    q_split = queries.reshape(count, n_sy, qw).transpose(1, 0, 2)
-    k_split = key_vectors.reshape(count, n_sy, qw).transpose(1, 0, 2)
-    pad_rows = (-(2 * count + 3)) % 16
-    packed = jnp.concatenate(
-        [q_split, k_split, decay_parts, jnp.zeros((n_sy, pad_rows, qw), jnp.bfloat16)], axis=1
-    )
-    got = lax.all_to_all(packed, "sy", 0, 0, tiled=True)
-    group_q = got[:, :count].reshape(n_sy, count, quarter, hd)
-    group_k = got[:, count : 2 * count].reshape(n_sy, count, quarter, hd)
-    parts = got[:, 2 * count : 2 * count + 3].astype(jnp.float32)
-    group_decay = (parts[:, 0] + parts[:, 1] + parts[:, 2]).reshape(n_sy, quarter, count)
 
     logits = jnp.dot(tokens, router, preferred_element_type=jnp.float32)
     matches = (
@@ -75,24 +63,59 @@
     select_tok = select.reshape(n_rows, count, 2).sum(axis=2)
     send = jnp.dot(select_tok, tokens, preferred_element_type=jnp.float32).astype(jnp.bfloat16)
 
+    decay_parts = jnp.concatenate(split3(log_decay.reshape(n_sy, 1, quarter * count)), axis=1)
+    slot_pairs = slots.reshape(count, 2).astype(jnp.float32)
+    id_pairs = expert_ids.astype(jnp.float32)
+    fields = [id_pairs[:, 0], slot_pairs[:, 0], id_pairs[:, 1], slot_pairs[:, 1]]
+    fields += split3(gate_first) + split3(gate_second)
+    n_fields = len(fields)
+    info_rows = -(-(n_fields * count) // qw)
+    info = jnp.stack(fields).reshape(-1)
+    info = jnp.pad(info, (0, info_rows * qw - n_fields * count)).reshape(1, info_rows, qw)
+    info = jnp.broadcast_to(info, (n_sy, info_rows, qw))
+    q_split = queries.reshape(count, n_sy, qw).transpose(1, 0, 2)
+    k_split = key_vectors.reshape(count, n_sy, qw).transpose(1, 0, 2)
+    used = 2 * count + 3 + info_rows
+    packed = jnp.concatenate(
+        [
+            q_split,
+            k_split,
+            decay_parts.astype(jnp.bfloat16),
+            info.astype(jnp.bfloat16),
+            jnp.zeros((n_sy, (-used) % 16, qw), jnp.bfloat16),
+        ],
+        axis=1,
+    )
+    got = lax.all_to_all(packed, "sy", 0, 0, tiled=True)
+    group_q = got[:, :count].reshape(n_sy, count, quarter, hd)
+    group_k = got[:, count : 2 * count].reshape(n_sy, count, quarter, hd)
+    parts = got[:, 2 * count : 2 * count + 3].astype(jnp.float32)
+    group_decay = (parts[:, 0] + parts[:, 1] + parts[:, 2]).reshape(n_sy, quarter, count)
+    got_info = got[:, 2 * count + 3 : used].astype(jnp.float32).reshape(n_sy, info_rows * qw)
+    got_info = got_info[:, : n_fields * count].reshape(n_sy, n_fields, count)
+    g_first = (got_info[:, 4] + got_info[:, 5]) + got_info[:, 6]
+    g_second = (got_info[:, 7] + got_info[:, 8]) + got_info[:, 9]
+    row_first = (got_info[:, 0] * SLOTS + got_info[:, 1]).astype(jnp.int32)
+    row_second = (got_info[:, 2] * SLOTS + got_info[:, 3]).astype(jnp.int32)
+
     recv = lax.all_to_all(send.reshape(n_experts, SLOTS, width), seq_axes, 0, 0, tiled=True)
     computed = expert_apply(
         recv.reshape(n_rows, width), w_gate[0], w_up[0], w_down[0], spike_level[0]
     )
-    back = lax.all_to_all(computed.reshape(n_experts, SLOTS, width), seq_axes, 0, 0, tiled=True)
-    back = back.reshape(n_rows, width)
-
-    dest2 = dest.reshape(count, 2)
-    pick0 = (dest2[:, 0:1] == jnp.arange(n_rows, dtype=jnp.int32)[None, :]).astype(jnp.bfloat16)
-    pick1 = (dest2[:, 1:2] == jnp.arange(n_rows, dtype=jnp.int32)[None, :]).astype(jnp.bfloat16)
-    first_out = jnp.dot(pick0, back, preferred_element_type=jnp.float32)
-    second_out = jnp.dot(pick1, back, preferred_element_type=jnp.float32)
-    expert_mix = (gate_first[:, None] * first_out + gate_second[:, None] * second_out).astype(
+    outgoing = computed.reshape(n_sz, n_sy, SLOTS, n_sy, qw).transpose(0, 3, 1, 2, 4)
+    back = lax.all_to_all(outgoing.reshape(n_sz * n_sy, -1), seq_axes, 0, 0, tiled=True)
+    table = back.reshape(n_experts, n_sy, SLOTS, qw).transpose(1, 0, 2, 3)
+    table = table.reshape(n_sy, n_rows, qw)
+    lanes = jnp.arange(n_rows, dtype=jnp.int32)[None, None, :]
+    pick0 = (row_first[:, :, None] == lanes).astype(jnp.bfloat16)
+    pick1 = (row_second[:, :, None] == lanes).astype(jnp.bfloat16)
+    first_out = jnp.einsum("btr,brc->btc", pick0, table, preferred_element_type=jnp.float32)
+    second_out = jnp.einsum("btr,brc->btc", pick1, table, preferred_element_type=jnp.float32)
+    mix_q = (g_first[:, :, None] * first_out + g_second[:, :, None] * second_out).astype(
         jnp.bfloat16
     )
 
-    v_split = expert_mix.reshape(count, n_sy, qw).transpose(1, 0, 2)
-    group_v = lax.all_to_all(v_split, "sy", 0, 0, tiled=True).reshape(n_sy, count, quarter, hd)
+    group_v = mix_q.reshape(n_sy, count, quarter, hd)
     cumulative = jnp.cumsum(group_decay, axis=2)
     scores = jnp.einsum(
         "bthd,bshd->bhts", group_q, group_k, preferred_element_type=jnp.float32
@@ -120,11 +143,14 @@
         lead = lead * block_total[b]
     group_state, group_span = run, lead
 
-    decay_row = jnp.zeros((8, hd), jnp.float32).at[0, :quarter].set(group_span)
-    piece_packed = jnp.concatenate([group_state.reshape(quarter * hd, hd), decay_row], axis=0)
+    span_rows = jnp.zeros((16, hd), jnp.float32).at[0:3, :quarter].set(jnp.stack(split3(group_span)))
+    piece_packed = jnp.concatenate(
+        [group_state.reshape(quarter * hd, hd), span_rows], axis=0
+    ).astype(jnp.bfloat16)
     pieces_packed = lax.all_gather(piece_packed, "sz", axis=0)
-    pieces = pieces_packed[:, : quarter * hd].reshape(n_sz, quarter, hd, hd)
-    spans = pieces_packed[:, quarter * hd, :quarter]
+    pieces = pieces_packed[:, : quarter * hd].astype(jnp.float32).reshape(n_sz, quarter, hd, hd)
+    span_parts = pieces_packed[:, quarter * hd : quarter * hd + 3, :quarter].astype(jnp.float32)
+    spans = (span_parts[:, 0] + span_parts[:, 1]) + span_parts[:, 2]
     run = jnp.zeros((quarter, hd, hd), jnp.float32)
     entering = [run]
     for g in range(n_sz - 1):
@@ -138,9 +164,10 @@
     )
     total_out = intra + inter
     normed = total_out * lax.rsqrt(jnp.mean(total_out * total_out, axis=3, keepdims=True) + 1e-06)
-    pieces_out = normed.astype(jnp.bfloat16).reshape(n_sy, count, qw)
-    mine = lax.all_to_all(pieces_out, "sy", 0, 0, tiled=True)
-    attended = mine.transpose(1, 0, 2).reshape(count, heads * hd)
+    att_q = normed.astype(jnp.bfloat16).reshape(n_sy, count, qw)
+    home = lax.all_to_all(jnp.stack([mix_q, att_q], axis=1), "sy", 0, 0, tiled=True)
+    expert_mix = home[:, 0].transpose(1, 0, 2).reshape(count, width)
+    attended = home[:, 1].transpose(1, 0, 2).reshape(count, heads * hd)
     return (expert_mix, attended)
 
 

time: 244 us -> 279 us (1.14)
  other arithmetic: 7.86 us -> 34 us
  local copies, waits for them, and re-layouts: 32.5 us -> 58.3 us
  waiting for transfers between devices: 117 us -> 107 us
  matrix products: 30.5 us -> 24.2 us
  starting transfers between devices: 27.2 us -> 23.7 us
    all_to_all x0 -> x2, other arithmetic: none -> 25.7 us  [body(): lax.all_to_all(outgoing.reshape(n_sz * n_sy, -1), seq_axes, 0, 0, tiled=T...]
    unnamed x26 -> x40, local copies, waits for them, and re-layouts: 11.4 us -> 27 us
    all_to_all x2 -> x1, waiting for transfers between devices: 48.2 us -> 42.1 us  [body(): lax.all_to_all(outgoing.reshape(n_sz * n_sy, -1), seq_axes, 0, 0, tiled=T...]
    all_to_all x1 -> x2, local copies, waits for them, and re-layouts: 2.06 us -> 6.77 us  [body(): lax.all_to_all(outgoing.reshape(n_sz * n_sy, -1), seq_axes, 0, 0, tiled=T...]
    reshape x3 -> x4, local copies, waits for them, and re-layouts: 2.89 us -> 6.62 us  [the longest x2 6.6 us: body(): computed.reshape(n_sz, n_sy, SLOTS, n_sy, qw).transpose(0, 3, 1, 2, 4)]
    all_to_all x2 -> x1, starting transfers between devices: 11.3 us -> 7.83 us  [body(): lax.all_to_all(outgoing.reshape(n_sz * n_sy, -1), seq_axes, 0, 0, tiled=T...]
    all_to_all x1, waiting for transfers between devices: 34 us -> 30.7 us  [body(): lax.all_to_all(send.reshape(n_experts, SLOTS, width), seq_axes, 0, 0, til...]
    dot_general x2, matrix products: 4.16 us -> 1.02 us  [the longest x1 0.52 us: body(): jnp.einsum('btr,brc->btc', pick1, table, preferred_element_type=jnp.float32)]
  transfers between devices with their start and end apart: 5 -> 4, of which waited for: 5 -> 3; matrix products, arithmetic and copies ran while one was open for 17% -> 23% of each run, Pallas kernels for 0% -> 0%
where the time goes in v3:
time: 279 us; the launch traced here: 276 us
  waiting for transfers between devices  107 us (38%)
  local copies, waits for them, and re-layouts  58.3 us (21%)
  other arithmetic  34 us (12%)
  matrix products  24.2 us (9%)
  starting transfers between devices  23.7 us (8%)
  blocking collectives  15 us (5%)
  between operations  14.5 us (5%)
    all_to_all x1, waiting for transfers between devices, body(): lax.all_to_all(outgoing.reshape(n_sz * n_sy, -1), seq_axes, 0, 0, tiled=T...  42.1 us
    all_gather x1, waiting for transfers between devices, body(): pieces_packed = lax.all_gather(piece_packed, 'sz', axis=0)  34 us
    all_to_all x1, waiting for transfers between devices, body(): lax.all_to_all(send.reshape(n_experts, SLOTS, width), seq_axes, 0, 0, til...  30.7 us
    unnamed x40, local copies, waits for them, and re-layouts  27 us
    all_to_all x2, other arithmetic, body(): lax.all_to_all(outgoing.reshape(n_sz * n_sy, -1), seq_axes, 0, 0, tiled=T...  25.7 us
    all_to_all x1, blocking collectives, body(): lax.all_to_all(jnp.stack([mix_q, att_q], axis=1), 'sy', 0, 0, tiled=True)  15 us
    all_to_all x1, starting transfers between devices, body(): lax.all_to_all(send.reshape(n_experts, SLOTS, width), seq_axes, 0, 0, til...  11.5 us
    dot_general x1, matrix products, expert_apply(): jnp.dot(spikes, down_matrix, preferred_element_type=jnp.float32)  8.3 us
  transfers between devices with their start and end apart: 4, of which 3 were waited for; matrix products, arithmetic and copies ran while one was open for 23% of the time, Pallas kernels for 0%

profile of v3, /device:TPU:36, one launch (start us, length us, event | category | flops | bytes accessed | tf_op | source)
XLA Modules:
  0.0 276.5 jit_solution(1553401449605919123)
XLA Ops:
  9.5 3.1 %convolution_convert_fusion = bf16[512,2048]{1,0:T(8,128)(2,1)} fusion(bf16[512,128]{1,0:T(8,128)(2,1)S(1)} %fusion.50, bf16[128,2048]{1,0:T(8,128)(2,1)} %param.12), kind=kOutput, calls=%fused_computation.6 | convolution fusion | flops 269484032 | bytes 2752512 | tf_op jit(solution)/shard_map/dot_general | solution.py:64
  12.6 11.5 %all-to-all-start.1 = ((bf16[32,16,2048]{2,1,0:T(8,128)(2,1)}), bf16[32,16,2048]{2,1,0:T(8,128)(2,1)}, u32[]{:S(2)}, u32[]{:S(2)}) async-start(bf16[32,16,2048]{2,1,0:T(8,128)(2,1)} %bitcast.183), calls=%async_computation.1 | async-start | bytes 4194304 | tf_op jit(solution)/shard_map/all_to_all | solution.py:101
  24.2 1.3 fusion.74
  27.1 1.1 copy.179
  29.3 2.0 copy.174
  31.3 2.0 copy.175
  35.1 5.6 %concatenate.23 = bf16[4,272,512]{1,2,0:T(8,128)(2,1)} concatenate(bf16[4,128,512]{1,2,0:T(8,128)(2,1)} %bitcast.192, bf16[4,128,512]{1,2,0:T(8,128)(2,1)} %bitcast.193, bf16[4,1,512]{1,2,0:T(8,128)(2,1)} %copy.178, bf16[4,1,512]{1,2,0:T(8,128)(2,1)} %copy.179, bf16[4,1,512]{1,2,0:T(8,128)(2,1)} %copy.180, bf16[4,3,512]{1,2,0:T(8,128)(2,1)} %broadcast_in_dim.10, ...), dimensions={1} | concatenate | bytes 2228224 | tf_op jit(solution)/shard_map/concatenate | solution.py:79
  40.7 2.5 copy.181
  43.2 30.7 %all-to-all-done.1 = bf16[32,16,2048]{2,1,0:T(8,128)(2,1)} async-done(((bf16[32,16,2048]{2,1,0:T(8,128)(2,1)}), bf16[32,16,2048]{2,1,0:T(8,128)(2,1)}, u32[]{:S(2)}, u32[]{:S(2)}) %all-to-all-start.1) | async-done | bytes 2097184 | tf_op jit(solution)/shard_map/all_to_all | solution.py:101
  73.9 4.3 %all-to-all-start = ((bf16[4,272,512]{2,1,0:T(8,128)(2,1)}), bf16[4,272,512]{2,1,0:T(8,128)(2,1)}, u32[]{:S(2)}, u32[]{:S(2)}) async-start(bf16[4,272,512]{2,1,0:T(8,128)(2,1)} %copy.181), calls=%async_computation | async-start | bytes 2228224 | tf_op jit(solution)/shard_map/all_to_all | solution.py:89
  78.1 5.5 %fusion.4 = f32[512,768]{1,0:T(8,128)} fusion(bf16[512,2048]{1,0:T(8,128)(2,1)} %bitcast.12, bf16[1,2048,768]{2,1,0:T(8,128)(2,1)} %param.15), kind=kOutput, calls=%fused_computation.4 | convolution fusion | flops 1610612736 | bytes 6815744 | tf_op jit(solution)/shard_map/dot_general | solution.py:12
  83.6 8.3 %fusion.6 = bf16[512,2048]{1,0:T(8,128)(2,1)} fusion(bf16[1,768,2048]{2,1,0:T(8,128)(2,1)S(1)} %copy-done, f32[512,768]{1,0:T(8,128)} %fusion.4, bf16[512,2048]{1,0:T(8,128)(2,1)} %bitcast.12, bf16[1,2048,768]{2,1,0:T(8,128)(2,1)} %param.16, f32[768]{0:T(1024)S(1)} %multiply_reduce_fusion.1), kind=kOutput, calls=%fused_computation.7 | convolution fusion | flops 3225419776 | bytes 12061696 | tf_op jit(solution)/shard_map/dot_general | solution.py:17
  91.9 4.5 %reshape.743 = bf16[8,4,16,4,512]{4,3,2,1,0:T(4,128)(2,1)} reshape(bf16[512,2048]{1,0:T(8,128)(2,1)} %fusion.6) | data formatting | bytes 4194304 | tf_op jit(solution)/shard_map/reshape | solution.py:105
  96.4 2.1 copy.223
  98.5 6.3 %all_to_all.20 = bf16[32,1,32768]{2,1,0:T(2,128)(2,1)} reshape(bf16[8,4,4,16,512]{4,3,2,1,0:T(8,128)(2,1)S(1)} %bitcast.182) | data formatting | bytes 4194304 | tf_op jit(solution)/shard_map/all_to_all | solution.py:106
  105.3 13.2 %reduce.12 = bf16[32,32768]{1,0:T(8,128)(2,1)S(1)} reduce(bf16[32,1,32768]{2,1,0:T(2,128)(2,1)} %all_to_all.20, bf16[]{:T(256)} %broadcast.391), dimensions={1}, to_apply=%all_to_all.20.reduce_sub_computation | reduce | bytes 4194306 | tf_op jit(solution)/shard_map/all_to_all | solution.py:106
  118.5 2.8 %reshape.764 = bf16[32,2,16384]{2,1,0:T(2,128)(2,1)} reshape(bf16[32,32768]{1,0:T(8,128)(2,1)S(1)} %reduce.12) | data formatting | bytes 4194304
  121.2 7.8 %all-to-all-start.2 = ((bf16[32,2,16384]{2,1,0:T(2,128)(2,1)}), bf16[32,2,16384]{2,1,0:T(2,128)(2,1)S(1)}, u32[]{:S(2)}, u32[]{:S(2)}) async-start(bf16[32,2,16384]{2,1,0:T(2,128)(2,1)} %reshape.764), calls=%async_computation.2 | async-start | bytes 4194304 | tf_op jit(solution)/shard_map/all_to_all | solution.py:106
  130.0 2.1 fusion.71
  132.4 1.2 reduce_window_sum.11
  134.2 42.1 %all-to-all-done.2 = bf16[32,2,16384]{2,1,0:T(2,128)(2,1)S(1)} async-done(((bf16[32,2,16384]{2,1,0:T(2,128)(2,1)}), bf16[32,2,16384]{2,1,0:T(2,128)(2,1)S(1)}, u32[]{:S(2)}, u32[]{:S(2)}) %all-to-all-start.2) | async-done | bytes 2097184 | tf_op jit(solution)/shard_map/all_to_all | solution.py:106
  176.4 6.7 %reshape.765 = bf16[32,1,32768]{2,1,0:T(2,128)(2,1)} reshape(bf16[32,2,16384]{2,1,0:T(2,128)(2,1)S(1)} %all-to-all-done.2) | data formatting | bytes 4194304
  183.1 12.5 %reduce.6 = bf16[32,32768]{1,0:T(8,128)(2,1)S(1)} reduce(bf16[32,1,32768]{2,1,0:T(2,128)(2,1)} %reshape.765, bf16[]{:T(256)} %constant.86), dimensions={1}, to_apply=%all_to_all.18.reduce_sub_computation | reduce | bytes 4194306 | tf_op jit(solution)/shard_map/all_to_all | solution.py:106
  202.0 34.0 %all-gather.2.cloned.1.call-done = bf16[8,528,128]{2,1,0:T(8,128)(2,1)} async-done(((bf16[1,528,128]{2,1,0:T(8,128)(2,1)}), bf16[8,528,128]{2,1,0:T(8,128)(2,1)}) %all-gather.2.cloned.1.call-update) | async-done | bytes 1081360 | tf_op jit(solution)/shard_map/all_gather | solution.py:150
  236.0 1.4 slice_convert_fusion
  240.6 2.0 fusion.12
  242.6 2.1 multiply_reduce_fusion
  245.3 15.0 %all_to_all.25 = bf16[4,2,128,512]{3,2,1,0:T(8,128)(2,1)S(1)} all-to-all(bf16[4,2,128,512]{3,2,1,0:T(8,128)(2,1)S(1)} %copy.195), channel_id=1, replica_groups=mesh['dp'=8,'sz'=8,'sy'=4] {'sy'}, dimensions={0} | all-to-all | bytes 2097152 | tf_op jit(solution)/shard_map/all_to_all | solution.py:168
  261.3 2.2 copy.207
  263.5 2.0 copy.198
  265.5 2.0 copy.208
  267.6 2.0 copy.199
  (104 shorter events, 20.1 us)
Async XLA Ops:
  7.2 76.5 %copy-start = (bf16[1,768,2048]{2,1,0:T(8,128)(2,1)S(1)}, bf16[1,768,2048]{2,1,0:T(8,128)(2,1)}, u32[]{:S(2)}) copy-start(bf16[1,768,2048]{2,1,0:T(8,128)(2,1)} %param.17) | copy-start | bytes 9437188
  12.6 11.6 %copy-start.9 = (bf16[2048,32]{0,1:T(8,128)(2,1)S(1)}, bf16[2048,32]{0,1:T(8,128)(2,1)}, u32[]{:S(2)}) copy-start(bf16[2048,32]{0,1:T(8,128)(2,1)} %param.14) | copy-start | bytes 393220
  12.6 12.9 %copy-start.10 = (s32[128,2]{0,1:T(2,128)S(1)}, s32[128,2]{0,1:T(2,128)}, u32[]{:S(2)}) copy-start(s32[128,2]{0,1:T(2,128)} %param.13) | copy-start | bytes 3076
  12.6 13.4 %copy-start.11 = (f32[16,128]{1,0:T(8,128)S(1)}, f32[16,128]{1,0:T(8,128)}, u32[]{:S(2)}) copy-start(f32[16,128]{1,0:T(8,128)} %param.21) | copy-start | bytes 24580
  12.6 61.3 %all-to-all-start.1 = ((bf16[32,16,2048]{2,1,0:T(8,128)(2,1)}), bf16[32,16,2048]{2,1,0:T(8,128)(2,1)}, u32[]{:S(2)}, u32[]{:S(2)}) async-start(bf16[32,16,2048]{2,1,0:T(8,128)(2,1)} %bitcast.183), calls=%async_computation.1 | async-start | bytes 4194304 | tf_op jit(solution)/shard_map/all_to_all | solution.py:101
  40.7 2.5 copy-start.12
  73.9 47.4 %all-to-all-start = ((bf16[4,272,512]{2,1,0:T(8,128)(2,1)}), bf16[4,272,512]{2,1,0:T(8,128)(2,1)}, u32[]{:S(2)}, u32[]{:S(2)}) async-start(bf16[4,272,512]{2,1,0:T(8,128)(2,1)} %copy.181), calls=%async_computation | async-start | bytes 2228224 | tf_op jit(solution)/shard_map/all_to_all | solution.py:89
  121.2 55.1 %all-to-all-start.2 = ((bf16[32,2,16384]{2,1,0:T(2,128)(2,1)}), bf16[32,2,16384]{2,1,0:T(2,128)(2,1)S(1)}, u32[]{:S(2)}, u32[]{:S(2)}) async-start(bf16[32,2,16384]{2,1,0:T(2,128)(2,1)} %reshape.764), calls=%async_computation.2 | async-start | bytes 4194304 | tf_op jit(solution)/shard_map/all_to_all | solution.py:106
  129.1 106.9 %all-gather.2.cloned.1.call-start = ((), (), s32[]{:S(2)}) async-start(), calls=%async_computation.4 | async-start | bytes 1216512 | tf_op jit(solution)/shard_map/all_gather | solution.py:150
  132.4 65.2 %copy-start.2 = (bf16[4,128,512]{1,2,0:T(8,128)(2,1)}, bf16[4,128,512]{1,2,0:T(8,128)(2,1)S(1)}, u32[]{:S(2)}) copy-start(bf16[4,128,512]{1,2,0:T(8,128)(2,1)S(1)} %copy.206) | copy-start | bytes 1572868
  198.2 2.7 copy-start.4
  237.4 1.6 copy-start.8
  239.4 1.0 copy-start.5
  239.4 1.1 copy-start.6
  239.4 1.2 copy-start.7
  239.6 3.0 %copy-start.3 = (bf16[4,128,512]{1,2,0:T(8,128)(2,1)S(1)}, bf16[4,128,512]{1,2,0:T(8,128)(2,1)}, u32[]{:S(2)}) copy-start(bf16[4,128,512]{1,2,0:T(8,128)(2,1)} %copy-done.2) | copy-start | bytes 1572868
  261.3 8.3 %copy-start.1 = (bf16[1,768,2048]{2,1,0:T(8,128)(2,1)S(1)}, bf16[1,768,2048]{2,1,0:T(8,128)(2,1)}, u32[]{:S(2)}) copy-start(bf16[1,768,2048]{2,1,0:T(8,128)(2,1)} %param.17) | copy-start | bytes 9437188
Sparse Core Ops, SparseCore 0:
  200.3 35.6 all-gather.1

commit v4 on v3

--- a/solution.py
+++ b/solution.py
@@ -103,14 +103,23 @@
         recv.reshape(n_rows, width), w_gate[0], w_up[0], w_down[0], spike_level[0]
     )
     outgoing = computed.reshape(n_sz, n_sy, SLOTS, n_sy, qw).transpose(0, 3, 1, 2, 4)
-    back = lax.all_to_all(outgoing.reshape(n_sz * n_sy, -1), seq_axes, 0, 0, tiled=True)
-    table = back.reshape(n_experts, n_sy, SLOTS, qw).transpose(1, 0, 2, 3)
-    table = table.reshape(n_sy, n_rows, qw)
-    lanes = jnp.arange(n_rows, dtype=jnp.int32)[None, None, :]
-    pick0 = (row_first[:, :, None] == lanes).astype(jnp.bfloat16)
-    pick1 = (row_second[:, :, None] == lanes).astype(jnp.bfloat16)
-    first_out = jnp.einsum("btr,brc->btc", pick0, table, preferred_element_type=jnp.float32)
-    second_out = jnp.einsum("btr,brc->btc", pick1, table, preferred_element_type=jnp.float32)
+    outgoing = outgoing.reshape(n_sz * n_sy, n_sy * SLOTS, qw)
+    back = lax.all_to_all(outgoing, seq_axes, 0, 0, tiled=True)
+    table = back.reshape(n_experts, n_sy, SLOTS, qw)
+    lanes_e = jnp.arange(n_experts, dtype=jnp.int32)[None, None, :, None]
+    lanes_s = jnp.arange(SLOTS, dtype=jnp.int32)[None, None, None, :]
+
+    def pick(row):
+        e = (row // SLOTS)[:, :, None, None]
+        s = (row % SLOTS)[:, :, None, None]
+        return ((e == lanes_e) & (s == lanes_s)).astype(jnp.bfloat16)
+
+    first_out = jnp.einsum(
+        "btes,ebsc->btc", pick(row_first), table, preferred_element_type=jnp.float32
+    )
+    second_out = jnp.einsum(
+        "btes,ebsc->btc", pick(row_second), table, preferred_element_type=jnp.float32
+    )
     mix_q = (g_first[:, :, None] * first_out + g_second[:, :, None] * second_out).astype(
         jnp.bfloat16
     )
@@ -143,14 +152,11 @@
         lead = lead * block_total[b]
     group_state, group_span = run, lead
 
-    span_rows = jnp.zeros((16, hd), jnp.float32).at[0:3, :quarter].set(jnp.stack(split3(group_span)))
-    piece_packed = jnp.concatenate(
-        [group_state.reshape(quarter * hd, hd), span_rows], axis=0
-    ).astype(jnp.bfloat16)
+    span_rows = jnp.zeros((8, hd), jnp.float32).at[0, :quarter].set(group_span)
+    piece_packed = jnp.concatenate([group_state.reshape(quarter * hd, hd), span_rows], axis=0)
     pieces_packed = lax.all_gather(piece_packed, "sz", axis=0)
-    pieces = pieces_packed[:, : quarter * hd].astype(jnp.float32).reshape(n_sz, quarter, hd, hd)
-    span_parts = pieces_packed[:, quarter * hd : quarter * hd + 3, :quarter].astype(jnp.float32)
-    spans = (span_parts[:, 0] + span_parts[:, 1]) + span_parts[:, 2]
+    pieces = pieces_packed[:, : quarter * hd].reshape(n_sz, quarter, hd, hd)
+    spans = pieces_packed[:, quarter * hd, :quarter]
     run = jnp.zeros((quarter, hd, hd), jnp.float32)
     entering = [run]
     for g in range(n_sz - 1):

time: 279 us -> 249 us (0.89)
  other arithmetic: 34 us -> 10.2 us
  local copies, waits for them, and re-layouts: 58.3 us -> 51.4 us
    all_to_all x2 -> x0, other arithmetic: 25.7 us -> none  [body(): lax.all_to_all(outgoing.reshape(n_sz * n_sy, -1), seq_axes, 0, 0, tiled=T...]
    unnamed x40 -> x33, local copies, waits for them, and re-layouts: 27 us -> 19.3 us
    all_to_all x2 -> x1, local copies, waits for them, and re-layouts: 6.77 us -> 2.75 us  [body(): back = lax.all_to_all(outgoing, seq_axes, 0, 0, tiled=True)]
  transfers between devices with their start and end apart: 4 -> 4, of which waited for: 3 -> 3; matrix products, arithmetic and copies ran while one was open for 23% -> 20% of each run, Pallas kernels for 0% -> 0%
where the time goes in v4:
time: 249 us; the launch traced here: 247 us
  waiting for transfers between devices  106 us (43%)
  local copies, waits for them, and re-layouts  51.4 us (21%)
  matrix products  25.8 us (10%)
  starting transfers between devices  23.9 us (10%)
  blocking collectives  15.1 us (6%)
  between operations  14.4 us (6%)
  other arithmetic  10.2 us (4%)
    all_to_all x1, waiting for transfers between devices, body(): back = lax.all_to_all(outgoing, seq_axes, 0, 0, tiled=True)  40.1 us
    all_gather x1, waiting for transfers between devices, body(): pieces_packed = lax.all_gather(piece_packed, 'sz', axis=0)  35.2 us
    all_to_all x1, waiting for transfers between devices, body(): lax.all_to_all(send.reshape(n_experts, SLOTS, width), seq_axes, 0, 0, til...  30.7 us
    unnamed x33, local copies, waits for them, and re-layouts  19.3 us
    all_to_all x1, blocking collectives, body(): lax.all_to_all(jnp.stack([mix_q, att_q], axis=1), 'sy', 0, 0, tiled=True)  15.1 us
    all_to_all x1, starting transfers between devices, body(): lax.all_to_all(send.reshape(n_experts, SLOTS, width), seq_axes, 0, 0, til...  11.5 us
    dot_general x1, matrix products, expert_apply(): jnp.dot(spikes, down_matrix, preferred_element_type=jnp.float32)  8.3 us
    concatenate x2, local copies, waits for them, and re-layouts, body(): jnp.concatenate([q_split, k_split, decay_parts.astype(jnp.bfloat16), info...  8.03 us
  transfers between devices with their start and end apart: 4, of which 3 were waited for; matrix products, arithmetic and copies ran while one was open for 20% of the time, Pallas kernels for 0%

profile of v4, /device:TPU:36, one launch (start us, length us, event | category | flops | bytes accessed | tf_op | source)
XLA Modules:
  0.0 246.8 jit_solution(11942143837887498228)
XLA Ops:
  9.5 3.1 %convolution_convert_fusion = bf16[512,2048]{1,0:T(8,128)(2,1)} fusion(bf16[512,128]{1,0:T(8,128)(2,1)S(1)} %fusion.55, bf16[128,2048]{1,0:T(8,128)(2,1)} %param.12), kind=kOutput, calls=%fused_computation.6 | convolution fusion | flops 269484032 | bytes 2752512 | tf_op jit(solution)/shard_map/dot_general | solution.py:64
  12.6 11.5 %all-to-all-start.1 = ((bf16[32,16,2048]{2,1,0:T(8,128)(2,1)}), bf16[32,16,2048]{2,1,0:T(8,128)(2,1)}, u32[]{:S(2)}, u32[]{:S(2)}) async-start(bf16[32,16,2048]{2,1,0:T(8,128)(2,1)} %bitcast.194), calls=%async_computation.1 | async-start | bytes 4194304 | tf_op jit(solution)/shard_map/all_to_all | solution.py:101
  24.2 1.3 fusion.80
  29.3 2.0 copy.191
  31.3 2.0 copy.192
  35.1 5.6 %concatenate.11 = bf16[4,272,512]{1,2,0:T(8,128)(2,1)} concatenate(bf16[4,128,512]{1,2,0:T(8,128)(2,1)} %bitcast.203, bf16[4,128,512]{1,2,0:T(8,128)(2,1)} %bitcast.204, bf16[4,1,512]{1,2,0:T(8,128)(2,1)} %copy.195, bf16[4,1,512]{1,2,0:T(8,128)(2,1)} %copy.196, bf16[4,1,512]{1,2,0:T(8,128)(2,1)} %copy.197, bf16[4,3,512]{1,2,0:T(8,128)(2,1)} %broadcast_in_dim.10, ...), dimensions={1} | concatenate | bytes 2228224 | tf_op jit(solution)/shard_map/concatenate | solution.py:79
  40.7 2.5 copy.198
  43.2 30.7 %all-to-all-done.1 = bf16[32,16,2048]{2,1,0:T(8,128)(2,1)} async-done(((bf16[32,16,2048]{2,1,0:T(8,128)(2,1)}), bf16[32,16,2048]{2,1,0:T(8,128)(2,1)}, u32[]{:S(2)}, u32[]{:S(2)}) %all-to-all-start.1) | async-done | bytes 2097184 | tf_op jit(solution)/shard_map/all_to_all | solution.py:101
  73.9 4.2 %all-to-all-start = ((bf16[4,272,512]{2,1,0:T(8,128)(2,1)}), bf16[4,272,512]{2,1,0:T(8,128)(2,1)}, u32[]{:S(2)}, u32[]{:S(2)}) async-start(bf16[4,272,512]{2,1,0:T(8,128)(2,1)} %copy.198), calls=%async_computation | async-start | bytes 2228224 | tf_op jit(solution)/shard_map/all_to_all | solution.py:89
  78.1 5.5 %fusion.4 = f32[512,768]{1,0:T(8,128)} fusion(bf16[512,2048]{1,0:T(8,128)(2,1)} %bitcast.14, bf16[1,2048,768]{2,1,0:T(8,128)(2,1)} %param.15), kind=kOutput, calls=%fused_computation.4 | convolution fusion | flops 1610612736 | bytes 6815744 | tf_op jit(solution)/shard_map/dot_general | solution.py:12
  83.6 8.3 %fusion.6 = bf16[512,2048]{1,0:T(8,128)(2,1)} fusion(bf16[1,768,2048]{2,1,0:T(8,128)(2,1)S(1)} %copy-done, f32[512,768]{1,0:T(8,128)} %fusion.4, bf16[512,2048]{1,0:T(8,128)(2,1)} %bitcast.14, bf16[1,2048,768]{2,1,0:T(8,128)(2,1)} %param.16, f32[768]{0:T(1024)S(1)} %multiply_reduce_fusion.1), kind=kOutput, calls=%fused_computation.7 | convolution fusion | flops 3225419776 | bytes 12061696 | tf_op jit(solution)/shard_map/dot_general | solution.py:17
  91.9 4.5 %reshape.703 = bf16[8,4,16,4,512]{4,3,2,1,0:T(4,128)(2,1)} reshape(bf16[512,2048]{1,0:T(8,128)(2,1)} %fusion.6) | data formatting | bytes 4194304 | tf_op jit(solution)/shard_map/reshape | solution.py:105
  96.4 3.5 %copy.202 = bf16[8,4,16,4,512]{4,2,1,3,0:T(8,128)(2,1)} copy(bf16[8,4,16,4,512]{4,3,2,1,0:T(4,128)(2,1)} %reshape.703) | data formatting | bytes 4194304 | tf_op jit(solution)/shard_map/reshape | solution.py:105
  99.9 7.9 %all-to-all-start.2 = ((bf16[32,64,512]{2,1,0:T(8,128)(2,1)}), bf16[32,64,512]{2,1,0:T(8,128)(2,1)}, u32[]{:S(2)}, u32[]{:S(2)}) async-start(bf16[32,64,512]{2,1,0:T(8,128)(2,1)} %bitcast.195), calls=%async_computation.2 | async-start | bytes 4194304 | tf_op jit(solution)/shard_map/all_to_all | solution.py:107
  108.9 2.2 fusion.77
  111.1 2.0 copy.228
  113.2 1.2 reduce_window_sum.11
  115.1 40.1 %all-to-all-done.2 = bf16[32,64,512]{2,1,0:T(8,128)(2,1)} async-done(((bf16[32,64,512]{2,1,0:T(8,128)(2,1)}), bf16[32,64,512]{2,1,0:T(8,128)(2,1)}, u32[]{:S(2)}, u32[]{:S(2)}) %all-to-all-start.2) | async-done | bytes 2097184 | tf_op jit(solution)/shard_map/all_to_all | solution.py:107
  155.2 2.8 %copy.203 = bf16[32,64,512]{2,0,1:T(8,128)(2,1)S(1)} copy(bf16[32,64,512]{2,1,0:T(8,128)(2,1)} %all-to-all-done.2) | data formatting | bytes 4194304 | tf_op jit(solution)/shard_map/all_to_all | solution.py:107
  163.0 2.0 copy.227
  165.1 35.2 %all-gather.3.cloned.1.call-done = f32[4160,128]{1,0:T(8,128)} async-done(((f32[520,128]{1,0:T(8,128)}), f32[4160,128]{1,0:T(8,128)}) %all-gather.3.cloned.1.call-update) | async-done | bytes 2129936 | tf_op jit(solution)/shard_map/all_gather | solution.py:157
  200.4 1.7 fusion.76
  204.4 2.1 fusion.15
  206.5 3.6 %multiply_reduce_fusion = (f32[4,128,4]{1,2,0:T(4,128)S(1)}, f32[4,128,4,128]{1,3,2,0:T(8,128)}) fusion(f32[4,128,4,128]{1,3,2,0:T(8,128)} %fusion.15, bf16[4,128,4,128]{1,3,2,0:T(8,128)(2,1)} %bitcast.216, bf16[4,128,4,128]{1,3,2,0:T(8,128)(2,1)} %bitcast.208, f32[4,4,128]{2,1,0:T(4,128)S(1)} %reduce_window_sum.11, ...), kind=kOutput, calls=%fused_computation.32 | convolution fusion | flops 136312832 | bytes 3702784 | tf_op jit(solution)/shard_map/bhts,bshd->bthd/dot_general | solution.py:136
  210.1 2.1 multiply_convert_fusion.1
  212.2 2.0 copy.226
  214.3 1.3 pad_maximum_fusion
  215.6 15.1 %all_to_all.20 = bf16[4,2,128,512]{3,2,1,0:T(8,128)(2,1)S(1)} all-to-all(bf16[4,2,128,512]{3,2,1,0:T(8,128)(2,1)S(1)} %copy.215), channel_id=1, replica_groups=mesh['dp'=8,'sz'=8,'sy'=4] {'sy'}, dimensions={0} | all-to-all | bytes 2097152 | tf_op jit(solution)/shard_map/all_to_all | solution.py:174
  231.8 2.0 copy.229
  233.8 2.0 copy.218
  235.9 2.0 copy.230
  237.9 2.0 copy.219
  (95 shorter events, 18.2 us)
Async XLA Ops:
  7.2 76.4 %copy-start = (bf16[1,768,2048]{2,1,0:T(8,128)(2,1)S(1)}, bf16[1,768,2048]{2,1,0:T(8,128)(2,1)}, u32[]{:S(2)}) copy-start(bf16[1,768,2048]{2,1,0:T(8,128)(2,1)} %param.17) | copy-start | bytes 9437188
  12.6 11.6 %copy-start.7 = (bf16[2048,32]{0,1:T(8,128)(2,1)S(1)}, bf16[2048,32]{0,1:T(8,128)(2,1)}, u32[]{:S(2)}) copy-start(bf16[2048,32]{0,1:T(8,128)(2,1)} %param.14) | copy-start | bytes 393220
  12.6 12.9 %copy-start.8 = (s32[128,2]{0,1:T(2,128)S(1)}, s32[128,2]{0,1:T(2,128)}, u32[]{:S(2)}) copy-start(s32[128,2]{0,1:T(2,128)} %param.13) | copy-start | bytes 3076
  12.6 13.4 %copy-start.9 = (f32[16,128]{1,0:T(8,128)S(1)}, f32[16,128]{1,0:T(8,128)}, u32[]{:S(2)}) copy-start(f32[16,128]{1,0:T(8,128)} %param.21) | copy-start | bytes 24580
  12.6 61.3 %all-to-all-start.1 = ((bf16[32,16,2048]{2,1,0:T(8,128)(2,1)}), bf16[32,16,2048]{2,1,0:T(8,128)(2,1)}, u32[]{:S(2)}, u32[]{:S(2)}) async-start(bf16[32,16,2048]{2,1,0:T(8,128)(2,1)} %bitcast.194), calls=%async_computation.1 | async-start | bytes 4194304 | tf_op jit(solution)/shard_map/all_to_all | solution.py:101
  40.7 2.5 copy-start.10
  73.9 26.0 %all-to-all-start = ((bf16[4,272,512]{2,1,0:T(8,128)(2,1)}), bf16[4,272,512]{2,1,0:T(8,128)(2,1)}, u32[]{:S(2)}, u32[]{:S(2)}) async-start(bf16[4,272,512]{2,1,0:T(8,128)(2,1)} %copy.198), calls=%async_computation | async-start | bytes 2228224 | tf_op jit(solution)/shard_map/all_to_all | solution.py:89
  99.9 55.3 %all-to-all-start.2 = ((bf16[32,64,512]{2,1,0:T(8,128)(2,1)}), bf16[32,64,512]{2,1,0:T(8,128)(2,1)}, u32[]{:S(2)}, u32[]{:S(2)}) async-start(bf16[32,64,512]{2,1,0:T(8,128)(2,1)} %bitcast.195), calls=%async_computation.2 | async-start | bytes 4194304 | tf_op jit(solution)/shard_map/all_to_all | solution.py:107
  107.8 92.6 %all-gather.3.cloned.1.call-start = ((), (), s32[]{:S(2)}) async-start(), calls=%async_computation.4 | async-start | bytes 2396160 | tf_op jit(solution)/shard_map/all_gather | solution.py:157
  158.5 1.0 copy-start.2
  159.0 2.1 copy-start.1
  200.4 2.4 copy-start.6
  203.2 1.0 copy-start.3
  203.3 1.1 copy-start.4
  203.3 1.2 copy-start.5
Sparse Core Ops, SparseCore 0:
  162.4 37.9 all-gather.2

commit v5 on v4

--- a/solution.py
+++ b/solution.py
@@ -152,17 +152,24 @@
         lead = lead * block_total[b]
     group_state, group_span = run, lead
 
-    span_rows = jnp.zeros((8, hd), jnp.float32).at[0, :quarter].set(group_span)
-    piece_packed = jnp.concatenate([group_state.reshape(quarter * hd, hd), span_rows], axis=0)
-    pieces_packed = lax.all_gather(piece_packed, "sz", axis=0)
-    pieces = pieces_packed[:, : quarter * hd].reshape(n_sz, quarter, hd, hd)
-    spans = pieces_packed[:, quarter * hd, :quarter]
-    run = jnp.zeros((quarter, hd, hd), jnp.float32)
-    entering = [run]
-    for g in range(n_sz - 1):
-        run = spans[g][:, None, None] * run + pieces[g]
-        entering.append(run)
-    before = lax.dynamic_index_in_dim(jnp.stack(entering), zi, 0, False)
+    def shifted(value, span, by):
+        pairs = [(i, i + by) for i in range(n_sz - by)]
+        got_value = lax.ppermute(value, "sz", pairs)
+        got_span = lax.ppermute(span, "sz", pairs)
+        return got_value, jnp.where(zi >= by, got_span, 1.0)
+
+    def join(earlier, later):
+        (v_e, s_e), (v_l, s_l) = earlier, later
+        return (s_l[:, None, None] * v_e + v_l, s_e * s_l)
+
+    one = shifted(group_state, group_span, 1)
+    two = shifted(group_state, group_span, 2)
+    window = join(two, one)
+    reach = 2
+    while reach < n_sz:
+        window = join(shifted(window[0], window[1], reach), window)
+        reach *= 2
+    before = window[0]
 
     carried = jnp.stack(leads)[:, :, None, None] * before[None] + jnp.stack(inside)
     inter = jnp.transpose(jnp.exp(cumulative), (0, 2, 1))[:, :, :, None] * jnp.einsum(

time: 249 us -> 249 us (level)
  starting transfers between devices: 23.9 us -> 47.7 us
  waiting for transfers between devices: 106 us -> 87.6 us
  between operations: 14.4 us -> 1.06 us
  blocking collectives: 15.1 us -> 25.3 us
    all_gather x1 -> x0, waiting for transfers between devices: 35.2 us -> none  [body(): pieces_packed = lax.all_gather(piece_packed, 'sz', axis=0)]
    ppermute x0 -> x7, starting transfers between devices: none -> 24.1 us  [the longest x4 16.9 us: shifted(): got_value = lax.ppermute(value, 'sz', pairs)]
    ppermute x0 -> x7, waiting for transfers between devices: none -> 16.5 us  [the longest x4 10.4 us: shifted(): got_value = lax.ppermute(value, 'sz', pairs)]
    all_to_all x1, blocking collectives: 15.1 us -> 25.3 us  [body(): lax.all_to_all(jnp.stack([mix_q, att_q], axis=1), 'sy', 0, 0, tiled=True)]
    unnamed x33 -> x28, local copies, waits for them, and re-layouts: 19.3 us -> 18.8 us
  transfers between devices with their start and end apart: 4 -> 10, of which waited for: 3 -> 5; matrix products, arithmetic and copies ran while one was open for 20% -> 21% of each run, Pallas kernels for 0% -> 0%
where the time goes in v5:
time: 249 us; the launch traced here: 247 us
  waiting for transfers between devices  87.6 us (35%)
  local copies, waits for them, and re-layouts  49 us (20%)
  starting transfers between devices  47.7 us (19%)
  matrix products  25.8 us (10%)
  blocking collectives  25.3 us (10%)
  other arithmetic  10.4 us (4%)
    all_to_all x1, waiting for transfers between devices, body(): back = lax.all_to_all(outgoing, seq_axes, 0, 0, tiled=True)  40.5 us
    all_to_all x1, waiting for transfers between devices, body(): lax.all_to_all(send.reshape(n_experts, SLOTS, width), seq_axes, 0, 0, til...  30.6 us
    all_to_all x1, blocking collectives, body(): lax.all_to_all(jnp.stack([mix_q, att_q], axis=1), 'sy', 0, 0, tiled=True)  25.3 us
    unnamed x28, local copies, waits for them, and re-layouts  18.8 us
    ppermute x4, starting transfers between devices, shifted(): got_value = lax.ppermute(value, 'sz', pairs)  16.9 us
    all_to_all x1, starting transfers between devices, body(): lax.all_to_all(send.reshape(n_experts, SLOTS, width), seq_axes, 0, 0, til...  11.4 us
    ppermute x4, waiting for transfers between devices, shifted(): got_value = lax.ppermute(value, 'sz', pairs)  10.4 us
    dot_general x1, matrix products, expert_apply(): jnp.dot(spikes, down_matrix, preferred_element_type=jnp.float32)  8.3 us
  transfers between devices with their start and end apart: 10, of which 5 were waited for; matrix products, arithmetic and copies ran while one was open for 21% of the time, Pallas kernels for 0%

profile of v5, /device:TPU:36, one launch (start us, length us, event | category | flops | bytes accessed | tf_op | source)
XLA Modules:
  0.0 246.7 jit_solution(8491922074600544229)
XLA Ops:
  3.0 3.1 %convolution_convert_fusion = bf16[512,2048]{1,0:T(8,128)(2,1)} fusion(bf16[512,128]{1,0:T(8,128)(2,1)S(1)} %fusion.55, bf16[128,2048]{1,0:T(8,128)(2,1)} %param.10), kind=kOutput, calls=%fused_computation.6 | convolution fusion | flops 269484032 | bytes 2752512 | tf_op jit(solution)/shard_map/dot_general | solution.py:64
  6.1 11.4 %all-to-all-start.1 = ((bf16[32,16,2048]{2,1,0:T(8,128)(2,1)}), bf16[32,16,2048]{2,1,0:T(8,128)(2,1)}, u32[]{:S(2)}, u32[]{:S(2)}) async-start(bf16[32,16,2048]{2,1,0:T(8,128)(2,1)} %bitcast.176), calls=%async_computation.1 | async-start | bytes 4194304 | tf_op jit(solution)/shard_map/all_to_all | solution.py:101
  17.5 2.1 copy.191
  28.5 5.6 %concatenate.6 = bf16[4,272,512]{1,2,0:T(8,128)(2,1)} concatenate(bf16[4,128,512]{1,2,0:T(8,128)(2,1)} %bitcast.179, bf16[4,128,512]{1,2,0:T(8,128)(2,1)} %bitcast.180, bf16[4,1,512]{1,2,0:T(8,128)(2,1)} %copy.195, bf16[4,1,512]{1,2,0:T(8,128)(2,1)} %copy.196, bf16[4,1,512]{1,2,0:T(8,128)(2,1)} %copy.197, bf16[4,3,512]{1,2,0:T(8,128)(2,1)} %broadcast_in_dim.17, ...), dimensions={1} | concatenate | bytes 2228224 | tf_op jit(solution)/shard_map/concatenate | solution.py:79
  34.1 2.5 %copy.198 = bf16[4,272,512]{2,1,0:T(8,128)(2,1)} copy(bf16[4,272,512]{1,2,0:T(8,128)(2,1)} %concatenate.6) | data formatting | bytes 2228224 | tf_op jit(solution)/shard_map/concatenate | solution.py:79
  36.6 30.6 %all-to-all-done.1 = bf16[32,16,2048]{2,1,0:T(8,128)(2,1)} async-done(((bf16[32,16,2048]{2,1,0:T(8,128)(2,1)}), bf16[32,16,2048]{2,1,0:T(8,128)(2,1)}, u32[]{:S(2)}, u32[]{:S(2)}) %all-to-all-start.1) | async-done | bytes 2097184 | tf_op jit(solution)/shard_map/all_to_all | solution.py:101
  67.2 4.3 %all-to-all-start = ((bf16[4,272,512]{2,1,0:T(8,128)(2,1)}), bf16[4,272,512]{2,1,0:T(8,128)(2,1)}, u32[]{:S(2)}, u32[]{:S(2)}) async-start(bf16[4,272,512]{2,1,0:T(8,128)(2,1)} %copy.198), calls=%async_computation | async-start | bytes 2228224 | tf_op jit(solution)/shard_map/all_to_all | solution.py:89
  71.5 5.5 %fusion.4 = f32[512,768]{1,0:T(8,128)} fusion(bf16[512,2048]{1,0:T(8,128)(2,1)} %bitcast.14, bf16[1,2048,768]{2,1,0:T(8,128)(2,1)} %param.13), kind=kOutput, calls=%fused_computation.4 | convolution fusion | flops 1610612736 | bytes 6815744 | tf_op jit(solution)/shard_map/dot_general | solution.py:12
  77.0 8.3 %fusion.6 = bf16[512,2048]{1,0:T(8,128)(2,1)} fusion(bf16[1,768,2048]{2,1,0:T(8,128)(2,1)S(1)} %copy-done, f32[512,768]{1,0:T(8,128)} %fusion.4, bf16[512,2048]{1,0:T(8,128)(2,1)} %bitcast.14, bf16[1,2048,768]{2,1,0:T(8,128)(2,1)} %param.14, f32[768]{0:T(1024)S(1)} %multiply_reduce_fusion.1), kind=kOutput, calls=%fused_computation.7 | convolution fusion | flops 3225419776 | bytes 12061696 | tf_op jit(solution)/shard_map/dot_general | solution.py:17
  85.3 4.5 %reshape.458 = bf16[8,4,16,4,512]{4,3,2,1,0:T(4,128)(2,1)} reshape(bf16[512,2048]{1,0:T(8,128)(2,1)} %fusion.6) | data formatting | bytes 4194304 | tf_op jit(solution)/shard_map/reshape | solution.py:105
  89.8 3.5 %copy.202 = bf16[8,4,16,4,512]{4,2,1,3,0:T(8,128)(2,1)} copy(bf16[8,4,16,4,512]{4,3,2,1,0:T(4,128)(2,1)} %reshape.458) | data formatting | bytes 4194304 | tf_op jit(solution)/shard_map/reshape | solution.py:105
  93.2 7.9 %all-to-all-start.2 = ((bf16[32,64,512]{2,1,0:T(8,128)(2,1)}), bf16[32,64,512]{2,1,0:T(8,128)(2,1)}, u32[]{:S(2)}, u32[]{:S(2)}) async-start(bf16[32,64,512]{2,1,0:T(8,128)(2,1)} %bitcast.177), calls=%async_computation.2 | async-start | bytes 4194304 | tf_op jit(solution)/shard_map/all_to_all | solution.py:107
  101.1 2.2 fusion.78
  103.4 2.0 copy.228
  108.0 40.5 %all-to-all-done.2 = bf16[32,64,512]{2,1,0:T(8,128)(2,1)} async-done(((bf16[32,64,512]{2,1,0:T(8,128)(2,1)}), bf16[32,64,512]{2,1,0:T(8,128)(2,1)}, u32[]{:S(2)}, u32[]{:S(2)}) %all-to-all-start.2) | async-done | bytes 2097184 | tf_op jit(solution)/shard_map/all_to_all | solution.py:107
  148.5 2.8 %copy.203 = bf16[32,64,512]{2,0,1:T(8,128)(2,1)S(1)} copy(bf16[32,64,512]{2,1,0:T(8,128)(2,1)} %all-to-all-done.2) | data formatting | bytes 4194304 | tf_op jit(solution)/shard_map/all_to_all | solution.py:107
  154.7 4.0 %collective-permute-start.4 = (f32[4,128,128]{2,1,0:T(8,128)S(1)}, f32[4,128,128]{2,1,0:T(8,128)}, u32[]{:S(2)}, u32[]{:S(2)}) collective-permute-start(f32[4,128,128]{2,1,0:T(8,128)S(1)} %fusion.56), channel_id=1, source_target_pairs={{0,4},{4,8},{8,12},{12,16},{16,20},{20,24},{24,28},{1,5},{5,9},{9,... | collective-permute-start | bytes 786440 | tf_op jit(solution)/shard_map/ppermute | solution.py:157
  158.7 3.2 %collective-permute-start.3 = (f32[4,128,128]{2,1,0:T(8,128)S(1)}, f32[4,128,128]{2,1,0:T(8,128)}, u32[]{:S(2)}, u32[]{:S(2)}) collective-permute-start(f32[4,128,128]{2,1,0:T(8,128)S(1)} %fusion.56), channel_id=1, source_target_pairs={{0,8},{4,12},{8,16},{12,20},{16,24},{20,28},{1,9},{5,13},{9,17},{1... | collective-permute-start | bytes 786440 | tf_op jit(solution)/shard_map/ppermute | solution.py:157
  163.9 2.3 collective-permute-start.1
  166.2 6.0 %collective-permute-done = f32[4]{0:T(128)S(1)} collective-permute-done((f32[4]{0:T(128)S(1)}, f32[4]{0:T(128)S(1)}, u32[]{:S(2)}, u32[]{:S(2)}) %collective-permute-start) | collective-permute-done | bytes 48 | tf_op jit(solution)/shard_map/ppermute | solution.py:158
  173.4 6.1 %collective-permute-start.5 = (f32[4,128,128]{2,1,0:T(8,128)S(1)}, f32[4,128,128]{2,1,0:T(8,128)}, u32[]{:S(2)}, u32[]{:S(2)}) collective-permute-start(f32[4,128,128]{2,1,0:T(8,128)S(1)} %multiply_add_fusion.4), channel_id=1, source_target_pairs={{0,8},{4,12},{8,16},{12,20},{16,24},{20,28},{1,9},{5,13},{9,17},{1... | collective-permute-start | bytes 786440 | tf_op jit(solution)/shard_map/ppermute | solution.py:157
  179.5 2.0 copy.227
  181.6 3.0 %collective-permute-start.2 = (f32[4]{0:T(128)S(1)}, f32[4]{0:T(128)S(1)}, u32[]{:S(2)}, u32[]{:S(2)}) collective-permute-start(f32[4]{0:T(128)S(1)} %get-tuple-element.20), channel_id=1, source_target_pairs={{0,8},{4,12},{8,16},{12,20},{16,24},{20,28},{1,9},{5,13},{9,17},{1... | collective-permute-start | bytes 56 | tf_op jit(solution)/shard_map/ppermute | solution.py:158
  184.6 5.0 %collective-permute-done.5 = f32[4,128,128]{2,1,0:T(8,128)} collective-permute-done((f32[4,128,128]{2,1,0:T(8,128)S(1)}, f32[4,128,128]{2,1,0:T(8,128)}, u32[]{:S(2)}, u32[]{:S(2)}) %collective-permute-start.5) | collective-permute-done | bytes 262176 | tf_op jit(solution)/shard_map/ppermute | solution.py:157
  190.7 3.6 %collective-permute-start.6 = (f32[4,128,128]{2,1,0:T(8,128)S(1)}, f32[4,128,128]{2,1,0:T(8,128)S(1)}, u32[]{:S(2)}, u32[]{:S(2)}) collective-permute-start(f32[4,128,128]{2,1,0:T(8,128)S(1)} %multiply_add_fusion.3), channel_id=1, source_target_pairs={{0,16},{4,20},{8,24},{12,28},{1,17},{5,21},{9,25},{13,29},{2,18},{... | collective-permute-start | bytes 786440 | tf_op jit(solution)/shard_map/ppermute | solution.py:157
  195.5 5.4 %collective-permute-done.6 = f32[4,128,128]{2,1,0:T(8,128)S(1)} collective-permute-done((f32[4,128,128]{2,1,0:T(8,128)S(1)}, f32[4,128,128]{2,1,0:T(8,128)S(1)}, u32[]{:S(2)}, u32[]{:S(2)}) %collective-permute-start.6) | collective-permute-done | bytes 262176 | tf_op jit(solution)/shard_map/ppermute | solution.py:157
  201.0 2.1 fusion.15
  203.1 3.6 %multiply_reduce_fusion = (f32[4,128,4]{1,2,0:T(4,128)S(1)}, f32[4,128,4,128]{1,3,2,0:T(8,128)}) fusion(f32[4,128,4,128]{1,3,2,0:T(8,128)} %fusion.15, bf16[4,128,4,128]{1,3,2,0:T(8,128)(2,1)} %bitcast.186, bf16[4,128,4,128]{1,3,2,0:T(8,128)(2,1)} %bitcast.184, f32[4,4,128]{2,1,0:T(4,128)S(1)} %reduce_window_sum.11, ...), kind=kOutput, calls=%fused_computation.31 | convolution fusion | flops 136312832 | bytes 3702784 | tf_op jit(solution)/shard_map/bhts,bshd->bthd/dot_general | solution.py:136
  206.6 2.1 multiply_convert_fusion.1
  208.8 2.0 copy.226
  212.2 25.3 %all_to_all.20 = bf16[4,2,128,512]{3,2,1,0:T(8,128)(2,1)S(1)} all-to-all(bf16[4,2,128,512]{3,2,1,0:T(8,128)(2,1)S(1)} %copy.215), channel_id=1, replica_groups=mesh['dp'=8,'sz'=8,'sy'=4] {'sy'}, dimensions={0} | all-to-all | bytes 2097152 | tf_op jit(solution)/shard_map/all_to_all | solution.py:181
  244.7 2.0 copy.219
  (92 shorter events, 31.2 us)
Async XLA Ops:
  0.6 76.3 %copy-start = (bf16[1,768,2048]{2,1,0:T(8,128)(2,1)S(1)}, bf16[1,768,2048]{2,1,0:T(8,128)(2,1)}, u32[]{:S(2)}) copy-start(bf16[1,768,2048]{2,1,0:T(8,128)(2,1)} %param.15) | copy-start | bytes 9437188
  6.1 61.1 %all-to-all-start.1 = ((bf16[32,16,2048]{2,1,0:T(8,128)(2,1)}), bf16[32,16,2048]{2,1,0:T(8,128)(2,1)}, u32[]{:S(2)}, u32[]{:S(2)}) async-start(bf16[32,16,2048]{2,1,0:T(8,128)(2,1)} %bitcast.176), calls=%async_computation.1 | async-start | bytes 4194304 | tf_op jit(solution)/shard_map/all_to_all | solution.py:101
  17.5 4.2 %copy-start.7 = (f32[16,128]{1,0:T(8,128)S(1)}, f32[16,128]{1,0:T(8,128)}, u32[]{:S(2)}) copy-start(f32[16,128]{1,0:T(8,128)} %param.19) | copy-start | bytes 24580
  17.5 7.4 %copy-start.5 = (bf16[2048,32]{0,1:T(8,128)(2,1)S(1)}, bf16[2048,32]{0,1:T(8,128)(2,1)}, u32[]{:S(2)}) copy-start(bf16[2048,32]{0,1:T(8,128)(2,1)} %param.12) | copy-start | bytes 393220
  17.5 8.7 %copy-start.6 = (s32[128,2]{0,1:T(2,128)S(1)}, s32[128,2]{0,1:T(2,128)}, u32[]{:S(2)}) copy-start(s32[128,2]{0,1:T(2,128)} %param.11) | copy-start | bytes 3076
  34.1 2.5 %copy-start.8 = (s32[1,768]{1,0:T(1,128)S(1)}, s32[1,768]{1,0:T(1,128)}, u32[]{:S(2)}) copy-start(s32[1,768]{1,0:T(1,128)} %param.16) | copy-start | bytes 9220
  67.2 26.1 %all-to-all-start = ((bf16[4,272,512]{2,1,0:T(8,128)(2,1)}), bf16[4,272,512]{2,1,0:T(8,128)(2,1)}, u32[]{:S(2)}, u32[]{:S(2)}) async-start(bf16[4,272,512]{2,1,0:T(8,128)(2,1)} %copy.198), calls=%async_computation | async-start | bytes 2228224 | tf_op jit(solution)/shard_map/all_to_all | solution.py:89
  93.2 55.3 %all-to-all-start.2 = ((bf16[32,64,512]{2,1,0:T(8,128)(2,1)}), bf16[32,64,512]{2,1,0:T(8,128)(2,1)}, u32[]{:S(2)}, u32[]{:S(2)}) async-start(bf16[32,64,512]{2,1,0:T(8,128)(2,1)} %bitcast.177), calls=%async_computation.2 | async-start | bytes 4194304 | tf_op jit(solution)/shard_map/all_to_all | solution.py:107
  151.8 1.0 copy-start.3
  152.4 2.3 copy-start.2
  153.5 1.0 copy-start.1
  154.7 17.6 %collective-permute-start.4 = (f32[4,128,128]{2,1,0:T(8,128)S(1)}, f32[4,128,128]{2,1,0:T(8,128)}, u32[]{:S(2)}, u32[]{:S(2)}) collective-permute-start(f32[4,128,128]{2,1,0:T(8,128)S(1)} %fusion.56), channel_id=1, source_target_pairs={{0,4},{4,8},{8,12},{12,16},{16,20},{20,24},{24,28},{1,5},{5,9},{9,... | collective-permute-start | bytes 786440 | tf_op jit(solution)/shard_map/ppermute | solution.py:157
  158.7 13.6 %collective-permute-start.3 = (f32[4,128,128]{2,1,0:T(8,128)S(1)}, f32[4,128,128]{2,1,0:T(8,128)}, u32[]{:S(2)}, u32[]{:S(2)}) collective-permute-start(f32[4,128,128]{2,1,0:T(8,128)S(1)} %fusion.56), channel_id=1, source_target_pairs={{0,8},{4,12},{8,16},{12,20},{16,24},{20,28},{1,9},{5,13},{9,17},{1... | collective-permute-start | bytes 786440 | tf_op jit(solution)/shard_map/ppermute | solution.py:157
  161.9 10.3 %collective-permute-start = (f32[4]{0:T(128)S(1)}, f32[4]{0:T(128)S(1)}, u32[]{:S(2)}, u32[]{:S(2)}) collective-permute-start(f32[4]{0:T(128)S(1)} %get-tuple-element.53), channel_id=1, source_target_pairs={{0,8},{4,12},{8,16},{12,20},{16,24},{20,28},{1,9},{5,13},{9,17},{1... | collective-permute-start | bytes 56 | tf_op jit(solution)/shard_map/ppermute | solution.py:158
  163.9 8.3 %collective-permute-start.1 = (f32[4]{0:T(128)S(1)}, f32[4]{0:T(128)S(1)}, u32[]{:S(2)}, u32[]{:S(2)}) collective-permute-start(f32[4]{0:T(128)S(1)} %get-tuple-element.53), channel_id=1, source_target_pairs={{0,4},{4,8},{8,12},{12,16},{16,20},{20,24},{24,28},{1,5},{5,9},{9,... | collective-permute-start | bytes 56 | tf_op jit(solution)/shard_map/ppermute | solution.py:158
  173.4 16.2 %collective-permute-start.5 = (f32[4,128,128]{2,1,0:T(8,128)S(1)}, f32[4,128,128]{2,1,0:T(8,128)}, u32[]{:S(2)}, u32[]{:S(2)}) collective-permute-start(f32[4,128,128]{2,1,0:T(8,128)S(1)} %multiply_add_fusion.4), channel_id=1, source_target_pairs={{0,8},{4,12},{8,16},{12,20},{16,24},{20,28},{1,9},{5,13},{9,17},{1... | collective-permute-start | bytes 786440 | tf_op jit(solution)/shard_map/ppermute | solution.py:157
  181.5 19.5 %copy-start.4 = (bf16[4,128,512]{1,2,0:T(8,128)(2,1)S(1)}, bf16[4,128,512]{1,2,0:T(8,128)(2,1)}, u32[]{:S(2)}) copy-start(bf16[4,128,512]{1,2,0:T(8,128)(2,1)} %copy.227) | copy-start | bytes 1572868
  181.6 12.6 %collective-permute-start.2 = (f32[4]{0:T(128)S(1)}, f32[4]{0:T(128)S(1)}, u32[]{:S(2)}, u32[]{:S(2)}) collective-permute-start(f32[4]{0:T(128)S(1)} %get-tuple-element.20), channel_id=1, source_target_pairs={{0,8},{4,12},{8,16},{12,20},{16,24},{20,28},{1,9},{5,13},{9,17},{1... | collective-permute-start | bytes 56 | tf_op jit(solution)/shard_map/ppermute | solution.py:158
  190.7 10.2 %collective-permute-start.6 = (f32[4,128,128]{2,1,0:T(8,128)S(1)}, f32[4,128,128]{2,1,0:T(8,128)S(1)}, u32[]{:S(2)}, u32[]{:S(2)}) collective-permute-start(f32[4,128,128]{2,1,0:T(8,128)S(1)} %multiply_add_fusion.3), channel_id=1, source_target_pairs={{0,16},{4,20},{8,24},{12,28},{1,17},{5,21},{9,25},{13,29},{2,18},{... | collective-permute-start | bytes 786440 | tf_op jit(solution)/shard_map/ppermute | solution.py:157

commit v6 on v5

--- a/solution.py
+++ b/solution.py
@@ -8,13 +8,12 @@
 GROUP = 4
 
 
-def expert_apply(token_rows, gate_matrix, up_matrix, down_matrix, levels):
+def expert_spikes(token_rows, gate_matrix, up_matrix, levels):
     gate_values = jnp.dot(token_rows, gate_matrix, preferred_element_type=jnp.float32)
     up_values = jnp.dot(token_rows, up_matrix, preferred_element_type=jnp.float32)
     hidden = jax.nn.silu(gate_values) * up_values
     threshold = 0.125 * levels.astype(jnp.float32)
-    spikes = (threshold * jnp.tanh(hidden / threshold)).astype(jnp.bfloat16)
-    return jnp.dot(spikes, down_matrix, preferred_element_type=jnp.float32).astype(jnp.bfloat16)
+    return (threshold * jnp.tanh(hidden / threshold)).astype(jnp.bfloat16)
 
 
 def split3(values):
@@ -99,10 +98,13 @@
     row_second = (got_info[:, 2] * SLOTS + got_info[:, 3]).astype(jnp.int32)
 
     recv = lax.all_to_all(send.reshape(n_experts, SLOTS, width), seq_axes, 0, 0, tiled=True)
-    computed = expert_apply(
-        recv.reshape(n_rows, width), w_gate[0], w_up[0], w_down[0], spike_level[0]
-    )
-    outgoing = computed.reshape(n_sz, n_sy, SLOTS, n_sy, qw).transpose(0, 3, 1, 2, 4)
+    spikes = expert_spikes(recv.reshape(n_rows, width), w_gate[0], w_up[0], spike_level[0])
+    outgoing = jnp.einsum(
+        "zrk,kjc->zjrc",
+        spikes.reshape(n_sz, n_sy * SLOTS, -1),
+        w_down[0].reshape(-1, n_sy, qw),
+        preferred_element_type=jnp.float32,
+    ).astype(jnp.bfloat16)
     outgoing = outgoing.reshape(n_sz * n_sy, n_sy * SLOTS, qw)
     back = lax.all_to_all(outgoing, seq_axes, 0, 0, tiled=True)
     table = back.reshape(n_experts, n_sy, SLOTS, qw)
@@ -178,9 +180,9 @@
     total_out = intra + inter
     normed = total_out * lax.rsqrt(jnp.mean(total_out * total_out, axis=3, keepdims=True) + 1e-06)
     att_q = normed.astype(jnp.bfloat16).reshape(n_sy, count, qw)
-    home = lax.all_to_all(jnp.stack([mix_q, att_q], axis=1), "sy", 0, 0, tiled=True)
-    expert_mix = home[:, 0].transpose(1, 0, 2).reshape(count, width)
-    attended = home[:, 1].transpose(1, 0, 2).reshape(count, heads * hd)
+    home = lax.all_to_all(jnp.stack([mix_q, att_q], axis=1), "sy", 0, 3, tiled=True)
+    expert_mix = home[0, 0]
+    attended = home[0, 1]
     return (expert_mix, attended)
 
 

time: 249 us -> 240 us (0.964)
  blocking collectives: 25.3 us -> 20.1 us
  starting transfers between devices: 47.7 us -> 51.3 us
  matrix products: 25.8 us -> 22.6 us
    reshape x2 -> x0, local copies, waits for them, and re-layouts: 7.97 us -> none  [body(): computed.reshape(n_sz, n_sy, SLOTS, n_sy, qw).transpose(0, 3, 1, 2, 4)]
    all_to_all x1, waiting for transfers between devices: 30.6 us -> 24.4 us  [body(): lax.all_to_all(send.reshape(n_experts, SLOTS, width), seq_axes, 0, 0, til...]
    another operation x3 -> x4, local copies, waits for them, and re-layouts: 3.19 us -> 9.41 us  [the longest x1 6.17 us: body(): w_down[0].reshape(-1, n_sy, qw)]
    all_to_all x1, blocking collectives: 25.3 us -> 20.1 us  [body(): lax.all_to_all(jnp.stack([mix_q, att_q], axis=1), 'sy', 0, 3, tiled=True)]
    ppermute x4, starting transfers between devices: 16.9 us -> 21.9 us  [shifted(): got_value = lax.ppermute(value, 'sz', pairs)]
    all_to_all x1, waiting for transfers between devices: 0.01 us -> 4.17 us  [body(): got = lax.all_to_all(packed, 'sy', 0, 0, tiled=True)]
    unnamed x28 -> x30, local copies, waits for them, and re-layouts: 18.8 us -> 14.7 us
    dot_general x2 -> x3, matrix products: 13.8 us -> 10.6 us  [the longest x1 3.82 us: expert_spikes(): jnp.dot(token_rows, up_matrix, preferred_element_type=jnp.float32)]
  transfers between devices with their start and end apart: 10 -> 10, of which waited for: 5 -> 6; matrix products, arithmetic and copies ran while one was open for 21% -> 20% of each run, Pallas kernels for 0% -> 0%
where the time goes in v6:
time: 240 us; the launch traced here: 238 us
  waiting for transfers between devices  86.3 us (36%)
  starting transfers between devices  51.3 us (21%)
  local copies, waits for them, and re-layouts  46.6 us (19%)
  matrix products  22.6 us (9%)
  blocking collectives  20.1 us (8%)
  other arithmetic  10.4 us (4%)
    all_to_all x1, waiting for transfers between devices, body(): back = lax.all_to_all(outgoing, seq_axes, 0, 0, tiled=True)  42.1 us
    all_to_all x1, waiting for transfers between devices, body(): lax.all_to_all(send.reshape(n_experts, SLOTS, width), seq_axes, 0, 0, til...  24.4 us
    ppermute x4, starting transfers between devices, shifted(): got_value = lax.ppermute(value, 'sz', pairs)  21.9 us
    all_to_all x1, blocking collectives, body(): lax.all_to_all(jnp.stack([mix_q, att_q], axis=1), 'sy', 0, 3, tiled=True)  20.1 us
    unnamed x30, local copies, waits for them, and re-layouts  14.7 us
    all_to_all x1, starting transfers between devices, body(): lax.all_to_all(send.reshape(n_experts, SLOTS, width), seq_axes, 0, 0, til...  11.4 us
    ppermute x4, waiting for transfers between devices, shifted(): got_value = lax.ppermute(value, 'sz', pairs)  9.35 us
    concatenate x2, local copies, waits for them, and re-layouts, body(): jnp.concatenate([q_split, k_split, decay_parts.astype(jnp.bfloat16), info...  8.05 us
  transfers between devices with their start and end apart: 10, of which 6 were waited for; matrix products, arithmetic and copies ran while one was open for 20% of the time, Pallas kernels for 0%

profile of v6, /device:TPU:36, one launch (start us, length us, event | category | flops | bytes accessed | tf_op | source)
XLA Modules:
  0.0 238.3 jit_solution(17730635020280823125)
XLA Ops:
  3.0 3.1 %convolution_convert_fusion = bf16[512,2048]{1,0:T(8,128)(2,1)} fusion(bf16[512,128]{1,0:T(8,128)(2,1)S(1)} %fusion.52, bf16[128,2048]{1,0:T(8,128)(2,1)} %param.10), kind=kOutput, calls=%fused_computation.7 | convolution fusion | flops 269484032 | bytes 2752512 | tf_op jit(solution)/shard_map/dot_general | solution.py:63
  6.1 11.4 %all-to-all-start.1 = ((bf16[32,16,2048]{2,1,0:T(8,128)(2,1)}), bf16[32,16,2048]{2,1,0:T(8,128)(2,1)}, u32[]{:S(2)}, u32[]{:S(2)}) async-start(bf16[32,16,2048]{2,1,0:T(8,128)(2,1)} %bitcast.179), calls=%async_computation.1 | async-start | bytes 4194304 | tf_op jit(solution)/shard_map/all_to_all | solution.py:100
  17.5 2.1 copy.187
  28.6 5.6 %concatenate.6 = bf16[4,272,512]{1,2,0:T(8,128)(2,1)} concatenate(bf16[4,128,512]{1,2,0:T(8,128)(2,1)} %bitcast.182, bf16[4,128,512]{1,2,0:T(8,128)(2,1)} %bitcast.183, bf16[4,1,512]{1,2,0:T(8,128)(2,1)} %copy.191, bf16[4,1,512]{1,2,0:T(8,128)(2,1)} %copy.192, bf16[4,1,512]{1,2,0:T(8,128)(2,1)} %copy.193, bf16[4,3,512]{1,2,0:T(8,128)(2,1)} %broadcast_in_dim.17, ...), dimensions={1} | concatenate | bytes 2228224 | tf_op jit(solution)/shard_map/concatenate | solution.py:78
  34.2 2.5 %copy.194 = bf16[4,272,512]{2,1,0:T(8,128)(2,1)} copy(bf16[4,272,512]{1,2,0:T(8,128)(2,1)} %concatenate.6) | data formatting | bytes 2228224 | tf_op jit(solution)/shard_map/concatenate | solution.py:78
  36.7 6.2 %reshape_squeeze.3 = bf16[768,4,512]{2,1,0:T(4,128)(2,1)} reshape(bf16[1,768,2048]{2,1,0:T(8,128)(2,1)} %param.15) | data formatting | bytes 6291456 | tf_op jit(solution)/shard_map/reshape;squeeze | solution.py:105
  42.9 24.4 %all-to-all-done.1 = bf16[32,16,2048]{2,1,0:T(8,128)(2,1)} async-done(((bf16[32,16,2048]{2,1,0:T(8,128)(2,1)}), bf16[32,16,2048]{2,1,0:T(8,128)(2,1)}, u32[]{:S(2)}, u32[]{:S(2)}) %all-to-all-start.1) | async-done | bytes 2097184 | tf_op jit(solution)/shard_map/all_to_all | solution.py:100
  67.2 4.3 %all-to-all-start = ((bf16[4,272,512]{2,1,0:T(8,128)(2,1)}), bf16[4,272,512]{2,1,0:T(8,128)(2,1)}, u32[]{:S(2)}, u32[]{:S(2)}) async-start(bf16[4,272,512]{2,1,0:T(8,128)(2,1)} %copy.194), calls=%async_computation | async-start | bytes 2228224 | tf_op jit(solution)/shard_map/all_to_all | solution.py:88
  71.5 3.5 %fusion.4 = f32[512,768]{1,0:T(8,128)S(1)} fusion(bf16[512,2048]{1,0:T(8,128)(2,1)} %bitcast.14, bf16[1,2048,768]{2,1,0:T(8,128)(2,1)S(1)} %copy-done), kind=kOutput, calls=%fused_computation.4 | convolution fusion | flops 1610612736 | bytes 6815744 | tf_op jit(solution)/shard_map/dot_general | solution.py:12
  75.1 3.8 %multiply_convert_fusion = bf16[512,768]{1,0:T(8,128)(2,1)S(1)} fusion(f32[512,768]{1,0:T(8,128)S(1)} %fusion.4, bf16[512,2048]{1,0:T(8,128)(2,1)} %bitcast.14, bf16[1,2048,768]{2,1,0:T(8,128)(2,1)S(1)} %copy-done.10, f32[768]{0:T(1024)S(1)} %multiply_reduce_fusion.1), kind=kOutput, calls=%fused_computation.9 | convolution fusion | flops 1613758464 | bytes 7605248 | tf_op jit(solution)/shard_map/dot_general | solution.py:13
  78.9 3.2 %fusion.7 = bf16[8,64,4,512]{3,1,2,0:T(8,128)(2,1)} fusion(bf16[8,64,768,1]{2,1,3,0:T(8,128)(2,1)S(1)} %bitcast.199, bf16[768,4,512]{2,1,0:T(4,128)(2,1)S(1)} %copy-done.3), kind=kOutput, calls=%fused_computation.8 | convolution fusion | flops 1611661312 | bytes 6029312 | tf_op jit(solution)/shard_map/zrk,kjc->zjrc/dot_general | solution.py:102
  82.2 4.2 %all-to-all-done = bf16[4,272,512]{2,1,0:T(8,128)(2,1)} async-done(((bf16[4,272,512]{2,1,0:T(8,128)(2,1)}), bf16[4,272,512]{2,1,0:T(8,128)(2,1)}, u32[]{:S(2)}, u32[]{:S(2)}) %all-to-all-start) | async-done | bytes 1114144 | tf_op jit(solution)/shard_map/all_to_all | solution.py:88
  86.3 6.1 %all-to-all-start.2 = ((bf16[32,64,512]{2,1,0:T(8,128)(2,1)}), bf16[32,64,512]{2,1,0:T(8,128)(2,1)}, u32[]{:S(2)}, u32[]{:S(2)}) async-start(bf16[32,64,512]{2,1,0:T(8,128)(2,1)} %bitcast.185), calls=%async_computation.2 | async-start | bytes 4194304 | tf_op jit(solution)/shard_map/all_to_all | solution.py:109
  92.5 2.2 fusion.74
  94.7 2.1 copy.224
  99.3 42.1 %all-to-all-done.2 = bf16[32,64,512]{2,1,0:T(8,128)(2,1)} async-done(((bf16[32,64,512]{2,1,0:T(8,128)(2,1)}), bf16[32,64,512]{2,1,0:T(8,128)(2,1)}, u32[]{:S(2)}, u32[]{:S(2)}) %all-to-all-start.2) | async-done | bytes 2097184 | tf_op jit(solution)/shard_map/all_to_all | solution.py:109
  141.4 2.8 %copy.199 = bf16[32,64,512]{2,0,1:T(8,128)(2,1)S(1)} copy(bf16[32,64,512]{2,1,0:T(8,128)(2,1)} %all-to-all-done.2) | data formatting | bytes 4194304 | tf_op jit(solution)/shard_map/all_to_all | solution.py:109
  147.6 4.2 %collective-permute-start.4 = (f32[4,128,128]{2,1,0:T(8,128)S(1)}, f32[4,128,128]{2,1,0:T(8,128)}, u32[]{:S(2)}, u32[]{:S(2)}) collective-permute-start(f32[4,128,128]{2,1,0:T(8,128)S(1)} %fusion.53), channel_id=1, source_target_pairs={{0,4},{4,8},{8,12},{12,16},{16,20},{20,24},{24,28},{1,5},{5,9},{9,... | collective-permute-start | bytes 786440 | tf_op jit(solution)/shard_map/ppermute | solution.py:159
  151.7 3.3 %collective-permute-start.3 = (f32[4,128,128]{2,1,0:T(8,128)S(1)}, f32[4,128,128]{2,1,0:T(8,128)}, u32[]{:S(2)}, u32[]{:S(2)}) collective-permute-start(f32[4,128,128]{2,1,0:T(8,128)S(1)} %fusion.53), channel_id=1, source_target_pairs={{0,8},{4,12},{8,16},{12,20},{16,24},{20,28},{1,9},{5,13},{9,17},{1... | collective-permute-start | bytes 786440 | tf_op jit(solution)/shard_map/ppermute | solution.py:159
  156.7 2.1 collective-permute-start.1
  158.8 6.4 %collective-permute-done = f32[4]{0:T(128)S(1)} collective-permute-done((f32[4]{0:T(128)S(1)}, f32[4]{0:T(128)S(1)}, u32[]{:S(2)}, u32[]{:S(2)}) %collective-permute-start) | collective-permute-done | bytes 48 | tf_op jit(solution)/shard_map/ppermute | solution.py:160
  166.3 6.1 %collective-permute-start.5 = (f32[4,128,128]{2,1,0:T(8,128)S(1)}, f32[4,128,128]{2,1,0:T(8,128)}, u32[]{:S(2)}, u32[]{:S(2)}) collective-permute-start(f32[4,128,128]{2,1,0:T(8,128)S(1)} %multiply_add_fusion.4), channel_id=1, source_target_pairs={{0,8},{4,12},{8,16},{12,20},{16,24},{20,28},{1,9},{5,13},{9,17},{1... | collective-permute-start | bytes 786440 | tf_op jit(solution)/shard_map/ppermute | solution.py:159
  172.4 2.0 copy.223
  174.6 3.7 %collective-permute-start.2 = (f32[4]{0:T(128)S(1)}, f32[4]{0:T(128)S(1)}, u32[]{:S(2)}, u32[]{:S(2)}) collective-permute-start(f32[4]{0:T(128)S(1)} %get-tuple-element.20), channel_id=1, source_target_pairs={{0,8},{4,12},{8,16},{12,20},{16,24},{20,28},{1,9},{5,13},{9,17},{1... | collective-permute-start | bytes 56 | tf_op jit(solution)/shard_map/ppermute | solution.py:160
  180.8 8.5 %collective-permute-start.6 = (f32[4,128,128]{2,1,0:T(8,128)S(1)}, f32[4,128,128]{2,1,0:T(8,128)S(1)}, u32[]{:S(2)}, u32[]{:S(2)}) collective-permute-start(f32[4,128,128]{2,1,0:T(8,128)S(1)} %multiply_add_fusion.3), channel_id=1, source_target_pairs={{0,16},{4,20},{8,24},{12,28},{1,17},{5,21},{9,25},{13,29},{2,18},{... | collective-permute-start | bytes 786440 | tf_op jit(solution)/shard_map/ppermute | solution.py:159
  190.5 7.9 %collective-permute-done.6 = f32[4,128,128]{2,1,0:T(8,128)S(1)} collective-permute-done((f32[4,128,128]{2,1,0:T(8,128)S(1)}, f32[4,128,128]{2,1,0:T(8,128)S(1)}, u32[]{:S(2)}, u32[]{:S(2)}) %collective-permute-start.6) | collective-permute-done | bytes 262176 | tf_op jit(solution)/shard_map/ppermute | solution.py:159
  198.5 2.0 fusion.16
  200.6 3.6 %multiply_reduce_fusion = (f32[4,128,4]{1,2,0:T(4,128)S(1)}, f32[4,128,4,128]{1,3,2,0:T(8,128)}) fusion(f32[4,128,4,128]{1,3,2,0:T(8,128)} %fusion.16, bf16[4,128,4,128]{1,3,2,0:T(8,128)(2,1)} %bitcast.188, bf16[4,128,4,128]{1,3,2,0:T(8,128)(2,1)} %bitcast.186, f32[4,4,128]{2,1,0:T(4,128)S(1)} %reduce_window_sum.11, ...), kind=kOutput, calls=%fused_computation.32 | convolution fusion | flops 136312832 | bytes 3702784 | tf_op jit(solution)/shard_map/bhts,bshd->bthd/dot_general | solution.py:138
  204.1 2.1 multiply_convert_fusion.1
  209.7 20.1 %all_to_all.33 = bf16[4,2,128,512]{3,2,1,0:T(8,128)(2,1)} all-to-all(bf16[4,2,128,512]{3,2,1,0:T(8,128)(2,1)S(1)} %copy.211), channel_id=1, replica_groups=mesh['dp'=8,'sz'=8,'sy'=4] {'sy'}, dimensions={0} | all-to-all | bytes 2097152 | tf_op jit(solution)/shard_map/all_to_all | solution.py:183
  229.8 2.3 copy.212
  232.0 2.2 slice_bitcast_fusion
  (95 shorter events, 31.4 us)
Async XLA Ops:
  0.6 70.9 %copy-start = (bf16[1,2048,768]{2,1,0:T(8,128)(2,1)S(1)}, bf16[1,2048,768]{2,1,0:T(8,128)(2,1)}, u32[]{:S(2)}) copy-start(bf16[1,2048,768]{2,1,0:T(8,128)(2,1)} %param.13) | copy-start | bytes 9437188
  6.1 61.1 %all-to-all-start.1 = ((bf16[32,16,2048]{2,1,0:T(8,128)(2,1)}), bf16[32,16,2048]{2,1,0:T(8,128)(2,1)}, u32[]{:S(2)}, u32[]{:S(2)}) async-start(bf16[32,16,2048]{2,1,0:T(8,128)(2,1)} %bitcast.179), calls=%async_computation.1 | async-start | bytes 4194304 | tf_op jit(solution)/shard_map/all_to_all | solution.py:100
  17.5 4.2 %copy-start.8 = (f32[16,128]{1,0:T(8,128)S(1)}, f32[16,128]{1,0:T(8,128)}, u32[]{:S(2)}) copy-start(f32[16,128]{1,0:T(8,128)} %param.19) | copy-start | bytes 24580
  17.5 7.4 %copy-start.6 = (bf16[2048,32]{0,1:T(8,128)(2,1)S(1)}, bf16[2048,32]{0,1:T(8,128)(2,1)}, u32[]{:S(2)}) copy-start(bf16[2048,32]{0,1:T(8,128)(2,1)} %param.12) | copy-start | bytes 393220
  17.5 8.7 %copy-start.7 = (s32[128,2]{0,1:T(2,128)S(1)}, s32[128,2]{0,1:T(2,128)}, u32[]{:S(2)}) copy-start(s32[128,2]{0,1:T(2,128)} %param.11) | copy-start | bytes 3076
  36.7 6.2 %copy-start.9 = (s32[1,768]{1,0:T(1,128)S(1)}, s32[1,768]{1,0:T(1,128)}, u32[]{:S(2)}) copy-start(s32[1,768]{1,0:T(1,128)} %param.16) | copy-start | bytes 9220
  67.2 19.1 %all-to-all-start = ((bf16[4,272,512]{2,1,0:T(8,128)(2,1)}), bf16[4,272,512]{2,1,0:T(8,128)(2,1)}, u32[]{:S(2)}, u32[]{:S(2)}) async-start(bf16[4,272,512]{2,1,0:T(8,128)(2,1)} %copy.194), calls=%async_computation | async-start | bytes 2228224 | tf_op jit(solution)/shard_map/all_to_all | solution.py:88
  71.5 3.6 %copy-start.10 = (bf16[1,2048,768]{2,1,0:T(8,128)(2,1)S(1)}, bf16[1,2048,768]{2,1,0:T(8,128)(2,1)}, u32[]{:S(2)}) copy-start(bf16[1,2048,768]{2,1,0:T(8,128)(2,1)} %param.14) | copy-start | bytes 9437188
  75.1 3.8 %copy-start.3 = (bf16[768,4,512]{2,1,0:T(4,128)(2,1)S(1)}, bf16[768,4,512]{2,1,0:T(4,128)(2,1)}, u32[]{:S(2)}) copy-start(bf16[768,4,512]{2,1,0:T(4,128)(2,1)} %reshape_squeeze.3) | copy-start | bytes 9437188
  86.3 55.1 %all-to-all-start.2 = ((bf16[32,64,512]{2,1,0:T(8,128)(2,1)}), bf16[32,64,512]{2,1,0:T(8,128)(2,1)}, u32[]{:S(2)}, u32[]{:S(2)}) async-start(bf16[32,64,512]{2,1,0:T(8,128)(2,1)} %bitcast.185), calls=%async_computation.2 | async-start | bytes 4194304 | tf_op jit(solution)/shard_map/all_to_all | solution.py:109
  144.7 1.0 copy-start.4
  145.3 2.3 copy-start.2
  146.4 1.0 copy-start.1
  147.6 17.6 %collective-permute-start.4 = (f32[4,128,128]{2,1,0:T(8,128)S(1)}, f32[4,128,128]{2,1,0:T(8,128)}, u32[]{:S(2)}, u32[]{:S(2)}) collective-permute-start(f32[4,128,128]{2,1,0:T(8,128)S(1)} %fusion.53), channel_id=1, source_target_pairs={{0,4},{4,8},{8,12},{12,16},{16,20},{20,24},{24,28},{1,5},{5,9},{9,... | collective-permute-start | bytes 786440 | tf_op jit(solution)/shard_map/ppermute | solution.py:159
  151.7 13.5 %collective-permute-start.3 = (f32[4,128,128]{2,1,0:T(8,128)S(1)}, f32[4,128,128]{2,1,0:T(8,128)}, u32[]{:S(2)}, u32[]{:S(2)}) collective-permute-start(f32[4,128,128]{2,1,0:T(8,128)S(1)} %fusion.53), channel_id=1, source_target_pairs={{0,8},{4,12},{8,16},{12,20},{16,24},{20,28},{1,9},{5,13},{9,17},{1... | collective-permute-start | bytes 786440 | tf_op jit(solution)/shard_map/ppermute | solution.py:159
  155.0 10.2 %collective-permute-start = (f32[4]{0:T(128)S(1)}, f32[4]{0:T(128)S(1)}, u32[]{:S(2)}, u32[]{:S(2)}) collective-permute-start(f32[4]{0:T(128)S(1)} %get-tuple-element.53), channel_id=1, source_target_pairs={{0,8},{4,12},{8,16},{12,20},{16,24},{20,28},{1,9},{5,13},{9,17},{1... | collective-permute-start | bytes 56 | tf_op jit(solution)/shard_map/ppermute | solution.py:160
  156.7 8.5 %collective-permute-start.1 = (f32[4]{0:T(128)S(1)}, f32[4]{0:T(128)S(1)}, u32[]{:S(2)}, u32[]{:S(2)}) collective-permute-start(f32[4]{0:T(128)S(1)} %get-tuple-element.53), channel_id=1, source_target_pairs={{0,4},{4,8},{8,12},{12,16},{16,20},{20,24},{24,28},{1,5},{5,9},{9,... | collective-permute-start | bytes 56 | tf_op jit(solution)/shard_map/ppermute | solution.py:160
  166.3 13.4 %collective-permute-start.5 = (f32[4,128,128]{2,1,0:T(8,128)S(1)}, f32[4,128,128]{2,1,0:T(8,128)}, u32[]{:S(2)}, u32[]{:S(2)}) collective-permute-start(f32[4,128,128]{2,1,0:T(8,128)S(1)} %multiply_add_fusion.4), channel_id=1, source_target_pairs={{0,8},{4,12},{8,16},{12,20},{16,24},{20,28},{1,9},{5,13},{9,17},{1... | collective-permute-start | bytes 786440 | tf_op jit(solution)/shard_map/ppermute | solution.py:159
  174.5 24.0 %copy-start.5 = (bf16[4,128,512]{1,2,0:T(8,128)(2,1)S(1)}, bf16[4,128,512]{1,2,0:T(8,128)(2,1)}, u32[]{:S(2)}) copy-start(bf16[4,128,512]{1,2,0:T(8,128)(2,1)} %copy.223) | copy-start | bytes 1572868
  174.6 14.7 %collective-permute-start.2 = (f32[4]{0:T(128)S(1)}, f32[4]{0:T(128)S(1)}, u32[]{:S(2)}, u32[]{:S(2)}) collective-permute-start(f32[4]{0:T(128)S(1)} %get-tuple-element.20), channel_id=1, source_target_pairs={{0,8},{4,12},{8,16},{12,20},{16,24},{20,28},{1,9},{5,13},{9,17},{1... | collective-permute-start | bytes 56 | tf_op jit(solution)/shard_map/ppermute | solution.py:160
  180.8 17.6 %collective-permute-start.6 = (f32[4,128,128]{2,1,0:T(8,128)S(1)}, f32[4,128,128]{2,1,0:T(8,128)S(1)}, u32[]{:S(2)}, u32[]{:S(2)}) collective-permute-start(f32[4,128,128]{2,1,0:T(8,128)S(1)} %multiply_add_fusion.3), channel_id=1, source_target_pairs={{0,16},{4,20},{8,24},{12,28},{1,17},{5,21},{9,25},{13,29},{2,18},{... | collective-permute-start | bytes 786440 | tf_op jit(solution)/shard_map/ppermute | solution.py:159

commit v7 on v4

--- a/solution.py
+++ b/solution.py
@@ -8,13 +8,12 @@
 GROUP = 4
 
 
-def expert_apply(token_rows, gate_matrix, up_matrix, down_matrix, levels):
+def expert_spikes(token_rows, gate_matrix, up_matrix, levels):
     gate_values = jnp.dot(token_rows, gate_matrix, preferred_element_type=jnp.float32)
     up_values = jnp.dot(token_rows, up_matrix, preferred_element_type=jnp.float32)
     hidden = jax.nn.silu(gate_values) * up_values
     threshold = 0.125 * levels.astype(jnp.float32)
-    spikes = (threshold * jnp.tanh(hidden / threshold)).astype(jnp.bfloat16)
-    return jnp.dot(spikes, down_matrix, preferred_element_type=jnp.float32).astype(jnp.bfloat16)
+    return (threshold * jnp.tanh(hidden / threshold)).astype(jnp.bfloat16)
 
 
 def split3(values):
@@ -99,10 +98,13 @@
     row_second = (got_info[:, 2] * SLOTS + got_info[:, 3]).astype(jnp.int32)
 
     recv = lax.all_to_all(send.reshape(n_experts, SLOTS, width), seq_axes, 0, 0, tiled=True)
-    computed = expert_apply(
-        recv.reshape(n_rows, width), w_gate[0], w_up[0], w_down[0], spike_level[0]
-    )
-    outgoing = computed.reshape(n_sz, n_sy, SLOTS, n_sy, qw).transpose(0, 3, 1, 2, 4)
+    spikes = expert_spikes(recv.reshape(n_rows, width), w_gate[0], w_up[0], spike_level[0])
+    outgoing = jnp.einsum(
+        "zrk,kjc->zjrc",
+        spikes.reshape(n_sz, n_sy * SLOTS, -1),
+        w_down[0].reshape(-1, n_sy, qw),
+        preferred_element_type=jnp.float32,
+    ).astype(jnp.bfloat16)
     outgoing = outgoing.reshape(n_sz * n_sy, n_sy * SLOTS, qw)
     back = lax.all_to_all(outgoing, seq_axes, 0, 0, tiled=True)
     table = back.reshape(n_experts, n_sy, SLOTS, qw)
@@ -171,9 +173,9 @@
     total_out = intra + inter
     normed = total_out * lax.rsqrt(jnp.mean(total_out * total_out, axis=3, keepdims=True) + 1e-06)
     att_q = normed.astype(jnp.bfloat16).reshape(n_sy, count, qw)
-    home = lax.all_to_all(jnp.stack([mix_q, att_q], axis=1), "sy", 0, 0, tiled=True)
-    expert_mix = home[:, 0].transpose(1, 0, 2).reshape(count, width)
-    attended = home[:, 1].transpose(1, 0, 2).reshape(count, heads * hd)
+    home = lax.all_to_all(jnp.stack([mix_q, att_q], axis=1), "sy", 0, 3, tiled=True)
+    expert_mix = home[0, 0]
+    attended = home[0, 1]
     return (expert_mix, attended)
 
 

time: 249 us -> 242 us (0.972)
  matrix products: 25.8 us -> 22.6 us
    reshape x2 -> x0, local copies, waits for them, and re-layouts: 7.96 us -> none  [body(): computed.reshape(n_sz, n_sy, SLOTS, n_sy, qw).transpose(0, 3, 1, 2, 4)]
    all_to_all x1, waiting for transfers between devices: 30.7 us -> 24.5 us  [body(): lax.all_to_all(send.reshape(n_experts, SLOTS, width), seq_axes, 0, 0, til...]
    another operation x4 -> x5, local copies, waits for them, and re-layouts: 3.2 us -> 9.41 us  [the longest x1 6.16 us: body(): w_down[0].reshape(-1, n_sy, qw)]
    all_to_all x1, waiting for transfers between devices: 0.01 us -> 4.15 us  [body(): got = lax.all_to_all(packed, 'sy', 0, 0, tiled=True)]
    unnamed x33 -> x35, local copies, waits for them, and re-layouts: 19.3 us -> 15.2 us
    dot_general x2 -> x3, matrix products: 13.8 us -> 10.6 us  [the longest x1 3.82 us: expert_spikes(): jnp.dot(token_rows, up_matrix, preferred_element_type=jnp.float32)]
  transfers between devices with their start and end apart: 4 -> 4, of which waited for: 3 -> 4; matrix products, arithmetic and copies ran while one was open for 20% -> 19% of each run, Pallas kernels for 0% -> 0%
where the time goes in v7:
time: 242 us; the launch traced here: 239 us
  waiting for transfers between devices  105 us (43%)
  local copies, waits for them, and re-layouts  49 us (20%)
  matrix products  22.6 us (9%)
  starting transfers between devices  22.2 us (9%)
  blocking collectives  15.2 us (6%)
  between operations  14.5 us (6%)
  other arithmetic  10.2 us (4%)
    all_to_all x1, waiting for transfers between devices, body(): back = lax.all_to_all(outgoing, seq_axes, 0, 0, tiled=True)  41.6 us
    all_gather x1, waiting for transfers between devices, body(): pieces_packed = lax.all_gather(piece_packed, 'sz', axis=0)  35.2 us
    all_to_all x1, waiting for transfers between devices, body(): lax.all_to_all(send.reshape(n_experts, SLOTS, width), seq_axes, 0, 0, til...  24.5 us
    unnamed x35, local copies, waits for them, and re-layouts  15.2 us
    all_to_all x1, blocking collectives, body(): lax.all_to_all(jnp.stack([mix_q, att_q], axis=1), 'sy', 0, 3, tiled=True)  15.2 us
    all_to_all x1, starting transfers between devices, body(): lax.all_to_all(send.reshape(n_experts, SLOTS, width), seq_axes, 0, 0, til...  11.5 us
    concatenate x2, local copies, waits for them, and re-layouts, body(): jnp.concatenate([q_split, k_split, decay_parts.astype(jnp.bfloat16), info...  8.04 us
    another operation x1, local copies, waits for them, and re-layouts, body(): w_down[0].reshape(-1, n_sy, qw)  6.16 us
  transfers between devices with their start and end apart: 4, of which 4 were waited for; matrix products, arithmetic and copies ran while one was open for 19% of the time, Pallas kernels for 0%

profile of v7, /device:TPU:36, one launch (start us, length us, event | category | flops | bytes accessed | tf_op | source)
XLA Modules:
  0.0 239.1 jit_solution(6094805414795426722)
XLA Ops:
  9.5 3.1 %convolution_convert_fusion = bf16[512,2048]{1,0:T(8,128)(2,1)} fusion(bf16[512,128]{1,0:T(8,128)(2,1)S(1)} %fusion.52, bf16[128,2048]{1,0:T(8,128)(2,1)} %param.12), kind=kOutput, calls=%fused_computation.7 | convolution fusion | flops 269484032 | bytes 2752512 | tf_op jit(solution)/shard_map/dot_general | solution.py:63
  12.6 11.5 %all-to-all-start.1 = ((bf16[32,16,2048]{2,1,0:T(8,128)(2,1)}), bf16[32,16,2048]{2,1,0:T(8,128)(2,1)}, u32[]{:S(2)}, u32[]{:S(2)}) async-start(bf16[32,16,2048]{2,1,0:T(8,128)(2,1)} %bitcast.197), calls=%async_computation.1 | async-start | bytes 4194304 | tf_op jit(solution)/shard_map/all_to_all | solution.py:100
  24.2 1.3 fusion.75
  29.4 2.0 copy.187
  31.4 2.0 copy.188
  35.2 5.6 %concatenate.11 = bf16[4,272,512]{1,2,0:T(8,128)(2,1)} concatenate(bf16[4,128,512]{1,2,0:T(8,128)(2,1)} %bitcast.206, bf16[4,128,512]{1,2,0:T(8,128)(2,1)} %bitcast.207, bf16[4,1,512]{1,2,0:T(8,128)(2,1)} %copy.191, bf16[4,1,512]{1,2,0:T(8,128)(2,1)} %copy.192, bf16[4,1,512]{1,2,0:T(8,128)(2,1)} %copy.193, bf16[4,3,512]{1,2,0:T(8,128)(2,1)} %broadcast_in_dim.10, ...), dimensions={1} | concatenate | bytes 2228224 | tf_op jit(solution)/shard_map/concatenate | solution.py:78
  40.8 2.5 %copy.194 = bf16[4,272,512]{2,1,0:T(8,128)(2,1)} copy(bf16[4,272,512]{1,2,0:T(8,128)(2,1)} %concatenate.11) | data formatting | bytes 2228224 | tf_op jit(solution)/shard_map/concatenate | solution.py:78
  43.3 6.2 %reshape_squeeze.3 = bf16[768,4,512]{2,1,0:T(4,128)(2,1)} reshape(bf16[1,768,2048]{2,1,0:T(8,128)(2,1)} %param.17) | data formatting | bytes 6291456 | tf_op jit(solution)/shard_map/reshape;squeeze | solution.py:105
  49.4 24.5 %all-to-all-done.1 = bf16[32,16,2048]{2,1,0:T(8,128)(2,1)} async-done(((bf16[32,16,2048]{2,1,0:T(8,128)(2,1)}), bf16[32,16,2048]{2,1,0:T(8,128)(2,1)}, u32[]{:S(2)}, u32[]{:S(2)}) %all-to-all-start.1) | async-done | bytes 2097184 | tf_op jit(solution)/shard_map/all_to_all | solution.py:100
  73.9 4.3 %all-to-all-start = ((bf16[4,272,512]{2,1,0:T(8,128)(2,1)}), bf16[4,272,512]{2,1,0:T(8,128)(2,1)}, u32[]{:S(2)}, u32[]{:S(2)}) async-start(bf16[4,272,512]{2,1,0:T(8,128)(2,1)} %copy.194), calls=%async_computation | async-start | bytes 2228224 | tf_op jit(solution)/shard_map/all_to_all | solution.py:88
  78.2 3.5 %fusion.4 = f32[512,768]{1,0:T(8,128)S(1)} fusion(bf16[512,2048]{1,0:T(8,128)(2,1)} %bitcast.14, bf16[1,2048,768]{2,1,0:T(8,128)(2,1)S(1)} %copy-done), kind=kOutput, calls=%fused_computation.4 | convolution fusion | flops 1610612736 | bytes 6815744 | tf_op jit(solution)/shard_map/dot_general | solution.py:12
  81.8 3.8 %multiply_convert_fusion = bf16[512,768]{1,0:T(8,128)(2,1)S(1)} fusion(f32[512,768]{1,0:T(8,128)S(1)} %fusion.4, bf16[512,2048]{1,0:T(8,128)(2,1)} %bitcast.14, bf16[1,2048,768]{2,1,0:T(8,128)(2,1)S(1)} %copy-done.12, f32[768]{0:T(1024)S(1)} %multiply_reduce_fusion.1), kind=kOutput, calls=%fused_computation.9 | convolution fusion | flops 1613758464 | bytes 7605248 | tf_op jit(solution)/shard_map/dot_general | solution.py:13
  85.6 3.2 %fusion.7 = bf16[8,64,4,512]{3,1,2,0:T(8,128)(2,1)} fusion(bf16[8,64,768,1]{2,1,3,0:T(8,128)(2,1)S(1)} %bitcast.229, bf16[768,4,512]{2,1,0:T(4,128)(2,1)S(1)} %copy-done.2), kind=kOutput, calls=%fused_computation.8 | convolution fusion | flops 1611661312 | bytes 6029312 | tf_op jit(solution)/shard_map/zrk,kjc->zjrc/dot_general | solution.py:102
  88.9 4.2 %all-to-all-done = bf16[4,272,512]{2,1,0:T(8,128)(2,1)} async-done(((bf16[4,272,512]{2,1,0:T(8,128)(2,1)}), bf16[4,272,512]{2,1,0:T(8,128)(2,1)}, u32[]{:S(2)}, u32[]{:S(2)}) %all-to-all-start) | async-done | bytes 1114144 | tf_op jit(solution)/shard_map/all_to_all | solution.py:88
  93.0 6.1 %all-to-all-start.2 = ((bf16[32,64,512]{2,1,0:T(8,128)(2,1)}), bf16[32,64,512]{2,1,0:T(8,128)(2,1)}, u32[]{:S(2)}, u32[]{:S(2)}) async-start(bf16[32,64,512]{2,1,0:T(8,128)(2,1)} %bitcast.209), calls=%async_computation.2 | async-start | bytes 4194304 | tf_op jit(solution)/shard_map/all_to_all | solution.py:109
  100.3 2.2 fusion.73
  102.5 2.0 copy.224
  106.5 41.6 %all-to-all-done.2 = bf16[32,64,512]{2,1,0:T(8,128)(2,1)} async-done(((bf16[32,64,512]{2,1,0:T(8,128)(2,1)}), bf16[32,64,512]{2,1,0:T(8,128)(2,1)}, u32[]{:S(2)}, u32[]{:S(2)}) %all-to-all-start.2) | async-done | bytes 2097184 | tf_op jit(solution)/shard_map/all_to_all | solution.py:109
  148.1 2.8 %copy.199 = bf16[32,64,512]{2,0,1:T(8,128)(2,1)S(1)} copy(bf16[32,64,512]{2,1,0:T(8,128)(2,1)} %all-to-all-done.2) | data formatting | bytes 4194304 | tf_op jit(solution)/shard_map/all_to_all | solution.py:109
  155.9 2.0 copy.223
  158.0 35.2 %all-gather.3.cloned.1.call-done = f32[4160,128]{1,0:T(8,128)} async-done(((f32[520,128]{1,0:T(8,128)}), f32[4160,128]{1,0:T(8,128)}) %all-gather.3.cloned.1.call-update) | async-done | bytes 2129936 | tf_op jit(solution)/shard_map/all_gather | solution.py:159
  193.2 1.7 fusion.72
  197.3 2.1 fusion.16
  199.4 3.6 %multiply_reduce_fusion = (f32[4,128,4]{1,2,0:T(4,128)S(1)}, f32[4,128,4,128]{1,3,2,0:T(8,128)}) fusion(f32[4,128,4,128]{1,3,2,0:T(8,128)} %fusion.16, bf16[4,128,4,128]{1,3,2,0:T(8,128)(2,1)} %bitcast.218, bf16[4,128,4,128]{1,3,2,0:T(8,128)(2,1)} %bitcast.210, f32[4,4,128]{2,1,0:T(4,128)S(1)} %reduce_window_sum.11, ...), kind=kOutput, calls=%fused_computation.33 | convolution fusion | flops 136312832 | bytes 3702784 | tf_op jit(solution)/shard_map/bhts,bshd->bthd/dot_general | solution.py:138
  202.9 2.1 multiply_convert_fusion.1
  205.1 2.0 copy.222
  207.1 1.3 pad_maximum_fusion
  208.5 15.2 %all_to_all.33 = bf16[4,2,128,512]{3,2,1,0:T(8,128)(2,1)} all-to-all(bf16[4,2,128,512]{3,2,1,0:T(8,128)(2,1)S(1)} %copy.211), channel_id=1, replica_groups=mesh['dp'=8,'sz'=8,'sy'=4] {'sy'}, dimensions={0} | all-to-all | bytes 2097152 | tf_op jit(solution)/shard_map/all_to_all | solution.py:176
  223.7 2.3 copy.212
  226.0 2.2 slice_bitcast_fusion
  228.2 2.0 copy.213
  230.2 2.0 copy.214
  (98 shorter events, 18.3 us)
Async XLA Ops:
  7.2 71.0 %copy-start = (bf16[1,2048,768]{2,1,0:T(8,128)(2,1)S(1)}, bf16[1,2048,768]{2,1,0:T(8,128)(2,1)}, u32[]{:S(2)}) copy-start(bf16[1,2048,768]{2,1,0:T(8,128)(2,1)} %param.15) | copy-start | bytes 9437188
  12.6 11.6 %copy-start.8 = (bf16[2048,32]{0,1:T(8,128)(2,1)S(1)}, bf16[2048,32]{0,1:T(8,128)(2,1)}, u32[]{:S(2)}) copy-start(bf16[2048,32]{0,1:T(8,128)(2,1)} %param.14) | copy-start | bytes 393220
  12.6 12.9 %copy-start.9 = (s32[128,2]{0,1:T(2,128)S(1)}, s32[128,2]{0,1:T(2,128)}, u32[]{:S(2)}) copy-start(s32[128,2]{0,1:T(2,128)} %param.13) | copy-start | bytes 3076
  12.6 13.4 %copy-start.10 = (f32[16,128]{1,0:T(8,128)S(1)}, f32[16,128]{1,0:T(8,128)}, u32[]{:S(2)}) copy-start(f32[16,128]{1,0:T(8,128)} %param.21) | copy-start | bytes 24580
  12.6 61.3 %all-to-all-start.1 = ((bf16[32,16,2048]{2,1,0:T(8,128)(2,1)}), bf16[32,16,2048]{2,1,0:T(8,128)(2,1)}, u32[]{:S(2)}, u32[]{:S(2)}) async-start(bf16[32,16,2048]{2,1,0:T(8,128)(2,1)} %bitcast.197), calls=%async_computation.1 | async-start | bytes 4194304 | tf_op jit(solution)/shard_map/all_to_all | solution.py:100
  43.3 6.2 %copy-start.11 = (s32[1,768]{1,0:T(1,128)S(1)}, s32[1,768]{1,0:T(1,128)}, u32[]{:S(2)}) copy-start(s32[1,768]{1,0:T(1,128)} %param.18) | copy-start | bytes 9220
  73.9 19.1 %all-to-all-start = ((bf16[4,272,512]{2,1,0:T(8,128)(2,1)}), bf16[4,272,512]{2,1,0:T(8,128)(2,1)}, u32[]{:S(2)}, u32[]{:S(2)}) async-start(bf16[4,272,512]{2,1,0:T(8,128)(2,1)} %copy.194), calls=%async_computation | async-start | bytes 2228224 | tf_op jit(solution)/shard_map/all_to_all | solution.py:88
  78.2 3.5 %copy-start.12 = (bf16[1,2048,768]{2,1,0:T(8,128)(2,1)S(1)}, bf16[1,2048,768]{2,1,0:T(8,128)(2,1)}, u32[]{:S(2)}) copy-start(bf16[1,2048,768]{2,1,0:T(8,128)(2,1)} %param.16) | copy-start | bytes 9437188
  81.8 3.8 %copy-start.2 = (bf16[768,4,512]{2,1,0:T(4,128)(2,1)S(1)}, bf16[768,4,512]{2,1,0:T(4,128)(2,1)}, u32[]{:S(2)}) copy-start(bf16[768,4,512]{2,1,0:T(4,128)(2,1)} %reshape_squeeze.3) | copy-start | bytes 9437188
  93.0 55.1 %all-to-all-start.2 = ((bf16[32,64,512]{2,1,0:T(8,128)(2,1)}), bf16[32,64,512]{2,1,0:T(8,128)(2,1)}, u32[]{:S(2)}, u32[]{:S(2)}) async-start(bf16[32,64,512]{2,1,0:T(8,128)(2,1)} %bitcast.209), calls=%async_computation.2 | async-start | bytes 4194304 | tf_op jit(solution)/shard_map/all_to_all | solution.py:109
  99.2 94.1 %all-gather.3.cloned.1.call-start = ((), (), s32[]{:S(2)}) async-start(), calls=%async_computation.4 | async-start | bytes 2396160 | tf_op jit(solution)/shard_map/all_gather | solution.py:159
  151.4 1.0 copy-start.3
  151.9 2.1 copy-start.1
  193.2 2.4 %copy-start.7 = (f32[8,4,128,128]{3,2,1,0:T(8,128)S(1)}, f32[8,4,128,128]{3,2,1,0:T(8,128)}, u32[]{:S(2)}) copy-start(f32[8,4,128,128]{3,2,1,0:T(8,128)} %broadcast_dynamic-update-slice_fusion) | copy-start | bytes 6291460
  196.1 1.0 copy-start.4
  196.1 1.1 copy-start.5
  196.1 1.2 copy-start.6
Sparse Core Ops, SparseCore 0:
  155.3 37.9 all-gather.2

commit v8 on v6

--- a/solution.py
+++ b/solution.py
@@ -154,22 +154,29 @@
         lead = lead * block_total[b]
     group_state, group_span = run, lead
 
-    def shifted(value, span, by):
+    state_rows = quarter * hd
+
+    def pack(value, span):
+        span_rows = jnp.zeros((8, hd), jnp.float32).at[0, :quarter].set(span)
+        return jnp.concatenate([value.reshape(state_rows, hd), span_rows], axis=0)
+
+    def unpack(packed):
+        return packed[:state_rows].reshape(quarter, hd, hd), packed[state_rows, :quarter]
+
+    def shifted(packed, by):
         pairs = [(i, i + by) for i in range(n_sz - by)]
-        got_value = lax.ppermute(value, "sz", pairs)
-        got_span = lax.ppermute(span, "sz", pairs)
+        got_value, got_span = unpack(lax.ppermute(packed, "sz", pairs))
         return got_value, jnp.where(zi >= by, got_span, 1.0)
 
     def join(earlier, later):
         (v_e, s_e), (v_l, s_l) = earlier, later
         return (s_l[:, None, None] * v_e + v_l, s_e * s_l)
 
-    one = shifted(group_state, group_span, 1)
-    two = shifted(group_state, group_span, 2)
-    window = join(two, one)
+    own = pack(group_state, group_span)
+    window = join(shifted(own, 2), shifted(own, 1))
     reach = 2
     while reach < n_sz:
-        window = join(shifted(window[0], window[1], reach), window)
+        window = join(shifted(pack(*window), reach), window)
         reach *= 2
     before = window[0]
 
@@ -180,9 +187,17 @@
     total_out = intra + inter
     normed = total_out * lax.rsqrt(jnp.mean(total_out * total_out, axis=3, keepdims=True) + 1e-06)
     att_q = normed.astype(jnp.bfloat16).reshape(n_sy, count, qw)
-    home = lax.all_to_all(jnp.stack([mix_q, att_q], axis=1), "sy", 0, 3, tiled=True)
-    expert_mix = home[0, 0]
-    attended = home[0, 1]
+    yi = lax.axis_index("sy")
+    outgoing_home = jnp.stack([mix_q, att_q], axis=1)
+    expert_mix = jnp.zeros((count, width), jnp.bfloat16)
+    attended = jnp.zeros((count, heads * hd), jnp.bfloat16)
+    for by in range(n_sy):
+        piece = lax.dynamic_index_in_dim(outgoing_home, (yi + by) % n_sy, 0, False)
+        if by:
+            piece = lax.ppermute(piece, "sy", [(i, (i + by) % n_sy) for i in range(n_sy)])
+        column = ((yi - by) % n_sy) * qw
+        expert_mix = lax.dynamic_update_slice(expert_mix, piece[0], (0, column))
+        attended = lax.dynamic_update_slice(attended, piece[1], (0, column))
     return (expert_mix, attended)
 
 

time: 240 us -> 239 us (level)
  waiting for transfers between devices: 86.3 us -> 107 us
  blocking collectives: 20.1 us -> 0 us
  local copies, waits for them, and re-layouts: 46.6 us -> 39.2 us
  other arithmetic: 10.4 us -> 13.9 us
    ppermute x7, waiting for transfers between devices: 15.7 us -> 36.7 us  [the longest x4 26 us: shifted(): got_value, got_span = unpack(lax.ppermute(packed, 'sz', pairs))]
    all_to_all x1 -> x0, blocking collectives: 20.1 us -> none  [body(): lax.all_to_all(jnp.stack([mix_q, att_q], axis=1), 'sy', 0, 3, tiled=True)]
    unnamed x30 -> x28, local copies, waits for them, and re-layouts: 14.7 us -> 10.6 us
    another operation x6 -> x7, local copies, waits for them, and re-layouts: 5.35 us -> 5.3 us
  transfers between devices with their start and end apart: 10 -> 10, of which waited for: 6 -> 9; matrix products, arithmetic and copies ran while one was open for 20% -> 19% of each run, Pallas kernels for 0% -> 0%
where the time goes in v8:
time: 239 us; the launch traced here: 237 us
  waiting for transfers between devices  107 us (45%)
  starting transfers between devices  51.7 us (22%)
  local copies, waits for them, and re-layouts  39.2 us (16%)
  matrix products  23.9 us (10%)
  other arithmetic  13.9 us (6%)
    all_to_all x1, waiting for transfers between devices, body(): back = lax.all_to_all(outgoing, seq_axes, 0, 0, tiled=True)  42 us
    ppermute x4, waiting for transfers between devices, shifted(): got_value, got_span = unpack(lax.ppermute(packed, 'sz', pairs))  26 us
    all_to_all x1, waiting for transfers between devices, body(): lax.all_to_all(send.reshape(n_experts, SLOTS, width), seq_axes, 0, 0, til...  24.5 us
    ppermute x4, starting transfers between devices, shifted(): got_value, got_span = unpack(lax.ppermute(packed, 'sz', pairs))  17.7 us
    ppermute x3, starting transfers between devices, body(): lax.ppermute(piece, 'sy', [(i, (i + by) % n_sy) for i in range(n_sy)])  12 us
    all_to_all x1, starting transfers between devices, body(): lax.all_to_all(send.reshape(n_experts, SLOTS, width), seq_axes, 0, 0, til...  11.5 us
    ppermute x3, waiting for transfers between devices, body(): lax.ppermute(piece, 'sy', [(i, (i + by) % n_sy) for i in range(n_sy)])  10.7 us
    unnamed x28, local copies, waits for them, and re-layouts  10.6 us
  transfers between devices with their start and end apart: 10, of which 9 were waited for; matrix products, arithmetic and copies ran while one was open for 19% of the time, Pallas kernels for 0%

profile of v8, /device:TPU:36, one launch (start us, length us, event | category | flops | bytes accessed | tf_op | source)
XLA Modules:
  0.0 237.2 jit_solution(18148159592181247112)
XLA Ops:
  3.0 3.1 %convolution_convert_fusion = bf16[512,2048]{1,0:T(8,128)(2,1)} fusion(bf16[512,128]{1,0:T(8,128)(2,1)S(1)} %fusion.52, bf16[128,2048]{1,0:T(8,128)(2,1)} %param.16), kind=kOutput, calls=%fused_computation.7 | convolution fusion | flops 269484032 | bytes 2752512 | tf_op jit(solution)/shard_map/dot_general | solution.py:63
  6.1 11.5 %all-to-all-start.1 = ((bf16[32,16,2048]{2,1,0:T(8,128)(2,1)}), bf16[32,16,2048]{2,1,0:T(8,128)(2,1)}, u32[]{:S(2)}, u32[]{:S(2)}) async-start(bf16[32,16,2048]{2,1,0:T(8,128)(2,1)} %bitcast.219), calls=%async_computation.1 | async-start | bytes 4194304 | tf_op jit(solution)/shard_map/all_to_all | solution.py:100
  28.6 5.5 %concatenate.21 = bf16[4,272,512]{1,2,0:T(8,128)(2,1)} concatenate(bf16[4,128,512]{1,2,0:T(8,128)(2,1)} %bitcast.221, bf16[4,128,512]{1,2,0:T(8,128)(2,1)} %bitcast.222, bf16[4,1,512]{1,2,0:T(8,128)(2,1)} %copy.170, bf16[4,1,512]{1,2,0:T(8,128)(2,1)} %copy.171, bf16[4,1,512]{1,2,0:T(8,128)(2,1)} %copy.172, bf16[4,3,512]{1,2,0:T(8,128)(2,1)} %broadcast_in_dim.15, ...), dimensions={1} | concatenate | bytes 2228224 | tf_op jit(solution)/shard_map/concatenate | solution.py:78
  34.1 2.5 %copy.173 = bf16[4,272,512]{2,1,0:T(8,128)(2,1)} copy(bf16[4,272,512]{1,2,0:T(8,128)(2,1)} %concatenate.21) | data formatting | bytes 2228224 | tf_op jit(solution)/shard_map/concatenate | solution.py:78
  36.7 6.2 %reshape_squeeze.3 = bf16[768,4,512]{2,1,0:T(4,128)(2,1)} reshape(bf16[1,768,2048]{2,1,0:T(8,128)(2,1)} %param.21) | data formatting | bytes 6291456 | tf_op jit(solution)/shard_map/reshape;squeeze | solution.py:105
  42.8 24.5 %all-to-all-done.1 = bf16[32,16,2048]{2,1,0:T(8,128)(2,1)} async-done(((bf16[32,16,2048]{2,1,0:T(8,128)(2,1)}), bf16[32,16,2048]{2,1,0:T(8,128)(2,1)}, u32[]{:S(2)}, u32[]{:S(2)}) %all-to-all-start.1) | async-done | bytes 2097184 | tf_op jit(solution)/shard_map/all_to_all | solution.py:100
  67.3 4.3 %all-to-all-start = ((bf16[4,272,512]{2,1,0:T(8,128)(2,1)}), bf16[4,272,512]{2,1,0:T(8,128)(2,1)}, u32[]{:S(2)}, u32[]{:S(2)}) async-start(bf16[4,272,512]{2,1,0:T(8,128)(2,1)} %copy.173), calls=%async_computation | async-start | bytes 2228224 | tf_op jit(solution)/shard_map/all_to_all | solution.py:88
  71.6 3.5 %fusion.4 = f32[512,768]{1,0:T(8,128)S(1)} fusion(bf16[512,2048]{1,0:T(8,128)(2,1)} %bitcast.14, bf16[1,2048,768]{2,1,0:T(8,128)(2,1)S(1)} %copy-done), kind=kOutput, calls=%fused_computation.4 | convolution fusion | flops 1610612736 | bytes 6815744 | tf_op jit(solution)/shard_map/dot_general | solution.py:12
  75.2 3.8 %multiply_convert_fusion = bf16[512,768]{1,0:T(8,128)(2,1)S(1)} fusion(f32[512,768]{1,0:T(8,128)S(1)} %fusion.4, bf16[512,2048]{1,0:T(8,128)(2,1)} %bitcast.14, bf16[1,2048,768]{2,1,0:T(8,128)(2,1)S(1)} %copy-done.10, f32[768]{0:T(1024)S(1)} %multiply_reduce_fusion.1), kind=kOutput, calls=%fused_computation.9 | convolution fusion | flops 1613758464 | bytes 7605248 | tf_op jit(solution)/shard_map/dot_general | solution.py:13
  79.0 3.2 %fusion.7 = bf16[8,64,4,512]{3,1,2,0:T(8,128)(2,1)} fusion(bf16[8,64,768,1]{2,1,3,0:T(8,128)(2,1)S(1)} %bitcast.242, bf16[768,4,512]{2,1,0:T(4,128)(2,1)S(1)} %copy-done.2), kind=kOutput, calls=%fused_computation.8 | convolution fusion | flops 1611661312 | bytes 6029312 | tf_op jit(solution)/shard_map/zrk,kjc->zjrc/dot_general | solution.py:102
  82.3 4.2 %all-to-all-done = bf16[4,272,512]{2,1,0:T(8,128)(2,1)} async-done(((bf16[4,272,512]{2,1,0:T(8,128)(2,1)}), bf16[4,272,512]{2,1,0:T(8,128)(2,1)}, u32[]{:S(2)}, u32[]{:S(2)}) %all-to-all-start) | async-done | bytes 1114144 | tf_op jit(solution)/shard_map/all_to_all | solution.py:88
  86.5 6.1 %all-to-all-start.2 = ((bf16[32,64,512]{2,1,0:T(8,128)(2,1)}), bf16[32,64,512]{2,1,0:T(8,128)(2,1)}, u32[]{:S(2)}, u32[]{:S(2)}) async-start(bf16[32,64,512]{2,1,0:T(8,128)(2,1)} %bitcast.224), calls=%async_computation.2 | async-start | bytes 4194304 | tf_op jit(solution)/shard_map/all_to_all | solution.py:109
  93.5 2.2 fusion.87
  95.8 2.1 copy.199
  99.6 42.0 %all-to-all-done.2 = bf16[32,64,512]{2,1,0:T(8,128)(2,1)} async-done(((bf16[32,64,512]{2,1,0:T(8,128)(2,1)}), bf16[32,64,512]{2,1,0:T(8,128)(2,1)}, u32[]{:S(2)}, u32[]{:S(2)}) %all-to-all-start.2) | async-done | bytes 2097184 | tf_op jit(solution)/shard_map/all_to_all | solution.py:109
  141.5 2.8 %copy.178 = bf16[32,64,512]{2,0,1:T(8,128)(2,1)S(1)} copy(bf16[32,64,512]{2,1,0:T(8,128)(2,1)} %all-to-all-done.2) | data formatting | bytes 4194304 | tf_op jit(solution)/shard_map/all_to_all | solution.py:109
  148.0 4.2 %collective-permute-start = (f32[520,128]{1,0:T(8,128)S(1)}, f32[520,128]{1,0:T(8,128)}, u32[]{:S(2)}, u32[]{:S(2)}) collective-permute-start(f32[520,128]{1,0:T(8,128)S(1)} %select_maximum_fusion.2), channel_id=1, source_target_pairs={{0,4},{4,8},{8,12},{12,16},{16,20},{20,24},{24,28},{1,5},{5,9},{9,... | collective-permute-start | bytes 798728 | tf_op jit(solution)/shard_map/ppermute | solution.py:168
  152.1 3.2 %collective-permute-start.1 = (f32[520,128]{1,0:T(8,128)S(1)}, f32[520,128]{1,0:T(8,128)}, u32[]{:S(2)}, u32[]{:S(2)}) collective-permute-start(f32[520,128]{1,0:T(8,128)S(1)} %select_maximum_fusion.2), channel_id=1, source_target_pairs={{0,8},{4,12},{8,16},{12,20},{16,24},{20,28},{1,9},{5,13},{9,17},{1... | collective-permute-start | bytes 798728 | tf_op jit(solution)/shard_map/ppermute | solution.py:168
  155.3 7.6 %collective-permute-done = f32[520,128]{1,0:T(8,128)} collective-permute-done((f32[520,128]{1,0:T(8,128)S(1)}, f32[520,128]{1,0:T(8,128)}, u32[]{:S(2)}, u32[]{:S(2)}) %collective-permute-start) | collective-permute-done | bytes 266272 | tf_op jit(solution)/shard_map/ppermute | solution.py:168
  162.9 5.8 %collective-permute-done.1 = f32[520,128]{1,0:T(8,128)} collective-permute-done((f32[520,128]{1,0:T(8,128)S(1)}, f32[520,128]{1,0:T(8,128)}, u32[]{:S(2)}, u32[]{:S(2)}) %collective-permute-start.1) | collective-permute-done | bytes 266272 | tf_op jit(solution)/shard_map/ppermute | solution.py:168
  171.2 5.5 %collective-permute-start.2 = (f32[520,128]{1,0:T(8,128)S(1)}, f32[520,128]{1,0:T(8,128)S(1)}, u32[]{:S(2)}, u32[]{:S(2)}) collective-permute-start(f32[520,128]{1,0:T(8,128)S(1)} %select_maximum_fusion.1), channel_id=1, source_target_pairs={{0,8},{4,12},{8,16},{12,20},{16,24},{20,28},{1,9},{5,13},{9,17},{1... | collective-permute-start | bytes 798728 | tf_op jit(solution)/shard_map/ppermute | solution.py:168
  176.7 6.8 %collective-permute-done.2 = f32[520,128]{1,0:T(8,128)S(1)} collective-permute-done((f32[520,128]{1,0:T(8,128)S(1)}, f32[520,128]{1,0:T(8,128)S(1)}, u32[]{:S(2)}, u32[]{:S(2)}) %collective-permute-start.2) | collective-permute-done | bytes 266272 | tf_op jit(solution)/shard_map/ppermute | solution.py:168
  185.8 4.9 %collective-permute-start.3 = (f32[520,128]{1,0:T(8,128)}, f32[520,128]{1,0:T(8,128)}, u32[]{:S(2)}, u32[]{:S(2)}) collective-permute-start(f32[520,128]{1,0:T(8,128)} %select_maximum_fusion), channel_id=1, source_target_pairs={{0,16},{4,20},{8,24},{12,28},{1,17},{5,21},{9,25},{13,29},{2,18},{... | collective-permute-start | bytes 798728 | tf_op jit(solution)/shard_map/ppermute | solution.py:168
  190.6 2.0 copy.198
  192.7 5.9 %collective-permute-done.3 = f32[520,128]{1,0:T(8,128)} collective-permute-done((f32[520,128]{1,0:T(8,128)}, f32[520,128]{1,0:T(8,128)}, u32[]{:S(2)}, u32[]{:S(2)}) %collective-permute-start.3) | collective-permute-done | bytes 266272 | tf_op jit(solution)/shard_map/ppermute | solution.py:168
  200.7 3.4 %fusion.16 = f32[4,128,4,128]{1,3,2,0:T(8,128)} fusion(bf16[4,128,4,128]{1,3,2,0:T(8,128)(2,1)} %bitcast.231, f32[1,4,128,128]{3,2,1,0:T(8,128)} %get-tuple-element.45, f32[1,4,128,128]{3,2,1,0:T(8,128)} %get-tuple-element.46, f32[1,4,128,128]{3,2,1,0:T(8,128)} %get-tuple-element.47, f32[4]{0:T(128)S(1)} %pad.21.clone, f32[4,128,128]{2,1,0:T(8,128)S(1)} %add_add_fusion, ...), kind=kOutput, calls=%fused_computation.27 | convolution fusion | flops 404226048 | bytes 2629712 | tf_op jit(solution)/shard_map/bthd,bhde->bthe/dot_general | solution.py:184
  204.1 3.6 %multiply_reduce_fusion = (f32[4,128,4]{1,2,0:T(4,128)S(1)}, f32[4,128,4,128]{1,3,2,0:T(8,128)}) fusion(f32[4,128,4,128]{1,3,2,0:T(8,128)} %fusion.16, bf16[4,128,4,128]{1,3,2,0:T(8,128)(2,1)} %bitcast.232, bf16[4,128,4,128]{1,3,2,0:T(8,128)(2,1)} %bitcast.225, f32[4,4,128]{2,1,0:T(4,128)S(1)} %reduce_window_sum.11, ...), kind=kOutput, calls=%fused_computation.39 | convolution fusion | flops 136312832 | bytes 3702784 | tf_op jit(solution)/shard_map/bhts,bshd->bthd/dot_general | solution.py:138
  207.7 2.1 multiply_convert_fusion.1
  213.2 2.8 %collective-permute-start.4 = (bf16[2,128,512]{2,1,0:T(8,128)(2,1)S(1)}, bf16[2,128,512]{2,1,0:T(8,128)(2,1)S(1)}, u32[]{:S(2)}, u32[]{:S(2)}) collective-permute-start(bf16[2,128,512]{2,1,0:T(8,128)(2,1)S(1)} %get-tuple-element.58), channel_id=1, source_target_pairs={{0,1},{1,2},{2,3},{3,0},{4,5},{5,6},{6,7},{7,4},{8,9},{9,10},{10,1... | collective-permute-start | bytes 786440 | tf_op jit(solution)/shard_map/ppermute | solution.py:197
  216.0 9.2 %collective-permute-start.5 = (bf16[2,128,512]{2,1,0:T(8,128)(2,1)S(1)}, bf16[2,128,512]{2,1,0:T(8,128)(2,1)S(1)}, u32[]{:S(2)}, u32[]{:S(2)}) collective-permute-start(bf16[2,128,512]{2,1,0:T(8,128)(2,1)S(1)} %get-tuple-element.59), channel_id=1, source_target_pairs={{0,2},{1,3},{2,0},{3,1},{4,6},{5,7},{6,4},{7,5},{8,10},{9,11},{10,... | collective-permute-start | bytes 786440 | tf_op jit(solution)/shard_map/ppermute | solution.py:197
  225.4 4.5 %collective-permute-done.4 = bf16[2,128,512]{2,1,0:T(8,128)(2,1)S(1)} collective-permute-done((bf16[2,128,512]{2,1,0:T(8,128)(2,1)S(1)}, bf16[2,128,512]{2,1,0:T(8,128)(2,1)S(1)}, u32[]{:S(2)}, u32[]{:S(2)}) %collective-permute-start.4) | collective-permute-done | bytes 262176 | tf_op jit(solution)/shard_map/ppermute | solution.py:197
  230.0 6.1 %collective-permute-done.5 = bf16[2,128,512]{2,1,0:T(8,128)(2,1)S(1)} collective-permute-done((bf16[2,128,512]{2,1,0:T(8,128)(2,1)S(1)}, bf16[2,128,512]{2,1,0:T(8,128)(2,1)S(1)}, u32[]{:S(2)}, u32[]{:S(2)}) %collective-permute-start.5) | collective-permute-done | bytes 262176 | tf_op jit(solution)/shard_map/ppermute | solution.py:197
  (104 shorter events, 31.1 us)
Async XLA Ops:
  0.6 71.0 %copy-start = (bf16[1,2048,768]{2,1,0:T(8,128)(2,1)S(1)}, bf16[1,2048,768]{2,1,0:T(8,128)(2,1)}, u32[]{:S(2)}) copy-start(bf16[1,2048,768]{2,1,0:T(8,128)(2,1)} %param.19) | copy-start | bytes 9437188
  6.1 11.6 %copy-start.6 = (bf16[2048,32]{0,1:T(8,128)(2,1)S(1)}, bf16[2048,32]{0,1:T(8,128)(2,1)}, u32[]{:S(2)}) copy-start(bf16[2048,32]{0,1:T(8,128)(2,1)} %param.18) | copy-start | bytes 393220
  6.1 12.9 %copy-start.7 = (s32[128,2]{0,1:T(2,128)S(1)}, s32[128,2]{0,1:T(2,128)}, u32[]{:S(2)}) copy-start(s32[128,2]{0,1:T(2,128)} %param.17) | copy-start | bytes 3076
  6.1 13.5 %copy-start.8 = (f32[16,128]{1,0:T(8,128)S(1)}, f32[16,128]{1,0:T(8,128)}, u32[]{:S(2)}) copy-start(f32[16,128]{1,0:T(8,128)} %param.25) | copy-start | bytes 24580
  6.1 61.3 %all-to-all-start.1 = ((bf16[32,16,2048]{2,1,0:T(8,128)(2,1)}), bf16[32,16,2048]{2,1,0:T(8,128)(2,1)}, u32[]{:S(2)}, u32[]{:S(2)}) async-start(bf16[32,16,2048]{2,1,0:T(8,128)(2,1)} %bitcast.219), calls=%async_computation.1 | async-start | bytes 4194304 | tf_op jit(solution)/shard_map/all_to_all | solution.py:100
  36.7 6.2 %copy-start.9 = (s32[1,768]{1,0:T(1,128)S(1)}, s32[1,768]{1,0:T(1,128)}, u32[]{:S(2)}) copy-start(s32[1,768]{1,0:T(1,128)} %param.22) | copy-start | bytes 9220
  67.3 19.1 %all-to-all-start = ((bf16[4,272,512]{2,1,0:T(8,128)(2,1)}), bf16[4,272,512]{2,1,0:T(8,128)(2,1)}, u32[]{:S(2)}, u32[]{:S(2)}) async-start(bf16[4,272,512]{2,1,0:T(8,128)(2,1)} %copy.173), calls=%async_computation | async-start | bytes 2228224 | tf_op jit(solution)/shard_map/all_to_all | solution.py:88
  71.6 3.5 %copy-start.10 = (bf16[1,2048,768]{2,1,0:T(8,128)(2,1)S(1)}, bf16[1,2048,768]{2,1,0:T(8,128)(2,1)}, u32[]{:S(2)}) copy-start(bf16[1,2048,768]{2,1,0:T(8,128)(2,1)} %param.20) | copy-start | bytes 9437188
  75.2 3.8 %copy-start.2 = (bf16[768,4,512]{2,1,0:T(4,128)(2,1)S(1)}, bf16[768,4,512]{2,1,0:T(4,128)(2,1)}, u32[]{:S(2)}) copy-start(bf16[768,4,512]{2,1,0:T(4,128)(2,1)} %reshape_squeeze.3) | copy-start | bytes 9437188
  86.5 55.1 %all-to-all-start.2 = ((bf16[32,64,512]{2,1,0:T(8,128)(2,1)}), bf16[32,64,512]{2,1,0:T(8,128)(2,1)}, u32[]{:S(2)}, u32[]{:S(2)}) async-start(bf16[32,64,512]{2,1,0:T(8,128)(2,1)} %bitcast.224), calls=%async_computation.2 | async-start | bytes 4194304 | tf_op jit(solution)/shard_map/all_to_all | solution.py:109
  144.8 1.0 copy-start.3
  145.4 2.2 copy-start.1
  148.0 14.9 %collective-permute-start = (f32[520,128]{1,0:T(8,128)S(1)}, f32[520,128]{1,0:T(8,128)}, u32[]{:S(2)}, u32[]{:S(2)}) collective-permute-start(f32[520,128]{1,0:T(8,128)S(1)} %select_maximum_fusion.2), channel_id=1, source_target_pairs={{0,4},{4,8},{8,12},{12,16},{16,20},{20,24},{24,28},{1,5},{5,9},{9,... | collective-permute-start | bytes 798728 | tf_op jit(solution)/shard_map/ppermute | solution.py:168
  152.1 16.5 %collective-permute-start.1 = (f32[520,128]{1,0:T(8,128)S(1)}, f32[520,128]{1,0:T(8,128)}, u32[]{:S(2)}, u32[]{:S(2)}) collective-permute-start(f32[520,128]{1,0:T(8,128)S(1)} %select_maximum_fusion.2), channel_id=1, source_target_pairs={{0,8},{4,12},{8,16},{12,20},{16,24},{20,28},{1,9},{5,13},{9,17},{1... | collective-permute-start | bytes 798728 | tf_op jit(solution)/shard_map/ppermute | solution.py:168
  171.2 12.3 %collective-permute-start.2 = (f32[520,128]{1,0:T(8,128)S(1)}, f32[520,128]{1,0:T(8,128)S(1)}, u32[]{:S(2)}, u32[]{:S(2)}) collective-permute-start(f32[520,128]{1,0:T(8,128)S(1)} %select_maximum_fusion.1), channel_id=1, source_target_pairs={{0,8},{4,12},{8,16},{12,20},{16,24},{20,28},{1,9},{5,13},{9,17},{1... | collective-permute-start | bytes 798728 | tf_op jit(solution)/shard_map/ppermute | solution.py:168
  185.8 12.8 %collective-permute-start.3 = (f32[520,128]{1,0:T(8,128)}, f32[520,128]{1,0:T(8,128)}, u32[]{:S(2)}, u32[]{:S(2)}) collective-permute-start(f32[520,128]{1,0:T(8,128)} %select_maximum_fusion), channel_id=1, source_target_pairs={{0,16},{4,20},{8,24},{12,28},{1,17},{5,21},{9,25},{13,29},{2,18},{... | collective-permute-start | bytes 798728 | tf_op jit(solution)/shard_map/ppermute | solution.py:168
  213.2 16.7 %collective-permute-start.4 = (bf16[2,128,512]{2,1,0:T(8,128)(2,1)S(1)}, bf16[2,128,512]{2,1,0:T(8,128)(2,1)S(1)}, u32[]{:S(2)}, u32[]{:S(2)}) collective-permute-start(bf16[2,128,512]{2,1,0:T(8,128)(2,1)S(1)} %get-tuple-element.58), channel_id=1, source_target_pairs={{0,1},{1,2},{2,3},{3,0},{4,5},{5,6},{6,7},{7,4},{8,9},{9,10},{10,1... | collective-permute-start | bytes 786440 | tf_op jit(solution)/shard_map/ppermute | solution.py:197
  216.0 20.1 %collective-permute-start.5 = (bf16[2,128,512]{2,1,0:T(8,128)(2,1)S(1)}, bf16[2,128,512]{2,1,0:T(8,128)(2,1)S(1)}, u32[]{:S(2)}, u32[]{:S(2)}) collective-permute-start(bf16[2,128,512]{2,1,0:T(8,128)(2,1)S(1)} %get-tuple-element.59), channel_id=1, source_target_pairs={{0,2},{1,3},{2,0},{3,1},{4,6},{5,7},{6,4},{7,5},{8,10},{9,11},{10,... | collective-permute-start | bytes 786440 | tf_op jit(solution)/shard_map/ppermute | solution.py:197
  225.3 10.8 %collective-permute-start.6 = (bf16[2,128,512]{2,1,0:T(8,128)(2,1)S(1)}, bf16[2,128,512]{2,1,0:T(8,128)(2,1)S(1)}, u32[]{:S(2)}, u32[]{:S(2)}) collective-permute-start(bf16[2,128,512]{2,1,0:T(8,128)(2,1)S(1)} %get-tuple-element.56), channel_id=1, source_target_pairs={{0,3},{1,0},{2,1},{3,2},{4,7},{5,4},{6,5},{7,6},{8,11},{9,8},{10,9... | collective-permute-start | bytes 786440 | tf_op jit(solution)/shard_map/ppermute | solution.py:197
  236.2 0.8 copy-start.4
  236.2 1.0 copy-start.5

commit v9 on v8

--- a/solution.py
+++ b/solution.py
@@ -154,6 +154,25 @@
         lead = lead * block_total[b]
     group_state, group_span = run, lead
 
+    growth = jnp.transpose(jnp.exp(cumulative), (0, 2, 1))[:, :, :, None]
+    q32 = group_q.astype(jnp.float32)
+    near = intra + growth * jnp.einsum(
+        "bthd,bhde->bthe", q32, jnp.stack(inside), precision=highest
+    )
+
+    yi = lax.axis_index("sy")
+
+    def send_home(quarters, total_width):
+        assembled = jnp.zeros((count, total_width), jnp.bfloat16)
+        for by in range(n_sy):
+            piece = lax.dynamic_index_in_dim(quarters, (yi + by) % n_sy, 0, False)
+            if by:
+                piece = lax.ppermute(piece, "sy", [(i, (i + by) % n_sy) for i in range(n_sy)])
+            assembled = lax.dynamic_update_slice(assembled, piece, (0, ((yi - by) % n_sy) * qw))
+        return assembled
+
+    expert_mix = send_home(mix_q, width)
+
     state_rows = quarter * hd
 
     def pack(value, span):
@@ -180,24 +199,11 @@
         reach *= 2
     before = window[0]
 
-    carried = jnp.stack(leads)[:, :, None, None] * before[None] + jnp.stack(inside)
-    inter = jnp.transpose(jnp.exp(cumulative), (0, 2, 1))[:, :, :, None] * jnp.einsum(
-        "bthd,bhde->bthe", group_q.astype(jnp.float32), carried, precision=highest
-    )
-    total_out = intra + inter
+    far = jnp.stack(leads)[:, :, None, None] * before[None]
+    total_out = near + growth * jnp.einsum("bthd,bhde->bthe", q32, far, precision=highest)
     normed = total_out * lax.rsqrt(jnp.mean(total_out * total_out, axis=3, keepdims=True) + 1e-06)
     att_q = normed.astype(jnp.bfloat16).reshape(n_sy, count, qw)
-    yi = lax.axis_index("sy")
-    outgoing_home = jnp.stack([mix_q, att_q], axis=1)
-    expert_mix = jnp.zeros((count, width), jnp.bfloat16)
-    attended = jnp.zeros((count, heads * hd), jnp.bfloat16)
-    for by in range(n_sy):
-        piece = lax.dynamic_index_in_dim(outgoing_home, (yi + by) % n_sy, 0, False)
-        if by:
-            piece = lax.ppermute(piece, "sy", [(i, (i + by) % n_sy) for i in range(n_sy)])
-        column = ((yi - by) % n_sy) * qw
-        expert_mix = lax.dynamic_update_slice(expert_mix, piece[0], (0, column))
-        attended = lax.dynamic_update_slice(attended, piece[1], (0, column))
+    attended = send_home(att_q, heads * hd)
     return (expert_mix, attended)
 
 

time: 239 us -> 231 us (0.967)
  waiting for transfers between devices: 107 us -> 87.3 us
  starting transfers between devices: 51.7 us -> 60.9 us
  local copies, waits for them, and re-layouts: 39.2 us -> 44.9 us
  other arithmetic: 13.9 us -> 9.44 us
    ppermute x4, waiting for transfers between devices: 26 us -> 13.2 us  [shifted(): got_value, got_span = unpack(lax.ppermute(packed, 'sz', pairs))]
    ppermute x3 -> x6, waiting for transfers between devices: 10.7 us -> 3.52 us  [send_home(): lax.ppermute(piece, 'sy', [(i, (i + by) % n_sy) for i in range(n_sy)])]
    ppermute x3 -> x6, starting transfers between devices: 12 us -> 17.8 us  [send_home(): lax.ppermute(piece, 'sy', [(i, (i + by) % n_sy) for i in range(n_sy)])]
    dynamic_slice x0 -> x5, local copies, waits for them, and re-layouts: none -> 4.93 us  [send_home(): piece = lax.dynamic_index_in_dim(quarters, (yi + by) % n_sy, 0, False)]
    ppermute x4, starting transfers between devices: 17.7 us -> 21.1 us  [shifted(): got_value, got_span = unpack(lax.ppermute(packed, 'sz', pairs))]
    another operation x7 -> x6, local copies, waits for them, and re-layouts: 5.3 us -> 3.26 us
    dot_general x1 -> x2, matrix products: 3.35 us -> 4.84 us  [the longest x1 2.76 us: body(): jnp.einsum('bthd,bhde->bthe', q32, far, precision=highest)]
    unnamed x28 -> x34, local copies, waits for them, and re-layouts: 10.6 us -> 10.4 us
  transfers between devices with their start and end apart: 10 -> 13, of which waited for: 9 -> 8; matrix products, arithmetic and copies ran while one was open for 19% -> 24% of each run, Pallas kernels for 0% -> 0%
where the time goes in v9:
time: 231 us; the launch traced here: 229 us
  waiting for transfers between devices  87.3 us (38%)
  starting transfers between devices  60.9 us (26%)
  local copies, waits for them, and re-layouts  44.9 us (19%)
  matrix products  25.7 us (11%)
  other arithmetic  9.44 us (4%)
    all_to_all x1, waiting for transfers between devices, body(): back = lax.all_to_all(outgoing, seq_axes, 0, 0, tiled=True)  42 us
    all_to_all x1, waiting for transfers between devices, body(): lax.all_to_all(send.reshape(n_experts, SLOTS, width), seq_axes, 0, 0, til...  24.5 us
    ppermute x4, starting transfers between devices, shifted(): got_value, got_span = unpack(lax.ppermute(packed, 'sz', pairs))  21.1 us
    ppermute x6, starting transfers between devices, send_home(): lax.ppermute(piece, 'sy', [(i, (i + by) % n_sy) for i in range(n_sy)])  17.8 us
    ppermute x4, waiting for transfers between devices, shifted(): got_value, got_span = unpack(lax.ppermute(packed, 'sz', pairs))  13.2 us
    all_to_all x1, starting transfers between devices, body(): lax.all_to_all(send.reshape(n_experts, SLOTS, width), seq_axes, 0, 0, til...  11.5 us
    unnamed x34, local copies, waits for them, and re-layouts  10.4 us
    concatenate x2, local copies, waits for them, and re-layouts, body(): jnp.concatenate([q_split, k_split, decay_parts.astype(jnp.bfloat16), info...  8.06 us
  transfers between devices with their start and end apart: 13, of which 8 were waited for; matrix products, arithmetic and copies ran while one was open for 24% of the time, Pallas kernels for 0%

profile of v9, /device:TPU:36, one launch (start us, length us, event | category | flops | bytes accessed | tf_op | source)
XLA Modules:
  0.0 229.5 jit_solution(9230848653075255938)
XLA Ops:
  3.0 3.1 %convolution_convert_fusion = bf16[512,2048]{1,0:T(8,128)(2,1)} fusion(bf16[512,128]{1,0:T(8,128)(2,1)S(1)} %fusion.55, bf16[128,2048]{1,0:T(8,128)(2,1)} %param.16), kind=kOutput, calls=%fused_computation.7 | convolution fusion | flops 269484032 | bytes 2752512 | tf_op jit(solution)/shard_map/dot_general | solution.py:63
  6.1 11.5 %all-to-all-start.1 = ((bf16[32,16,2048]{2,1,0:T(8,128)(2,1)}), bf16[32,16,2048]{2,1,0:T(8,128)(2,1)}, u32[]{:S(2)}, u32[]{:S(2)}) async-start(bf16[32,16,2048]{2,1,0:T(8,128)(2,1)} %bitcast.200), calls=%async_computation.1 | async-start | bytes 4194304 | tf_op jit(solution)/shard_map/all_to_all | solution.py:100
  22.7 2.0 copy.200
  28.6 5.6 %concatenate.21 = bf16[4,272,512]{1,2,0:T(8,128)(2,1)} concatenate(bf16[4,128,512]{1,2,0:T(8,128)(2,1)} %bitcast.207, bf16[4,128,512]{1,2,0:T(8,128)(2,1)} %bitcast.208, bf16[4,1,512]{1,2,0:T(8,128)(2,1)} %copy.204, bf16[4,1,512]{1,2,0:T(8,128)(2,1)} %copy.205, bf16[4,1,512]{1,2,0:T(8,128)(2,1)} %copy.206, bf16[4,3,512]{1,2,0:T(8,128)(2,1)} %broadcast_in_dim.15, ...), dimensions={1} | concatenate | bytes 2228224 | tf_op jit(solution)/shard_map/concatenate | solution.py:78
  34.2 2.5 %copy.207 = bf16[4,272,512]{2,1,0:T(8,128)(2,1)} copy(bf16[4,272,512]{1,2,0:T(8,128)(2,1)} %concatenate.21) | data formatting | bytes 2228224 | tf_op jit(solution)/shard_map/concatenate | solution.py:78
  36.7 6.2 %reshape_squeeze.3 = bf16[768,4,512]{2,1,0:T(4,128)(2,1)} reshape(bf16[1,768,2048]{2,1,0:T(8,128)(2,1)} %param.21) | data formatting | bytes 6291456 | tf_op jit(solution)/shard_map/reshape;squeeze | solution.py:105
  42.9 24.5 %all-to-all-done.1 = bf16[32,16,2048]{2,1,0:T(8,128)(2,1)} async-done(((bf16[32,16,2048]{2,1,0:T(8,128)(2,1)}), bf16[32,16,2048]{2,1,0:T(8,128)(2,1)}, u32[]{:S(2)}, u32[]{:S(2)}) %all-to-all-start.1) | async-done | bytes 2097184 | tf_op jit(solution)/shard_map/all_to_all | solution.py:100
  67.3 4.3 %all-to-all-start = ((bf16[4,272,512]{2,1,0:T(8,128)(2,1)}), bf16[4,272,512]{2,1,0:T(8,128)(2,1)}, u32[]{:S(2)}, u32[]{:S(2)}) async-start(bf16[4,272,512]{2,1,0:T(8,128)(2,1)} %copy.207), calls=%async_computation | async-start | bytes 2228224 | tf_op jit(solution)/shard_map/all_to_all | solution.py:88
  71.6 3.5 %fusion.4 = f32[512,768]{1,0:T(8,128)S(1)} fusion(bf16[512,2048]{1,0:T(8,128)(2,1)} %bitcast.14, bf16[1,2048,768]{2,1,0:T(8,128)(2,1)S(1)} %copy-done), kind=kOutput, calls=%fused_computation.4 | convolution fusion | flops 1610612736 | bytes 6815744 | tf_op jit(solution)/shard_map/dot_general | solution.py:12
  75.2 3.8 %multiply_convert_fusion = bf16[512,768]{1,0:T(8,128)(2,1)S(1)} fusion(f32[512,768]{1,0:T(8,128)S(1)} %fusion.4, bf16[512,2048]{1,0:T(8,128)(2,1)} %bitcast.14, bf16[1,2048,768]{2,1,0:T(8,128)(2,1)S(1)} %copy-done.13, f32[768]{0:T(1024)S(1)} %multiply_reduce_fusion.1), kind=kOutput, calls=%fused_computation.9 | convolution fusion | flops 1613758464 | bytes 7605248 | tf_op jit(solution)/shard_map/dot_general | solution.py:13
  79.0 3.2 %fusion.7 = bf16[8,64,4,512]{3,1,2,0:T(8,128)(2,1)} fusion(bf16[8,64,768,1]{2,1,3,0:T(8,128)(2,1)S(1)} %bitcast.226, bf16[768,4,512]{2,1,0:T(4,128)(2,1)S(1)} %copy-done.4), kind=kOutput, calls=%fused_computation.8 | convolution fusion | flops 1611661312 | bytes 6029312 | tf_op jit(solution)/shard_map/zrk,kjc->zjrc/dot_general | solution.py:102
  82.3 4.2 %all-to-all-done = bf16[4,272,512]{2,1,0:T(8,128)(2,1)} async-done(((bf16[4,272,512]{2,1,0:T(8,128)(2,1)}), bf16[4,272,512]{2,1,0:T(8,128)(2,1)}, u32[]{:S(2)}, u32[]{:S(2)}) %all-to-all-start) | async-done | bytes 1114144 | tf_op jit(solution)/shard_map/all_to_all | solution.py:88
  86.4 6.2 %all-to-all-start.2 = ((bf16[32,64,512]{2,1,0:T(8,128)(2,1)}), bf16[32,64,512]{2,1,0:T(8,128)(2,1)}, u32[]{:S(2)}, u32[]{:S(2)}) async-start(bf16[32,64,512]{2,1,0:T(8,128)(2,1)} %bitcast.209), calls=%async_computation.2 | async-start | bytes 4194304 | tf_op jit(solution)/shard_map/all_to_all | solution.py:109
  93.5 2.2 fusion.75
  95.7 2.0 copy.238
  99.6 42.0 %all-to-all-done.2 = bf16[32,64,512]{2,1,0:T(8,128)(2,1)} async-done(((bf16[32,64,512]{2,1,0:T(8,128)(2,1)}), bf16[32,64,512]{2,1,0:T(8,128)(2,1)}, u32[]{:S(2)}, u32[]{:S(2)}) %all-to-all-start.2) | async-done | bytes 2097184 | tf_op jit(solution)/shard_map/all_to_all | solution.py:109
  141.5 2.8 %copy.212 = bf16[32,64,512]{2,0,1:T(8,128)(2,1)S(1)} copy(bf16[32,64,512]{2,1,0:T(8,128)(2,1)} %all-to-all-done.2) | data formatting | bytes 4194304 | tf_op jit(solution)/shard_map/all_to_all | solution.py:109
  148.6 4.1 %collective-permute-start.3 = (f32[520,128]{1,0:T(8,128)}, f32[520,128]{1,0:T(8,128)}, u32[]{:S(2)}, u32[]{:S(2)}) collective-permute-start(f32[520,128]{1,0:T(8,128)} %select_maximum_fusion.2), channel_id=1, source_target_pairs={{0,4},{4,8},{8,12},{12,16},{16,20},{20,24},{24,28},{1,5},{5,9},{9,... | collective-permute-start | bytes 798728 | tf_op jit(solution)/shard_map/ppermute | solution.py:187
  152.7 3.2 %collective-permute-start.4 = (f32[520,128]{1,0:T(8,128)}, f32[520,128]{1,0:T(8,128)}, u32[]{:S(2)}, u32[]{:S(2)}) collective-permute-start(f32[520,128]{1,0:T(8,128)} %select_maximum_fusion.2), channel_id=1, source_target_pairs={{0,8},{4,12},{8,16},{12,20},{16,24},{20,28},{1,9},{5,13},{9,17},{1... | collective-permute-start | bytes 798728 | tf_op jit(solution)/shard_map/ppermute | solution.py:187
  156.2 2.0 copy.237
  161.4 2.5 %collective-permute-start.2 = (bf16[128,512]{1,0:T(8,128)(2,1)S(1)}, bf16[128,512]{1,0:T(8,128)(2,1)S(1)}, u32[]{:S(2)}, u32[]{:S(2)}) collective-permute-start(bf16[128,512]{1,0:T(8,128)(2,1)S(1)} %get-tuple-element.64), channel_id=1, source_target_pairs={{0,3},{1,0},{2,1},{3,2},{4,7},{5,4},{6,5},{7,6},{8,11},{9,8},{10,9... | collective-permute-start | bytes 393224 | tf_op jit(solution)/shard_map/ppermute | solution.py:170
  163.9 5.7 %collective-permute-done.4 = f32[520,128]{1,0:T(8,128)} collective-permute-done((f32[520,128]{1,0:T(8,128)}, f32[520,128]{1,0:T(8,128)}, u32[]{:S(2)}, u32[]{:S(2)}) %collective-permute-start.4) | collective-permute-done | bytes 266272 | tf_op jit(solution)/shard_map/ppermute | solution.py:187
  171.6 5.4 %collective-permute-start.5 = (f32[520,128]{1,0:T(8,128)S(1)}, f32[520,128]{1,0:T(8,128)S(1)}, u32[]{:S(2)}, u32[]{:S(2)}) collective-permute-start(f32[520,128]{1,0:T(8,128)S(1)} %select_maximum_fusion.1), channel_id=1, source_target_pairs={{0,8},{4,12},{8,16},{12,20},{16,24},{20,28},{1,9},{5,13},{9,17},{1... | collective-permute-start | bytes 798728 | tf_op jit(solution)/shard_map/ppermute | solution.py:187
  177.9 2.1 fusion.18
  180.0 3.7 %collective-permute-done.5 = f32[520,128]{1,0:T(8,128)S(1)} collective-permute-done((f32[520,128]{1,0:T(8,128)S(1)}, f32[520,128]{1,0:T(8,128)S(1)}, u32[]{:S(2)}, u32[]{:S(2)}) %collective-permute-start.5) | collective-permute-done | bytes 266272 | tf_op jit(solution)/shard_map/ppermute | solution.py:187
  184.7 8.4 %collective-permute-start.6 = (f32[520,128]{1,0:T(8,128)S(1)}, f32[520,128]{1,0:T(8,128)S(1)}, u32[]{:S(2)}, u32[]{:S(2)}) collective-permute-start(f32[520,128]{1,0:T(8,128)S(1)} %select_maximum_fusion), channel_id=1, source_target_pairs={{0,16},{4,20},{8,24},{12,28},{1,17},{5,21},{9,25},{13,29},{2,18},{... | collective-permute-start | bytes 798728 | tf_op jit(solution)/shard_map/ppermute | solution.py:187
  193.2 3.8 %collective-permute-done.6 = f32[520,128]{1,0:T(8,128)S(1)} collective-permute-done((f32[520,128]{1,0:T(8,128)S(1)}, f32[520,128]{1,0:T(8,128)S(1)}, u32[]{:S(2)}, u32[]{:S(2)}) %collective-permute-start.6) | collective-permute-done | bytes 266272 | tf_op jit(solution)/shard_map/ppermute | solution.py:187
  198.0 2.8 %fusion.17 = f32[4,128,4,128]{1,3,2,0:T(8,128)} fusion(bf16[4,128,4,128]{1,3,2,0:T(8,128)(2,1)} %bitcast.201, f32[4,128,128]{1,2,0:T(8,128)} %copy.223, f32[4,4]{1,0:T(4,128)S(1)} %pad_maximum_fusion, f32[4,128,4]{1,2,0:T(4,128)S(1)} %get-tuple-element.81), kind=kOutput, calls=%fused_computation.20 | convolution fusion | flops 403177472 | bytes 1843264 | tf_op jit(solution)/shard_map/bthd,bhde->bthe/dot_general | solution.py:203
  200.7 3.9 %multiply_reduce_fusion = (f32[4,128,4]{1,2,0:T(4,128)S(1)}, f32[4,128,4,128]{1,3,2,0:T(8,128)}) fusion(f32[4,128,4,128]{1,3,2,0:T(8,128)} %fusion.17, f32[4,128,4,128]{1,3,2,0:T(8,128)} %fusion.18, bf16[4,128,4,128]{1,3,2,0:T(8,128)(2,1)} %bitcast.202, bf16[4,128,4,128]{1,3,2,0:T(8,128)(2,1)} %bitcast.204, f32[4,4,128]{2,1,0:T(4,128)S(1)} %reduce_window_sum.11, ...), kind=kOutput, calls=%fused_computation.34 | convolution fusion | flops 136574976 | bytes 4751360 | tf_op jit(solution)/shard_map/bhts,bshd->bthd/dot_general | solution.py:138
  209.4 3.0 %collective-permute-start.7 = (bf16[128,512]{1,0:T(8,128)(2,1)}, bf16[128,512]{1,0:T(8,128)(2,1)}, u32[]{:S(2)}, u32[]{:S(2)}) collective-permute-start(bf16[128,512]{1,0:T(8,128)(2,1)} %bitcast.216), channel_id=1, source_target_pairs={{0,1},{1,2},{2,3},{3,0},{4,5},{5,6},{6,7},{7,4},{8,9},{9,10},{10,1... | collective-permute-start | bytes 393224 | tf_op jit(solution)/shard_map/ppermute | solution.py:170
  213.1 9.6 %collective-permute-start.8 = (bf16[128,512]{1,0:T(8,128)(2,1)}, bf16[128,512]{1,0:T(8,128)(2,1)S(1)}, u32[]{:S(2)}, u32[]{:S(2)}) collective-permute-start(bf16[128,512]{1,0:T(8,128)(2,1)} %bitcast.215), channel_id=1, source_target_pairs={{0,2},{1,3},{2,0},{3,1},{4,6},{5,7},{6,4},{7,5},{8,10},{9,11},{10,... | collective-permute-start | bytes 393224 | tf_op jit(solution)/shard_map/ppermute | solution.py:170
  225.2 2.9 %collective-permute-done.8 = bf16[128,512]{1,0:T(8,128)(2,1)S(1)} collective-permute-done((bf16[128,512]{1,0:T(8,128)(2,1)}, bf16[128,512]{1,0:T(8,128)(2,1)S(1)}, u32[]{:S(2)}, u32[]{:S(2)}) %collective-permute-start.8) | collective-permute-done | bytes 131104 | tf_op jit(solution)/shard_map/ppermute | solution.py:170
  (125 shorter events, 35.4 us)
Async XLA Ops:
  0.6 71.0 %copy-start = (bf16[1,2048,768]{2,1,0:T(8,128)(2,1)S(1)}, bf16[1,2048,768]{2,1,0:T(8,128)(2,1)}, u32[]{:S(2)}) copy-start(bf16[1,2048,768]{2,1,0:T(8,128)(2,1)} %param.19) | copy-start | bytes 9437188
  6.1 11.6 %copy-start.9 = (bf16[2048,32]{0,1:T(8,128)(2,1)S(1)}, bf16[2048,32]{0,1:T(8,128)(2,1)}, u32[]{:S(2)}) copy-start(bf16[2048,32]{0,1:T(8,128)(2,1)} %param.18) | copy-start | bytes 393220
  6.1 12.9 %copy-start.10 = (s32[128,2]{0,1:T(2,128)S(1)}, s32[128,2]{0,1:T(2,128)}, u32[]{:S(2)}) copy-start(s32[128,2]{0,1:T(2,128)} %param.17) | copy-start | bytes 3076
  6.1 13.5 %copy-start.11 = (f32[16,128]{1,0:T(8,128)S(1)}, f32[16,128]{1,0:T(8,128)}, u32[]{:S(2)}) copy-start(f32[16,128]{1,0:T(8,128)} %param.25) | copy-start | bytes 24580
  6.1 61.3 %all-to-all-start.1 = ((bf16[32,16,2048]{2,1,0:T(8,128)(2,1)}), bf16[32,16,2048]{2,1,0:T(8,128)(2,1)}, u32[]{:S(2)}, u32[]{:S(2)}) async-start(bf16[32,16,2048]{2,1,0:T(8,128)(2,1)} %bitcast.200), calls=%async_computation.1 | async-start | bytes 4194304 | tf_op jit(solution)/shard_map/all_to_all | solution.py:100
  36.7 6.2 %copy-start.12 = (s32[1,768]{1,0:T(1,128)S(1)}, s32[1,768]{1,0:T(1,128)}, u32[]{:S(2)}) copy-start(s32[1,768]{1,0:T(1,128)} %param.22) | copy-start | bytes 9220
  67.3 19.1 %all-to-all-start = ((bf16[4,272,512]{2,1,0:T(8,128)(2,1)}), bf16[4,272,512]{2,1,0:T(8,128)(2,1)}, u32[]{:S(2)}, u32[]{:S(2)}) async-start(bf16[4,272,512]{2,1,0:T(8,128)(2,1)} %copy.207), calls=%async_computation | async-start | bytes 2228224 | tf_op jit(solution)/shard_map/all_to_all | solution.py:88
  71.6 3.5 %copy-start.13 = (bf16[1,2048,768]{2,1,0:T(8,128)(2,1)S(1)}, bf16[1,2048,768]{2,1,0:T(8,128)(2,1)}, u32[]{:S(2)}) copy-start(bf16[1,2048,768]{2,1,0:T(8,128)(2,1)} %param.20) | copy-start | bytes 9437188
  75.2 3.8 %copy-start.4 = (bf16[768,4,512]{2,1,0:T(4,128)(2,1)S(1)}, bf16[768,4,512]{2,1,0:T(4,128)(2,1)}, u32[]{:S(2)}) copy-start(bf16[768,4,512]{2,1,0:T(4,128)(2,1)} %reshape_squeeze.3) | copy-start | bytes 9437188
  86.4 55.1 %all-to-all-start.2 = ((bf16[32,64,512]{2,1,0:T(8,128)(2,1)}), bf16[32,64,512]{2,1,0:T(8,128)(2,1)}, u32[]{:S(2)}, u32[]{:S(2)}) async-start(bf16[32,64,512]{2,1,0:T(8,128)(2,1)} %bitcast.209), calls=%async_computation.2 | async-start | bytes 4194304 | tf_op jit(solution)/shard_map/all_to_all | solution.py:109
  144.8 1.0 copy-start.3
  145.4 2.1 copy-start.1
  148.6 15.3 %collective-permute-start.3 = (f32[520,128]{1,0:T(8,128)}, f32[520,128]{1,0:T(8,128)}, u32[]{:S(2)}, u32[]{:S(2)}) collective-permute-start(f32[520,128]{1,0:T(8,128)} %select_maximum_fusion.2), channel_id=1, source_target_pairs={{0,4},{4,8},{8,12},{12,16},{16,20},{20,24},{24,28},{1,5},{5,9},{9,... | collective-permute-start | bytes 798728 | tf_op jit(solution)/shard_map/ppermute | solution.py:187
  152.7 16.9 %collective-permute-start.4 = (f32[520,128]{1,0:T(8,128)}, f32[520,128]{1,0:T(8,128)}, u32[]{:S(2)}, u32[]{:S(2)}) collective-permute-start(f32[520,128]{1,0:T(8,128)} %select_maximum_fusion.2), channel_id=1, source_target_pairs={{0,8},{4,12},{8,16},{12,20},{16,24},{20,28},{1,9},{5,13},{9,17},{1... | collective-permute-start | bytes 798728 | tf_op jit(solution)/shard_map/ppermute | solution.py:187
  158.2 19.7 %copy-start.2 = (bf16[4,128,512]{1,2,0:T(8,128)(2,1)S(1)}, bf16[4,128,512]{1,2,0:T(8,128)(2,1)}, u32[]{:S(2)}) copy-start(bf16[4,128,512]{1,2,0:T(8,128)(2,1)} %copy.237) | copy-start | bytes 1572868
  158.2 19.7 %copy-start.5 = (f32[1,4,128,128]{3,2,1,0:T(8,128)S(1)}, f32[1,4,128,128]{3,2,1,0:T(8,128)}, u32[]{:S(2)}) copy-start(f32[1,4,128,128]{3,2,1,0:T(8,128)} %get-tuple-element.41) | copy-start | bytes 786436
  158.2 19.7 %copy-start.6 = (f32[1,4,128,128]{3,2,1,0:T(8,128)S(1)}, f32[1,4,128,128]{3,2,1,0:T(8,128)}, u32[]{:S(2)}) copy-start(f32[1,4,128,128]{3,2,1,0:T(8,128)} %get-tuple-element.42) | copy-start | bytes 786436
  159.4 33.7 %collective-permute-start = (bf16[128,512]{1,0:T(8,128)(2,1)S(1)}, bf16[128,512]{1,0:T(8,128)(2,1)S(1)}, u32[]{:S(2)}, u32[]{:S(2)}) collective-permute-start(bf16[128,512]{1,0:T(8,128)(2,1)S(1)} %get-tuple-element.66), channel_id=1, source_target_pairs={{0,1},{1,2},{2,3},{3,0},{4,5},{5,6},{6,7},{7,4},{8,9},{9,10},{10,1... | collective-permute-start | bytes 393224 | tf_op jit(solution)/shard_map/ppermute | solution.py:170
  160.1 33.0 %collective-permute-start.1 = (bf16[128,512]{1,0:T(8,128)(2,1)S(1)}, bf16[128,512]{1,0:T(8,128)(2,1)S(1)}, u32[]{:S(2)}, u32[]{:S(2)}) collective-permute-start(bf16[128,512]{1,0:T(8,128)(2,1)S(1)} %get-tuple-element.65), channel_id=1, source_target_pairs={{0,2},{1,3},{2,0},{3,1},{4,6},{5,7},{6,4},{7,5},{8,10},{9,11},{10,... | collective-permute-start | bytes 393224 | tf_op jit(solution)/shard_map/ppermute | solution.py:170
  161.4 31.7 %collective-permute-start.2 = (bf16[128,512]{1,0:T(8,128)(2,1)S(1)}, bf16[128,512]{1,0:T(8,128)(2,1)S(1)}, u32[]{:S(2)}, u32[]{:S(2)}) collective-permute-start(bf16[128,512]{1,0:T(8,128)(2,1)S(1)} %get-tuple-element.64), channel_id=1, source_target_pairs={{0,3},{1,0},{2,1},{3,2},{4,7},{5,4},{6,5},{7,6},{8,11},{9,8},{10,9... | collective-permute-start | bytes 393224 | tf_op jit(solution)/shard_map/ppermute | solution.py:170
  171.6 12.2 %collective-permute-start.5 = (f32[520,128]{1,0:T(8,128)S(1)}, f32[520,128]{1,0:T(8,128)S(1)}, u32[]{:S(2)}, u32[]{:S(2)}) collective-permute-start(f32[520,128]{1,0:T(8,128)S(1)} %select_maximum_fusion.1), channel_id=1, source_target_pairs={{0,8},{4,12},{8,16},{12,20},{16,24},{20,28},{1,9},{5,13},{9,17},{1... | collective-permute-start | bytes 798728 | tf_op jit(solution)/shard_map/ppermute | solution.py:187
  184.7 12.3 %collective-permute-start.6 = (f32[520,128]{1,0:T(8,128)S(1)}, f32[520,128]{1,0:T(8,128)S(1)}, u32[]{:S(2)}, u32[]{:S(2)}) collective-permute-start(f32[520,128]{1,0:T(8,128)S(1)} %select_maximum_fusion), channel_id=1, source_target_pairs={{0,16},{4,20},{8,24},{12,28},{1,17},{5,21},{9,25},{13,29},{2,18},{... | collective-permute-start | bytes 798728 | tf_op jit(solution)/shard_map/ppermute | solution.py:187
  193.1 3.8 %copy-start.8 = (bf16[128,2048]{1,0:T(8,128)(2,1)}, bf16[128,2048]{1,0:T(8,128)(2,1)S(1)}, u32[]{:S(2)}) copy-start(bf16[128,2048]{1,0:T(8,128)(2,1)S(1)} %constant_dynamic-update-slice_fusion.2) | copy-start | bytes 1572868
  209.4 14.9 %collective-permute-start.7 = (bf16[128,512]{1,0:T(8,128)(2,1)}, bf16[128,512]{1,0:T(8,128)(2,1)}, u32[]{:S(2)}, u32[]{:S(2)}) collective-permute-start(bf16[128,512]{1,0:T(8,128)(2,1)} %bitcast.216), channel_id=1, source_target_pairs={{0,1},{1,2},{2,3},{3,0},{4,5},{5,6},{6,7},{7,4},{8,9},{9,10},{10,1... | collective-permute-start | bytes 393224 | tf_op jit(solution)/shard_map/ppermute | solution.py:170
  213.1 15.0 %collective-permute-start.8 = (bf16[128,512]{1,0:T(8,128)(2,1)}, bf16[128,512]{1,0:T(8,128)(2,1)S(1)}, u32[]{:S(2)}, u32[]{:S(2)}) collective-permute-start(bf16[128,512]{1,0:T(8,128)(2,1)} %bitcast.215), channel_id=1, source_target_pairs={{0,2},{1,3},{2,0},{3,1},{4,6},{5,7},{6,4},{7,5},{8,10},{9,11},{10,... | collective-permute-start | bytes 393224 | tf_op jit(solution)/shard_map/ppermute | solution.py:170
  223.5 5.2 %collective-permute-start.9 = (bf16[128,512]{1,0:T(8,128)(2,1)}, bf16[128,512]{1,0:T(8,128)(2,1)S(1)}, u32[]{:S(2)}, u32[]{:S(2)}) collective-permute-start(bf16[128,512]{1,0:T(8,128)(2,1)} %bitcast.214), channel_id=1, source_target_pairs={{0,3},{1,0},{2,1},{3,2},{4,7},{5,4},{6,5},{7,6},{8,11},{9,8},{10,9... | collective-permute-start | bytes 393224 | tf_op jit(solution)/shard_map/ppermute | solution.py:170
  228.7 0.8 copy-start.7

commit v10 on v9

--- a/solution.py
+++ b/solution.py
@@ -85,7 +85,15 @@
         ],
         axis=1,
     )
-    got = lax.all_to_all(packed, "sy", 0, 0, tiled=True)
+    yi = lax.axis_index("sy")
+    got = jnp.zeros_like(packed)
+    for by in range(n_sy):
+        piece = lax.dynamic_index_in_dim(packed, (yi + by) % n_sy, 0, True)
+        if by:
+            piece = lax.ppermute(piece, "sy", [(i, (i + by) % n_sy) for i in range(n_sy)])
+        got = lax.dynamic_update_slice(got, piece, ((yi - by) % n_sy, 0, 0))
+    recv = lax.all_to_all(send.reshape(n_experts, SLOTS, width), seq_axes, 0, 0, tiled=True)
+    spikes = expert_spikes(recv.reshape(n_rows, width), w_gate[0], w_up[0], spike_level[0])
     group_q = got[:, :count].reshape(n_sy, count, quarter, hd)
     group_k = got[:, count : 2 * count].reshape(n_sy, count, quarter, hd)
     parts = got[:, 2 * count : 2 * count + 3].astype(jnp.float32)
@@ -97,8 +105,6 @@
     row_first = (got_info[:, 0] * SLOTS + got_info[:, 1]).astype(jnp.int32)
     row_second = (got_info[:, 2] * SLOTS + got_info[:, 3]).astype(jnp.int32)
 
-    recv = lax.all_to_all(send.reshape(n_experts, SLOTS, width), seq_axes, 0, 0, tiled=True)
-    spikes = expert_spikes(recv.reshape(n_rows, width), w_gate[0], w_up[0], spike_level[0])
     outgoing = jnp.einsum(
         "zrk,kjc->zjrc",
         spikes.reshape(n_sz, n_sy * SLOTS, -1),
@@ -160,7 +166,6 @@
         "bthd,bhde->bthe", q32, jnp.stack(inside), precision=highest
     )
 
-    yi = lax.axis_index("sy")
 
     def send_home(quarters, total_width):
         assembled = jnp.zeros((count, total_width), jnp.bfloat16)

time: 231 us -> 226 us (0.978)
  waiting for transfers between devices: 87.3 us -> 68.2 us
  starting transfers between devices: 60.9 us -> 70.1 us
  other arithmetic: 9.44 us -> 11.9 us
    all_to_all x1, waiting for transfers between devices: 42 us -> 0.01 us  [body(): back = lax.all_to_all(outgoing, seq_axes, 0, 0, tiled=True)]
    ppermute x0 -> x3, waiting for transfers between devices: none -> 32.1 us  [body(): lax.ppermute(piece, 'sy', [(i, (i + by) % n_sy) for i in range(n_sy)])]
    ppermute x4, starting transfers between devices: 21.1 us -> 34.7 us  [shifted(): got_value, got_span = unpack(lax.ppermute(packed, 'sz', pairs))]
    ppermute x6, starting transfers between devices: 17.8 us -> 11.5 us  [send_home(): lax.ppermute(piece, 'sy', [(i, (i + by) % n_sy) for i in range(n_sy)])]
    ppermute x0 -> x3, starting transfers between devices: none -> 5.74 us  [body(): lax.ppermute(piece, 'sy', [(i, (i + by) % n_sy) for i in range(n_sy)])]
    dynamic_update_slice x0 -> x3, local copies, waits for them, and re-layouts: none -> 4.46 us  [body(): got = lax.dynamic_update_slice(got, piece, ((yi - by) % n_sy, 0, 0))]
    all_to_all x1 -> x0, starting transfers between devices: 4.28 us -> none  [body(): got = lax.all_to_all(packed, 'sy', 0, 0, tiled=True)]
    all_to_all x1 -> x0, waiting for transfers between devices: 4.18 us -> none  [body(): got = lax.all_to_all(packed, 'sy', 0, 0, tiled=True)]
  transfers between devices with their start and end apart: 13 -> 15, of which waited for: 8 -> 9; matrix products, arithmetic and copies ran while one was open for 24% -> 26% of each run, Pallas kernels for 0% -> 0%
where the time goes in v10:
time: 226 us; the launch traced here: 224 us
  starting transfers between devices  70.1 us (31%)
  waiting for transfers between devices  68.2 us (30%)
  local copies, waits for them, and re-layouts  47.1 us (21%)
  matrix products  25.6 us (11%)
  other arithmetic  11.9 us (5%)
    ppermute x4, starting transfers between devices, shifted(): got_value, got_span = unpack(lax.ppermute(packed, 'sz', pairs))  34.7 us
    ppermute x3, waiting for transfers between devices, body(): lax.ppermute(piece, 'sy', [(i, (i + by) % n_sy) for i in range(n_sy)])  32.1 us
    all_to_all x1, waiting for transfers between devices, body(): lax.all_to_all(send.reshape(n_experts, SLOTS, width), seq_axes, 0, 0, til...  22.2 us
    all_to_all x1, starting transfers between devices, body(): lax.all_to_all(send.reshape(n_experts, SLOTS, width), seq_axes, 0, 0, til...  11.5 us
    ppermute x6, starting transfers between devices, send_home(): lax.ppermute(piece, 'sy', [(i, (i + by) % n_sy) for i in range(n_sy)])  11.5 us
    ppermute x4, waiting for transfers between devices, shifted(): got_value, got_span = unpack(lax.ppermute(packed, 'sz', pairs))  9.68 us
    unnamed x33, local copies, waits for them, and re-layouts  6.96 us
    all_to_all x1, starting transfers between devices, body(): back = lax.all_to_all(outgoing, seq_axes, 0, 0, tiled=True)  6.51 us
  transfers between devices with their start and end apart: 15, of which 9 were waited for; matrix products, arithmetic and copies ran while one was open for 26% of the time, Pallas kernels for 0%

profile of v10, /device:TPU:36, one launch (start us, length us, event | category | flops | bytes accessed | tf_op | source)
XLA Modules:
  0.0 224.3 jit_solution(4189588498900935471)
XLA Ops:
  3.0 3.1 %convolution_convert_fusion = bf16[512,2048]{1,0:T(8,128)(2,1)} fusion(bf16[512,128]{1,0:T(8,128)(2,1)S(1)} %fusion.56, bf16[128,2048]{1,0:T(8,128)(2,1)} %param.16), kind=kOutput, calls=%fused_computation.7 | convolution fusion | flops 269484032 | bytes 2752512 | tf_op jit(solution)/shard_map/dot_general | solution.py:63
  6.1 11.5 %all-to-all-start = ((bf16[32,16,2048]{2,1,0:T(8,128)(2,1)}), bf16[32,16,2048]{2,1,0:T(8,128)(2,1)}, u32[]{:S(2)}, u32[]{:S(2)}) async-start(bf16[32,16,2048]{2,1,0:T(8,128)(2,1)} %bitcast.197), calls=%async_computation | async-start | bytes 4194304 | tf_op jit(solution)/shard_map/all_to_all | solution.py:95
  22.8 2.0 copy.140
  24.8 2.0 copy.141
  28.7 5.6 %concatenate.21 = bf16[4,272,512]{1,2,0:T(8,128)(2,1)} concatenate(bf16[4,128,512]{1,2,0:T(8,128)(2,1)} %bitcast.203, bf16[4,128,512]{1,2,0:T(8,128)(2,1)} %bitcast.204, bf16[4,1,512]{1,2,0:T(8,128)(2,1)} %copy.144, bf16[4,1,512]{1,2,0:T(8,128)(2,1)} %copy.145, bf16[4,1,512]{1,2,0:T(8,128)(2,1)} %copy.146, bf16[4,3,512]{1,2,0:T(8,128)(2,1)} %broadcast_in_dim.18, ...), dimensions={1} | concatenate | bytes 2228224 | tf_op jit(solution)/shard_map/concatenate | solution.py:78
  38.9 6.2 %reshape_squeeze.3 = bf16[768,4,512]{2,1,0:T(4,128)(2,1)} reshape(bf16[1,768,2048]{2,1,0:T(8,128)(2,1)} %param.21) | data formatting | bytes 6291456 | tf_op jit(solution)/shard_map/reshape;squeeze | solution.py:111
  45.1 22.2 %all-to-all-done = bf16[32,16,2048]{2,1,0:T(8,128)(2,1)} async-done(((bf16[32,16,2048]{2,1,0:T(8,128)(2,1)}), bf16[32,16,2048]{2,1,0:T(8,128)(2,1)}, u32[]{:S(2)}, u32[]{:S(2)}) %all-to-all-start) | async-done | bytes 2097184 | tf_op jit(solution)/shard_map/all_to_all | solution.py:95
  67.3 3.5 %fusion.4 = f32[512,768]{1,0:T(8,128)S(1)} fusion(bf16[512,2048]{1,0:T(8,128)(2,1)} %bitcast.15, bf16[1,2048,768]{2,1,0:T(8,128)(2,1)S(1)} %copy-done), kind=kOutput, calls=%fused_computation.4 | convolution fusion | flops 1610612736 | bytes 6815744 | tf_op jit(solution)/shard_map/dot_general | solution.py:12
  70.9 3.8 %multiply_convert_fusion = bf16[512,768]{1,0:T(8,128)(2,1)S(1)} fusion(f32[512,768]{1,0:T(8,128)S(1)} %fusion.4, bf16[512,2048]{1,0:T(8,128)(2,1)} %bitcast.15, bf16[1,2048,768]{2,1,0:T(8,128)(2,1)S(1)} %copy-done.14, f32[768]{0:T(1024)S(1)} %multiply_reduce_fusion.1), kind=kOutput, calls=%fused_computation.9 | convolution fusion | flops 1613758464 | bytes 7605248 | tf_op jit(solution)/shard_map/dot_general | solution.py:13
  74.7 3.2 %fusion.7 = bf16[8,64,4,512]{3,1,2,0:T(8,128)(2,1)} fusion(bf16[8,64,768,1]{2,1,3,0:T(8,128)(2,1)S(1)} %bitcast.222, bf16[768,4,512]{2,1,0:T(4,128)(2,1)S(1)} %copy-done.5), kind=kOutput, calls=%fused_computation.8 | convolution fusion | flops 1611661312 | bytes 6029312 | tf_op jit(solution)/shard_map/zrk,kjc->zjrc/dot_general | solution.py:108
  77.9 6.5 %all-to-all-start.1 = ((bf16[32,64,512]{2,1,0:T(8,128)(2,1)}), bf16[32,64,512]{2,1,0:T(8,128)(2,1)}, u32[]{:S(2)}, u32[]{:S(2)}) async-start(bf16[32,64,512]{2,1,0:T(8,128)(2,1)} %bitcast.206), calls=%async_computation.1 | async-start | bytes 4194304 | tf_op jit(solution)/shard_map/all_to_all | solution.py:115
  84.4 3.1 %collective-permute-start.1 = (bf16[1,272,512]{1,2,0:T(8,128)(2,1)}, bf16[1,272,512]{1,2,0:T(8,128)(2,1)}, u32[]{:S(2)}, u32[]{:S(2)}) collective-permute-start(bf16[1,272,512]{1,2,0:T(8,128)(2,1)} %get-tuple-element.57), channel_id=1, source_target_pairs={{0,2},{1,3},{2,0},{3,1},{4,6},{5,7},{6,4},{7,5},{8,10},{9,11},{10,... | collective-permute-start | bytes 835592 | tf_op jit(solution)/shard_map/ppermute | solution.py:93
  89.5 20.0 %collective-permute-done.1 = bf16[1,272,512]{1,2,0:T(8,128)(2,1)} collective-permute-done((bf16[1,272,512]{1,2,0:T(8,128)(2,1)}, bf16[1,272,512]{1,2,0:T(8,128)(2,1)}, u32[]{:S(2)}, u32[]{:S(2)}) %collective-permute-start.1) | collective-permute-done | bytes 278560 | tf_op jit(solution)/shard_map/ppermute | solution.py:93
  111.2 12.2 %collective-permute-done.2 = bf16[1,272,512]{1,2,0:T(8,128)(2,1)} collective-permute-done((bf16[1,272,512]{1,2,0:T(8,128)(2,1)}, bf16[1,272,512]{1,2,0:T(8,128)(2,1)}, u32[]{:S(2)}, u32[]{:S(2)}) %collective-permute-start.2) | collective-permute-done | bytes 278560 | tf_op jit(solution)/shard_map/ppermute | solution.py:93
  123.4 1.8 constant_dynamic-update-slice_fusion.5
  125.3 2.3 %slice_convert_fusion = (f32[4,3,512]{1,2,0:T(8,128)S(1)}, bf16[4,3,512]{1,2,0:T(8,128)(2,1)}) fusion(bf16[4,272,512]{1,2,0:T(8,128)(2,1)} %constant_dynamic-update-slice_fusion.5), kind=kLoop, calls=%fused_computation.50 | loop fusion | flops 6144 | bytes 61440 | tf_op jit(solution)/shard_map/convert_element_type | solution.py:99
  131.7 2.3 %fusion.76 = (bf16[4,128,512]{1,2,0:T(8,128)(2,1)}, bf16[4,128,512]{1,2,0:T(8,128)(2,1)}) fusion(bf16[4,272,512]{1,2,0:T(8,128)(2,1)} %constant_dynamic-update-slice_fusion.5), kind=kLoop, calls=%fused_computation.201 | loop fusion | bytes 2097152 | tf_op jit(solution)/shard_map/slice | solution.py:98
  134.0 2.8 %copy.152 = bf16[32,64,512]{2,0,1:T(8,128)(2,1)S(1)} copy(bf16[32,64,512]{2,1,0:T(8,128)(2,1)} %all-to-all-done.1) | data formatting | bytes 4194304 | tf_op jit(solution)/shard_map/all_to_all | solution.py:115
  141.0 3.2 %collective-permute-start.6 = (f32[520,128]{1,0:T(8,128)}, f32[520,128]{1,0:T(8,128)}, u32[]{:S(2)}, u32[]{:S(2)}) collective-permute-start(f32[520,128]{1,0:T(8,128)} %select_maximum_fusion.2), channel_id=1, source_target_pairs={{0,4},{4,8},{8,12},{12,16},{16,20},{20,24},{24,28},{1,5},{5,9},{9,... | collective-permute-start | bytes 798728 | tf_op jit(solution)/shard_map/ppermute | solution.py:192
  144.2 6.3 %collective-permute-start.7 = (f32[520,128]{1,0:T(8,128)}, f32[520,128]{1,0:T(8,128)}, u32[]{:S(2)}, u32[]{:S(2)}) collective-permute-start(f32[520,128]{1,0:T(8,128)} %select_maximum_fusion.2), channel_id=1, source_target_pairs={{0,8},{4,12},{8,16},{12,20},{16,24},{20,28},{1,9},{5,13},{9,17},{1... | collective-permute-start | bytes 798728 | tf_op jit(solution)/shard_map/ppermute | solution.py:192
  152.9 3.1 %collective-permute-start.4 = (bf16[128,512]{1,0:T(8,128)(2,1)S(1)}, bf16[128,512]{1,0:T(8,128)(2,1)S(1)}, u32[]{:S(2)}, u32[]{:S(2)}) collective-permute-start(bf16[128,512]{1,0:T(8,128)(2,1)S(1)} %get-tuple-element.69), channel_id=1, source_target_pairs={{0,2},{1,3},{2,0},{3,1},{4,6},{5,7},{6,4},{7,5},{8,10},{9,11},{10,... | collective-permute-start | bytes 393224 | tf_op jit(solution)/shard_map/ppermute | solution.py:175
  157.2 2.1 collective-permute-done.7
  161.3 9.0 %collective-permute-start.8 = (f32[520,128]{1,0:T(8,128)S(1)}, f32[520,128]{1,0:T(8,128)S(1)}, u32[]{:S(2)}, u32[]{:S(2)}) collective-permute-start(f32[520,128]{1,0:T(8,128)S(1)} %select_maximum_fusion.1), channel_id=1, source_target_pairs={{0,8},{4,12},{8,16},{12,20},{16,24},{20,28},{1,9},{5,13},{9,17},{1... | collective-permute-start | bytes 798728 | tf_op jit(solution)/shard_map/ppermute | solution.py:192
  171.3 2.1 fusion.18
  173.4 3.8 %collective-permute-done.8 = f32[520,128]{1,0:T(8,128)S(1)} collective-permute-done((f32[520,128]{1,0:T(8,128)S(1)}, f32[520,128]{1,0:T(8,128)S(1)}, u32[]{:S(2)}, u32[]{:S(2)}) %collective-permute-start.8) | collective-permute-done | bytes 266272 | tf_op jit(solution)/shard_map/ppermute | solution.py:192
  178.1 16.3 %collective-permute-start.9 = (f32[520,128]{1,0:T(8,128)S(1)}, f32[520,128]{1,0:T(8,128)S(1)}, u32[]{:S(2)}, u32[]{:S(2)}) collective-permute-start(f32[520,128]{1,0:T(8,128)S(1)} %select_maximum_fusion), channel_id=1, source_target_pairs={{0,16},{4,20},{8,24},{12,28},{1,17},{5,21},{9,25},{13,29},{2,18},{... | collective-permute-start | bytes 798728 | tf_op jit(solution)/shard_map/ppermute | solution.py:192
  194.5 3.8 %collective-permute-done.9 = f32[520,128]{1,0:T(8,128)S(1)} collective-permute-done((f32[520,128]{1,0:T(8,128)S(1)}, f32[520,128]{1,0:T(8,128)S(1)}, u32[]{:S(2)}, u32[]{:S(2)}) %collective-permute-start.9) | collective-permute-done | bytes 266272 | tf_op jit(solution)/shard_map/ppermute | solution.py:192
  199.3 2.8 %fusion.17 = f32[4,128,4,128]{1,3,2,0:T(8,128)} fusion(bf16[4,128,4,128]{1,3,2,0:T(8,128)(2,1)} %bitcast.198, f32[4,128,128]{1,2,0:T(8,128)} %copy.161, f32[4,4]{1,0:T(4,128)S(1)} %pad_maximum_fusion, f32[4,128,4]{1,2,0:T(4,128)S(1)} %get-tuple-element.85), kind=kOutput, calls=%fused_computation.20 | convolution fusion | flops 403177472 | bytes 1843264 | tf_op jit(solution)/shard_map/bthd,bhde->bthe/dot_general | solution.py:208
  202.1 3.9 %multiply_reduce_fusion = (f32[4,128,4]{1,2,0:T(4,128)S(1)}, f32[4,128,4,128]{1,3,2,0:T(8,128)}) fusion(f32[4,128,4,128]{1,3,2,0:T(8,128)} %fusion.17, f32[4,128,4,128]{1,3,2,0:T(8,128)} %fusion.18, bf16[4,128,4,128]{1,3,2,0:T(8,128)(2,1)} %bitcast.199, bf16[4,128,4,128]{1,3,2,0:T(8,128)(2,1)} %bitcast.201, f32[4,4,128]{2,1,0:T(4,128)S(1)} %reduce_window_sum.11, ...), kind=kOutput, calls=%fused_computation.37 | convolution fusion | flops 136574976 | bytes 4751360 | tf_op jit(solution)/shard_map/bhts,bshd->bthd/dot_general | solution.py:144
  213.1 4.4 %collective-permute-start.11 = (bf16[128,512]{1,0:T(8,128)(2,1)}, bf16[128,512]{1,0:T(8,128)(2,1)S(1)}, u32[]{:S(2)}, u32[]{:S(2)}) collective-permute-start(bf16[128,512]{1,0:T(8,128)(2,1)} %bitcast.212), channel_id=1, source_target_pairs={{0,2},{1,3},{2,0},{3,1},{4,6},{5,7},{6,4},{7,5},{8,10},{9,11},{10,... | collective-permute-start | bytes 393224 | tf_op jit(solution)/shard_map/ppermute | solution.py:175
  219.5 1.8 collective-permute-done.11
  221.3 2.1 collective-permute-done.12
  (134 shorter events, 44.2 us)
Async XLA Ops:
  0.6 66.7 %copy-start = (bf16[1,2048,768]{2,1,0:T(8,128)(2,1)S(1)}, bf16[1,2048,768]{2,1,0:T(8,128)(2,1)}, u32[]{:S(2)}) copy-start(bf16[1,2048,768]{2,1,0:T(8,128)(2,1)} %param.19) | copy-start | bytes 9437188
  6.1 11.6 %copy-start.10 = (bf16[2048,32]{0,1:T(8,128)(2,1)S(1)}, bf16[2048,32]{0,1:T(8,128)(2,1)}, u32[]{:S(2)}) copy-start(bf16[2048,32]{0,1:T(8,128)(2,1)} %param.18) | copy-start | bytes 393220
  6.1 12.9 %copy-start.11 = (s32[128,2]{0,1:T(2,128)S(1)}, s32[128,2]{0,1:T(2,128)}, u32[]{:S(2)}) copy-start(s32[128,2]{0,1:T(2,128)} %param.17) | copy-start | bytes 3076
  6.1 13.5 %copy-start.12 = (f32[16,128]{1,0:T(8,128)S(1)}, f32[16,128]{1,0:T(8,128)}, u32[]{:S(2)}) copy-start(f32[16,128]{1,0:T(8,128)} %param.25) | copy-start | bytes 24580
  6.1 61.3 %all-to-all-start = ((bf16[32,16,2048]{2,1,0:T(8,128)(2,1)}), bf16[32,16,2048]{2,1,0:T(8,128)(2,1)}, u32[]{:S(2)}, u32[]{:S(2)}) async-start(bf16[32,16,2048]{2,1,0:T(8,128)(2,1)} %bitcast.197), calls=%async_computation | async-start | bytes 4194304 | tf_op jit(solution)/shard_map/all_to_all | solution.py:95
  34.2 2.0 copy-start.3
  37.4 7.7 %copy-start.13 = (s32[1,768]{1,0:T(1,128)S(1)}, s32[1,768]{1,0:T(1,128)}, u32[]{:S(2)}) copy-start(s32[1,768]{1,0:T(1,128)} %param.22) | copy-start | bytes 9220
  37.4 51.3 %collective-permute-start = (bf16[1,272,512]{1,2,0:T(8,128)(2,1)}, bf16[1,272,512]{1,2,0:T(8,128)(2,1)S(1)}, u32[]{:S(2)}, u32[]{:S(2)}) collective-permute-start(bf16[1,272,512]{1,2,0:T(8,128)(2,1)} %get-tuple-element.58), channel_id=1, source_target_pairs={{0,1},{1,2},{2,3},{3,0},{4,5},{5,6},{6,7},{7,4},{8,9},{9,10},{10,1... | collective-permute-start | bytes 835592 | tf_op jit(solution)/shard_map/ppermute | solution.py:93
  67.3 3.5 %copy-start.14 = (bf16[1,2048,768]{2,1,0:T(8,128)(2,1)S(1)}, bf16[1,2048,768]{2,1,0:T(8,128)(2,1)}, u32[]{:S(2)}) copy-start(bf16[1,2048,768]{2,1,0:T(8,128)(2,1)} %param.20) | copy-start | bytes 9437188
  70.9 3.8 %copy-start.5 = (bf16[768,4,512]{2,1,0:T(4,128)(2,1)S(1)}, bf16[768,4,512]{2,1,0:T(4,128)(2,1)}, u32[]{:S(2)}) copy-start(bf16[768,4,512]{2,1,0:T(4,128)(2,1)} %reshape_squeeze.3) | copy-start | bytes 9437188
  77.9 56.0 %all-to-all-start.1 = ((bf16[32,64,512]{2,1,0:T(8,128)(2,1)}), bf16[32,64,512]{2,1,0:T(8,128)(2,1)}, u32[]{:S(2)}, u32[]{:S(2)}) async-start(bf16[32,64,512]{2,1,0:T(8,128)(2,1)} %bitcast.206), calls=%async_computation.1 | async-start | bytes 4194304 | tf_op jit(solution)/shard_map/all_to_all | solution.py:115
  84.4 25.0 %collective-permute-start.1 = (bf16[1,272,512]{1,2,0:T(8,128)(2,1)}, bf16[1,272,512]{1,2,0:T(8,128)(2,1)}, u32[]{:S(2)}, u32[]{:S(2)}) collective-permute-start(bf16[1,272,512]{1,2,0:T(8,128)(2,1)} %get-tuple-element.57), channel_id=1, source_target_pairs={{0,2},{1,3},{2,0},{3,1},{4,6},{5,7},{6,4},{7,5},{8,10},{9,11},{10,... | collective-permute-start | bytes 835592 | tf_op jit(solution)/shard_map/ppermute | solution.py:93
  87.5 35.9 %collective-permute-start.2 = (bf16[1,272,512]{1,2,0:T(8,128)(2,1)}, bf16[1,272,512]{1,2,0:T(8,128)(2,1)}, u32[]{:S(2)}, u32[]{:S(2)}) collective-permute-start(bf16[1,272,512]{1,2,0:T(8,128)(2,1)} %get-tuple-element.56), channel_id=1, source_target_pairs={{0,3},{1,0},{2,1},{3,2},{4,7},{5,4},{6,5},{7,6},{8,11},{9,8},{10,9... | collective-permute-start | bytes 835592 | tf_op jit(solution)/shard_map/ppermute | solution.py:93
  137.2 1.0 copy-start.4
  137.8 2.1 copy-start.1
  141.0 16.3 %collective-permute-start.6 = (f32[520,128]{1,0:T(8,128)}, f32[520,128]{1,0:T(8,128)}, u32[]{:S(2)}, u32[]{:S(2)}) collective-permute-start(f32[520,128]{1,0:T(8,128)} %select_maximum_fusion.2), channel_id=1, source_target_pairs={{0,4},{4,8},{8,12},{12,16},{16,20},{20,24},{24,28},{1,5},{5,9},{9,... | collective-permute-start | bytes 798728 | tf_op jit(solution)/shard_map/ppermute | solution.py:192
  144.2 15.2 %collective-permute-start.7 = (f32[520,128]{1,0:T(8,128)}, f32[520,128]{1,0:T(8,128)}, u32[]{:S(2)}, u32[]{:S(2)}) collective-permute-start(f32[520,128]{1,0:T(8,128)} %select_maximum_fusion.2), channel_id=1, source_target_pairs={{0,8},{4,12},{8,16},{12,20},{16,24},{20,28},{1,9},{5,13},{9,17},{1... | collective-permute-start | bytes 798728 | tf_op jit(solution)/shard_map/ppermute | solution.py:192
  150.6 20.7 %copy-start.2 = (bf16[4,128,512]{1,2,0:T(8,128)(2,1)S(1)}, bf16[4,128,512]{1,2,0:T(8,128)(2,1)}, u32[]{:S(2)}) copy-start(bf16[4,128,512]{1,2,0:T(8,128)(2,1)} %get-tuple-element.53) | copy-start | bytes 1572868
  150.6 20.7 %copy-start.6 = (f32[1,4,128,128]{3,2,1,0:T(8,128)S(1)}, f32[1,4,128,128]{3,2,1,0:T(8,128)}, u32[]{:S(2)}) copy-start(f32[1,4,128,128]{3,2,1,0:T(8,128)} %get-tuple-element.41) | copy-start | bytes 786436
  150.6 20.7 %copy-start.7 = (f32[1,4,128,128]{3,2,1,0:T(8,128)S(1)}, f32[1,4,128,128]{3,2,1,0:T(8,128)}, u32[]{:S(2)}) copy-start(f32[1,4,128,128]{3,2,1,0:T(8,128)} %get-tuple-element.42) | copy-start | bytes 786436
  151.8 42.6 %collective-permute-start.3 = (bf16[128,512]{1,0:T(8,128)(2,1)S(1)}, bf16[128,512]{1,0:T(8,128)(2,1)S(1)}, u32[]{:S(2)}, u32[]{:S(2)}) collective-permute-start(bf16[128,512]{1,0:T(8,128)(2,1)S(1)} %get-tuple-element.70), channel_id=1, source_target_pairs={{0,1},{1,2},{2,3},{3,0},{4,5},{5,6},{6,7},{7,4},{8,9},{9,10},{10,1... | collective-permute-start | bytes 393224 | tf_op jit(solution)/shard_map/ppermute | solution.py:175
  152.9 41.6 %collective-permute-start.4 = (bf16[128,512]{1,0:T(8,128)(2,1)S(1)}, bf16[128,512]{1,0:T(8,128)(2,1)S(1)}, u32[]{:S(2)}, u32[]{:S(2)}) collective-permute-start(bf16[128,512]{1,0:T(8,128)(2,1)S(1)} %get-tuple-element.69), channel_id=1, source_target_pairs={{0,2},{1,3},{2,0},{3,1},{4,6},{5,7},{6,4},{7,5},{8,10},{9,11},{10,... | collective-permute-start | bytes 393224 | tf_op jit(solution)/shard_map/ppermute | solution.py:175
  156.0 38.5 %collective-permute-start.5 = (bf16[128,512]{1,0:T(8,128)(2,1)S(1)}, bf16[128,512]{1,0:T(8,128)(2,1)S(1)}, u32[]{:S(2)}, u32[]{:S(2)}) collective-permute-start(bf16[128,512]{1,0:T(8,128)(2,1)S(1)} %get-tuple-element.68), channel_id=1, source_target_pairs={{0,3},{1,0},{2,1},{3,2},{4,7},{5,4},{6,5},{7,6},{8,11},{9,8},{10,9... | collective-permute-start | bytes 393224 | tf_op jit(solution)/shard_map/ppermute | solution.py:175
  161.3 15.8 %collective-permute-start.8 = (f32[520,128]{1,0:T(8,128)S(1)}, f32[520,128]{1,0:T(8,128)S(1)}, u32[]{:S(2)}, u32[]{:S(2)}) collective-permute-start(f32[520,128]{1,0:T(8,128)S(1)} %select_maximum_fusion.1), channel_id=1, source_target_pairs={{0,8},{4,12},{8,16},{12,20},{16,24},{20,28},{1,9},{5,13},{9,17},{1... | collective-permute-start | bytes 798728 | tf_op jit(solution)/shard_map/ppermute | solution.py:192
  178.1 20.2 %collective-permute-start.9 = (f32[520,128]{1,0:T(8,128)S(1)}, f32[520,128]{1,0:T(8,128)S(1)}, u32[]{:S(2)}, u32[]{:S(2)}) collective-permute-start(f32[520,128]{1,0:T(8,128)S(1)} %select_maximum_fusion), channel_id=1, source_target_pairs={{0,16},{4,20},{8,24},{12,28},{1,17},{5,21},{9,25},{13,29},{2,18},{... | collective-permute-start | bytes 798728 | tf_op jit(solution)/shard_map/ppermute | solution.py:192
  194.5 3.8 %copy-start.9 = (bf16[128,2048]{1,0:T(8,128)(2,1)}, bf16[128,2048]{1,0:T(8,128)(2,1)S(1)}, u32[]{:S(2)}) copy-start(bf16[128,2048]{1,0:T(8,128)(2,1)S(1)} %constant_dynamic-update-slice_fusion.2) | copy-start | bytes 1572868
  210.7 7.9 %collective-permute-start.10 = (bf16[128,512]{1,0:T(8,128)(2,1)}, bf16[128,512]{1,0:T(8,128)(2,1)}, u32[]{:S(2)}, u32[]{:S(2)}) collective-permute-start(bf16[128,512]{1,0:T(8,128)(2,1)} %bitcast.213), channel_id=1, source_target_pairs={{0,1},{1,2},{2,3},{3,0},{4,5},{5,6},{6,7},{7,4},{8,9},{9,10},{10,1... | collective-permute-start | bytes 393224 | tf_op jit(solution)/shard_map/ppermute | solution.py:175
  213.1 8.2 %collective-permute-start.11 = (bf16[128,512]{1,0:T(8,128)(2,1)}, bf16[128,512]{1,0:T(8,128)(2,1)S(1)}, u32[]{:S(2)}, u32[]{:S(2)}) collective-permute-start(bf16[128,512]{1,0:T(8,128)(2,1)} %bitcast.212), channel_id=1, source_target_pairs={{0,2},{1,3},{2,0},{3,1},{4,6},{5,7},{6,4},{7,5},{8,10},{9,11},{10,... | collective-permute-start | bytes 393224 | tf_op jit(solution)/shard_map/ppermute | solution.py:175
  218.3 5.2 %collective-permute-start.12 = (bf16[128,512]{1,0:T(8,128)(2,1)}, bf16[128,512]{1,0:T(8,128)(2,1)S(1)}, u32[]{:S(2)}, u32[]{:S(2)}) collective-permute-start(bf16[128,512]{1,0:T(8,128)(2,1)} %bitcast.211), channel_id=1, source_target_pairs={{0,3},{1,0},{2,1},{3,2},{4,7},{5,4},{6,5},{7,6},{8,11},{9,8},{10,9... | collective-permute-start | bytes 393224 | tf_op jit(solution)/shard_map/ppermute | solution.py:175
  223.5 0.8 copy-start.8

commit v11 on v10

--- a/solution.py
+++ b/solution.py
@@ -187,8 +187,8 @@
     def unpack(packed):
         return packed[:state_rows].reshape(quarter, hd, hd), packed[state_rows, :quarter]
 
-    def shifted(packed, by):
-        pairs = [(i, i + by) for i in range(n_sz - by)]
+    def shifted(packed, by, first=0):
+        pairs = [(i, i + by) for i in range(first, n_sz - by)]
         got_value, got_span = unpack(lax.ppermute(packed, "sz", pairs))
         return got_value, jnp.where(zi >= by, got_span, 1.0)
 
@@ -200,7 +200,7 @@
     window = join(shifted(own, 2), shifted(own, 1))
     reach = 2
     while reach < n_sz:
-        window = join(shifted(pack(*window), reach), window)
+        window = join(shifted(pack(*window), reach, first=1), window)
         reach *= 2
     before = window[0]
 

time: 226 us -> 223 us (0.987)
  waiting for transfers between devices: 68.2 us -> 65.2 us
    ppermute x4, waiting for transfers between devices: 9.68 us -> 6.66 us  [shifted(): got_value, got_span = unpack(lax.ppermute(packed, 'sz', pairs))]
where the time goes in v11:
time: 223 us; the launch traced here: 221 us
  starting transfers between devices  70.2 us (31%)
  waiting for transfers between devices  65.2 us (29%)
  local copies, waits for them, and re-layouts  47.1 us (21%)
  matrix products  25.6 us (11%)
  other arithmetic  11.9 us (5%)
    ppermute x4, starting transfers between devices, shifted(): got_value, got_span = unpack(lax.ppermute(packed, 'sz', pairs))  34.7 us
    ppermute x3, waiting for transfers between devices, body(): lax.ppermute(piece, 'sy', [(i, (i + by) % n_sy) for i in range(n_sy)])  32.1 us
    all_to_all x1, waiting for transfers between devices, body(): lax.all_to_all(send.reshape(n_experts, SLOTS, width), seq_axes, 0, 0, til...  22.2 us
    ppermute x6, starting transfers between devices, send_home(): lax.ppermute(piece, 'sy', [(i, (i + by) % n_sy) for i in range(n_sy)])  11.7 us
    all_to_all x1, starting transfers between devices, body(): lax.all_to_all(send.reshape(n_experts, SLOTS, width), seq_axes, 0, 0, til...  11.5 us
    unnamed x33, local copies, waits for them, and re-layouts  6.96 us
    ppermute x4, waiting for transfers between devices, shifted(): got_value, got_span = unpack(lax.ppermute(packed, 'sz', pairs))  6.66 us
    all_to_all x1, starting transfers between devices, body(): back = lax.all_to_all(outgoing, seq_axes, 0, 0, tiled=True)  6.51 us
  transfers between devices with their start and end apart: 15, of which 9 were waited for; matrix products, arithmetic and copies ran while one was open for 26% of the time, Pallas kernels for 0%

profile of v11, /device:TPU:36, one launch (start us, length us, event | category | flops | bytes accessed | tf_op | source)
XLA Modules:
  0.0 221.4 jit_solution(6933667035152162452)
XLA Ops:
  3.0 3.1 %convolution_convert_fusion = bf16[512,2048]{1,0:T(8,128)(2,1)} fusion(bf16[512,128]{1,0:T(8,128)(2,1)S(1)} %fusion.56, bf16[128,2048]{1,0:T(8,128)(2,1)} %param.16), kind=kOutput, calls=%fused_computation.7 | convolution fusion | flops 269484032 | bytes 2752512 | tf_op jit(solution)/shard_map/dot_general | solution.py:63
  6.1 11.5 %all-to-all-start = ((bf16[32,16,2048]{2,1,0:T(8,128)(2,1)}), bf16[32,16,2048]{2,1,0:T(8,128)(2,1)}, u32[]{:S(2)}, u32[]{:S(2)}) async-start(bf16[32,16,2048]{2,1,0:T(8,128)(2,1)} %bitcast.197), calls=%async_computation | async-start | bytes 4194304 | tf_op jit(solution)/shard_map/all_to_all | solution.py:95
  22.8 2.0 copy.140
  24.8 2.0 copy.141
  28.7 5.6 %concatenate.21 = bf16[4,272,512]{1,2,0:T(8,128)(2,1)} concatenate(bf16[4,128,512]{1,2,0:T(8,128)(2,1)} %bitcast.203, bf16[4,128,512]{1,2,0:T(8,128)(2,1)} %bitcast.204, bf16[4,1,512]{1,2,0:T(8,128)(2,1)} %copy.144, bf16[4,1,512]{1,2,0:T(8,128)(2,1)} %copy.145, bf16[4,1,512]{1,2,0:T(8,128)(2,1)} %copy.146, bf16[4,3,512]{1,2,0:T(8,128)(2,1)} %broadcast_in_dim.18, ...), dimensions={1} | concatenate | bytes 2228224 | tf_op jit(solution)/shard_map/concatenate | solution.py:78
  38.9 6.2 %reshape_squeeze.3 = bf16[768,4,512]{2,1,0:T(4,128)(2,1)} reshape(bf16[1,768,2048]{2,1,0:T(8,128)(2,1)} %param.21) | data formatting | bytes 6291456 | tf_op jit(solution)/shard_map/reshape;squeeze | solution.py:111
  45.1 22.2 %all-to-all-done = bf16[32,16,2048]{2,1,0:T(8,128)(2,1)} async-done(((bf16[32,16,2048]{2,1,0:T(8,128)(2,1)}), bf16[32,16,2048]{2,1,0:T(8,128)(2,1)}, u32[]{:S(2)}, u32[]{:S(2)}) %all-to-all-start) | async-done | bytes 2097184 | tf_op jit(solution)/shard_map/all_to_all | solution.py:95
  67.3 3.5 %fusion.4 = f32[512,768]{1,0:T(8,128)S(1)} fusion(bf16[512,2048]{1,0:T(8,128)(2,1)} %bitcast.15, bf16[1,2048,768]{2,1,0:T(8,128)(2,1)S(1)} %copy-done), kind=kOutput, calls=%fused_computation.4 | convolution fusion | flops 1610612736 | bytes 6815744 | tf_op jit(solution)/shard_map/dot_general | solution.py:12
  70.9 3.8 %multiply_convert_fusion = bf16[512,768]{1,0:T(8,128)(2,1)S(1)} fusion(f32[512,768]{1,0:T(8,128)S(1)} %fusion.4, bf16[512,2048]{1,0:T(8,128)(2,1)} %bitcast.15, bf16[1,2048,768]{2,1,0:T(8,128)(2,1)S(1)} %copy-done.14, f32[768]{0:T(1024)S(1)} %multiply_reduce_fusion.1), kind=kOutput, calls=%fused_computation.9 | convolution fusion | flops 1613758464 | bytes 7605248 | tf_op jit(solution)/shard_map/dot_general | solution.py:13
  74.7 3.2 %fusion.7 = bf16[8,64,4,512]{3,1,2,0:T(8,128)(2,1)} fusion(bf16[8,64,768,1]{2,1,3,0:T(8,128)(2,1)S(1)} %bitcast.222, bf16[768,4,512]{2,1,0:T(4,128)(2,1)S(1)} %copy-done.5), kind=kOutput, calls=%fused_computation.8 | convolution fusion | flops 1611661312 | bytes 6029312 | tf_op jit(solution)/shard_map/zrk,kjc->zjrc/dot_general | solution.py:108
  77.9 6.5 %all-to-all-start.1 = ((bf16[32,64,512]{2,1,0:T(8,128)(2,1)}), bf16[32,64,512]{2,1,0:T(8,128)(2,1)}, u32[]{:S(2)}, u32[]{:S(2)}) async-start(bf16[32,64,512]{2,1,0:T(8,128)(2,1)} %bitcast.206), calls=%async_computation.1 | async-start | bytes 4194304 | tf_op jit(solution)/shard_map/all_to_all | solution.py:115
  84.4 3.1 %collective-permute-start.1 = (bf16[1,272,512]{1,2,0:T(8,128)(2,1)}, bf16[1,272,512]{1,2,0:T(8,128)(2,1)}, u32[]{:S(2)}, u32[]{:S(2)}) collective-permute-start(bf16[1,272,512]{1,2,0:T(8,128)(2,1)} %get-tuple-element.57), channel_id=1, source_target_pairs={{0,2},{1,3},{2,0},{3,1},{4,6},{5,7},{6,4},{7,5},{8,10},{9,11},{10,... | collective-permute-start | bytes 835592 | tf_op jit(solution)/shard_map/ppermute | solution.py:93
  89.5 20.0 %collective-permute-done.1 = bf16[1,272,512]{1,2,0:T(8,128)(2,1)} collective-permute-done((bf16[1,272,512]{1,2,0:T(8,128)(2,1)}, bf16[1,272,512]{1,2,0:T(8,128)(2,1)}, u32[]{:S(2)}, u32[]{:S(2)}) %collective-permute-start.1) | collective-permute-done | bytes 278560 | tf_op jit(solution)/shard_map/ppermute | solution.py:93
  111.2 12.2 %collective-permute-done.2 = bf16[1,272,512]{1,2,0:T(8,128)(2,1)} collective-permute-done((bf16[1,272,512]{1,2,0:T(8,128)(2,1)}, bf16[1,272,512]{1,2,0:T(8,128)(2,1)}, u32[]{:S(2)}, u32[]{:S(2)}) %collective-permute-start.2) | collective-permute-done | bytes 278560 | tf_op jit(solution)/shard_map/ppermute | solution.py:93
  123.4 1.8 constant_dynamic-update-slice_fusion.5
  125.3 2.3 %slice_convert_fusion = (f32[4,3,512]{1,2,0:T(8,128)S(1)}, bf16[4,3,512]{1,2,0:T(8,128)(2,1)}) fusion(bf16[4,272,512]{1,2,0:T(8,128)(2,1)} %constant_dynamic-update-slice_fusion.5), kind=kLoop, calls=%fused_computation.50 | loop fusion | flops 6144 | bytes 61440 | tf_op jit(solution)/shard_map/convert_element_type | solution.py:99
  131.7 2.3 %fusion.76 = (bf16[4,128,512]{1,2,0:T(8,128)(2,1)}, bf16[4,128,512]{1,2,0:T(8,128)(2,1)}) fusion(bf16[4,272,512]{1,2,0:T(8,128)(2,1)} %constant_dynamic-update-slice_fusion.5), kind=kLoop, calls=%fused_computation.201 | loop fusion | bytes 2097152 | tf_op jit(solution)/shard_map/slice | solution.py:98
  134.0 2.8 %copy.152 = bf16[32,64,512]{2,0,1:T(8,128)(2,1)S(1)} copy(bf16[32,64,512]{2,1,0:T(8,128)(2,1)} %all-to-all-done.1) | data formatting | bytes 4194304 | tf_op jit(solution)/shard_map/all_to_all | solution.py:115
  141.0 3.2 %collective-permute-start.6 = (f32[520,128]{1,0:T(8,128)}, f32[520,128]{1,0:T(8,128)}, u32[]{:S(2)}, u32[]{:S(2)}) collective-permute-start(f32[520,128]{1,0:T(8,128)} %select_maximum_fusion.2), channel_id=1, source_target_pairs={{0,4},{4,8},{8,12},{12,16},{16,20},{20,24},{24,28},{1,5},{5,9},{9,... | collective-permute-start | bytes 798728 | tf_op jit(solution)/shard_map/ppermute | solution.py:192
  144.2 6.3 %collective-permute-start.7 = (f32[520,128]{1,0:T(8,128)}, f32[520,128]{1,0:T(8,128)}, u32[]{:S(2)}, u32[]{:S(2)}) collective-permute-start(f32[520,128]{1,0:T(8,128)} %select_maximum_fusion.2), channel_id=1, source_target_pairs={{0,8},{4,12},{8,16},{12,20},{16,24},{20,28},{1,9},{5,13},{9,17},{1... | collective-permute-start | bytes 798728 | tf_op jit(solution)/shard_map/ppermute | solution.py:192
  152.9 3.1 %collective-permute-start.4 = (bf16[128,512]{1,0:T(8,128)(2,1)S(1)}, bf16[128,512]{1,0:T(8,128)(2,1)S(1)}, u32[]{:S(2)}, u32[]{:S(2)}) collective-permute-start(bf16[128,512]{1,0:T(8,128)(2,1)S(1)} %get-tuple-element.69), channel_id=1, source_target_pairs={{0,2},{1,3},{2,0},{3,1},{4,6},{5,7},{6,4},{7,5},{8,10},{9,11},{10,... | collective-permute-start | bytes 393224 | tf_op jit(solution)/shard_map/ppermute | solution.py:175
  157.2 2.1 collective-permute-done.7
  161.3 9.1 %collective-permute-start.8 = (f32[520,128]{1,0:T(8,128)S(1)}, f32[520,128]{1,0:T(8,128)S(1)}, u32[]{:S(2)}, u32[]{:S(2)}) collective-permute-start(f32[520,128]{1,0:T(8,128)S(1)} %select_maximum_fusion.1), channel_id=1, source_target_pairs={{4,12},{8,16},{12,20},{16,24},{20,28},{5,13},{9,17},{13,21},{17,25... | collective-permute-start | bytes 798728 | tf_op jit(solution)/shard_map/ppermute | solution.py:192
  171.3 2.1 fusion.18
  175.2 16.1 %collective-permute-start.9 = (f32[520,128]{1,0:T(8,128)S(1)}, f32[520,128]{1,0:T(8,128)S(1)}, u32[]{:S(2)}, u32[]{:S(2)}) collective-permute-start(f32[520,128]{1,0:T(8,128)S(1)} %select_maximum_fusion), channel_id=1, source_target_pairs={{4,20},{8,24},{12,28},{5,21},{9,25},{13,29},{6,22},{10,26},{14,30}... | collective-permute-start | bytes 798728 | tf_op jit(solution)/shard_map/ppermute | solution.py:192
  191.4 3.8 %collective-permute-done.9 = f32[520,128]{1,0:T(8,128)S(1)} collective-permute-done((f32[520,128]{1,0:T(8,128)S(1)}, f32[520,128]{1,0:T(8,128)S(1)}, u32[]{:S(2)}, u32[]{:S(2)}) %collective-permute-start.9) | collective-permute-done | bytes 266272 | tf_op jit(solution)/shard_map/ppermute | solution.py:192
  196.2 2.8 %fusion.17 = f32[4,128,4,128]{1,3,2,0:T(8,128)} fusion(bf16[4,128,4,128]{1,3,2,0:T(8,128)(2,1)} %bitcast.198, f32[4,128,128]{1,2,0:T(8,128)} %copy.161, f32[4,4]{1,0:T(4,128)S(1)} %pad_maximum_fusion, f32[4,128,4]{1,2,0:T(4,128)S(1)} %get-tuple-element.85), kind=kOutput, calls=%fused_computation.20 | convolution fusion | flops 403177472 | bytes 1843264 | tf_op jit(solution)/shard_map/bthd,bhde->bthe/dot_general | solution.py:208
  199.0 3.9 %multiply_reduce_fusion = (f32[4,128,4]{1,2,0:T(4,128)S(1)}, f32[4,128,4,128]{1,3,2,0:T(8,128)}) fusion(f32[4,128,4,128]{1,3,2,0:T(8,128)} %fusion.17, f32[4,128,4,128]{1,3,2,0:T(8,128)} %fusion.18, bf16[4,128,4,128]{1,3,2,0:T(8,128)(2,1)} %bitcast.199, bf16[4,128,4,128]{1,3,2,0:T(8,128)(2,1)} %bitcast.201, f32[4,4,128]{2,1,0:T(4,128)S(1)} %reduce_window_sum.11, ...), kind=kOutput, calls=%fused_computation.37 | convolution fusion | flops 136574976 | bytes 4751360 | tf_op jit(solution)/shard_map/bhts,bshd->bthd/dot_general | solution.py:144
  207.6 1.9 collective-permute-start.10
  210.3 4.4 %collective-permute-start.11 = (bf16[128,512]{1,0:T(8,128)(2,1)}, bf16[128,512]{1,0:T(8,128)(2,1)S(1)}, u32[]{:S(2)}, u32[]{:S(2)}) collective-permute-start(bf16[128,512]{1,0:T(8,128)(2,1)} %bitcast.212), channel_id=1, source_target_pairs={{0,2},{1,3},{2,0},{3,1},{4,6},{5,7},{6,4},{7,5},{8,10},{9,11},{10,... | collective-permute-start | bytes 393224 | tf_op jit(solution)/shard_map/ppermute | solution.py:175
  216.6 1.8 collective-permute-done.11
  218.5 2.1 collective-permute-done.12
  (134 shorter events, 43.3 us)
Async XLA Ops:
  0.6 66.7 %copy-start = (bf16[1,2048,768]{2,1,0:T(8,128)(2,1)S(1)}, bf16[1,2048,768]{2,1,0:T(8,128)(2,1)}, u32[]{:S(2)}) copy-start(bf16[1,2048,768]{2,1,0:T(8,128)(2,1)} %param.19) | copy-start | bytes 9437188
  6.1 11.6 %copy-start.10 = (bf16[2048,32]{0,1:T(8,128)(2,1)S(1)}, bf16[2048,32]{0,1:T(8,128)(2,1)}, u32[]{:S(2)}) copy-start(bf16[2048,32]{0,1:T(8,128)(2,1)} %param.18) | copy-start | bytes 393220
  6.1 12.9 %copy-start.11 = (s32[128,2]{0,1:T(2,128)S(1)}, s32[128,2]{0,1:T(2,128)}, u32[]{:S(2)}) copy-start(s32[128,2]{0,1:T(2,128)} %param.17) | copy-start | bytes 3076
  6.1 13.5 %copy-start.12 = (f32[16,128]{1,0:T(8,128)S(1)}, f32[16,128]{1,0:T(8,128)}, u32[]{:S(2)}) copy-start(f32[16,128]{1,0:T(8,128)} %param.25) | copy-start | bytes 24580
  6.1 61.3 %all-to-all-start = ((bf16[32,16,2048]{2,1,0:T(8,128)(2,1)}), bf16[32,16,2048]{2,1,0:T(8,128)(2,1)}, u32[]{:S(2)}, u32[]{:S(2)}) async-start(bf16[32,16,2048]{2,1,0:T(8,128)(2,1)} %bitcast.197), calls=%async_computation | async-start | bytes 4194304 | tf_op jit(solution)/shard_map/all_to_all | solution.py:95
  34.2 2.0 copy-start.3
  37.4 7.7 %copy-start.13 = (s32[1,768]{1,0:T(1,128)S(1)}, s32[1,768]{1,0:T(1,128)}, u32[]{:S(2)}) copy-start(s32[1,768]{1,0:T(1,128)} %param.22) | copy-start | bytes 9220
  37.4 51.3 %collective-permute-start = (bf16[1,272,512]{1,2,0:T(8,128)(2,1)}, bf16[1,272,512]{1,2,0:T(8,128)(2,1)S(1)}, u32[]{:S(2)}, u32[]{:S(2)}) collective-permute-start(bf16[1,272,512]{1,2,0:T(8,128)(2,1)} %get-tuple-element.58), channel_id=1, source_target_pairs={{0,1},{1,2},{2,3},{3,0},{4,5},{5,6},{6,7},{7,4},{8,9},{9,10},{10,1... | collective-permute-start | bytes 835592 | tf_op jit(solution)/shard_map/ppermute | solution.py:93
  67.3 3.5 %copy-start.14 = (bf16[1,2048,768]{2,1,0:T(8,128)(2,1)S(1)}, bf16[1,2048,768]{2,1,0:T(8,128)(2,1)}, u32[]{:S(2)}) copy-start(bf16[1,2048,768]{2,1,0:T(8,128)(2,1)} %param.20) | copy-start | bytes 9437188
  70.9 3.8 %copy-start.5 = (bf16[768,4,512]{2,1,0:T(4,128)(2,1)S(1)}, bf16[768,4,512]{2,1,0:T(4,128)(2,1)}, u32[]{:S(2)}) copy-start(bf16[768,4,512]{2,1,0:T(4,128)(2,1)} %reshape_squeeze.3) | copy-start | bytes 9437188
  77.9 56.0 %all-to-all-start.1 = ((bf16[32,64,512]{2,1,0:T(8,128)(2,1)}), bf16[32,64,512]{2,1,0:T(8,128)(2,1)}, u32[]{:S(2)}, u32[]{:S(2)}) async-start(bf16[32,64,512]{2,1,0:T(8,128)(2,1)} %bitcast.206), calls=%async_computation.1 | async-start | bytes 4194304 | tf_op jit(solution)/shard_map/all_to_all | solution.py:115
  84.4 25.0 %collective-permute-start.1 = (bf16[1,272,512]{1,2,0:T(8,128)(2,1)}, bf16[1,272,512]{1,2,0:T(8,128)(2,1)}, u32[]{:S(2)}, u32[]{:S(2)}) collective-permute-start(bf16[1,272,512]{1,2,0:T(8,128)(2,1)} %get-tuple-element.57), channel_id=1, source_target_pairs={{0,2},{1,3},{2,0},{3,1},{4,6},{5,7},{6,4},{7,5},{8,10},{9,11},{10,... | collective-permute-start | bytes 835592 | tf_op jit(solution)/shard_map/ppermute | solution.py:93
  87.5 35.9 %collective-permute-start.2 = (bf16[1,272,512]{1,2,0:T(8,128)(2,1)}, bf16[1,272,512]{1,2,0:T(8,128)(2,1)}, u32[]{:S(2)}, u32[]{:S(2)}) collective-permute-start(bf16[1,272,512]{1,2,0:T(8,128)(2,1)} %get-tuple-element.56), channel_id=1, source_target_pairs={{0,3},{1,0},{2,1},{3,2},{4,7},{5,4},{6,5},{7,6},{8,11},{9,8},{10,9... | collective-permute-start | bytes 835592 | tf_op jit(solution)/shard_map/ppermute | solution.py:93
  137.2 1.0 copy-start.4
  137.8 2.1 copy-start.1
  141.0 16.3 %collective-permute-start.6 = (f32[520,128]{1,0:T(8,128)}, f32[520,128]{1,0:T(8,128)}, u32[]{:S(2)}, u32[]{:S(2)}) collective-permute-start(f32[520,128]{1,0:T(8,128)} %select_maximum_fusion.2), channel_id=1, source_target_pairs={{0,4},{4,8},{8,12},{12,16},{16,20},{20,24},{24,28},{1,5},{5,9},{9,... | collective-permute-start | bytes 798728 | tf_op jit(solution)/shard_map/ppermute | solution.py:192
  144.2 15.1 %collective-permute-start.7 = (f32[520,128]{1,0:T(8,128)}, f32[520,128]{1,0:T(8,128)}, u32[]{:S(2)}, u32[]{:S(2)}) collective-permute-start(f32[520,128]{1,0:T(8,128)} %select_maximum_fusion.2), channel_id=1, source_target_pairs={{0,8},{4,12},{8,16},{12,20},{16,24},{20,28},{1,9},{5,13},{9,17},{1... | collective-permute-start | bytes 798728 | tf_op jit(solution)/shard_map/ppermute | solution.py:192
  150.6 20.7 %copy-start.2 = (bf16[4,128,512]{1,2,0:T(8,128)(2,1)S(1)}, bf16[4,128,512]{1,2,0:T(8,128)(2,1)}, u32[]{:S(2)}) copy-start(bf16[4,128,512]{1,2,0:T(8,128)(2,1)} %get-tuple-element.53) | copy-start | bytes 1572868
  150.6 20.7 %copy-start.6 = (f32[1,4,128,128]{3,2,1,0:T(8,128)S(1)}, f32[1,4,128,128]{3,2,1,0:T(8,128)}, u32[]{:S(2)}) copy-start(f32[1,4,128,128]{3,2,1,0:T(8,128)} %get-tuple-element.41) | copy-start | bytes 786436
  150.6 20.7 %copy-start.7 = (f32[1,4,128,128]{3,2,1,0:T(8,128)S(1)}, f32[1,4,128,128]{3,2,1,0:T(8,128)}, u32[]{:S(2)}) copy-start(f32[1,4,128,128]{3,2,1,0:T(8,128)} %get-tuple-element.42) | copy-start | bytes 786436
  151.8 39.5 %collective-permute-start.3 = (bf16[128,512]{1,0:T(8,128)(2,1)S(1)}, bf16[128,512]{1,0:T(8,128)(2,1)S(1)}, u32[]{:S(2)}, u32[]{:S(2)}) collective-permute-start(bf16[128,512]{1,0:T(8,128)(2,1)S(1)} %get-tuple-element.70), channel_id=1, source_target_pairs={{0,1},{1,2},{2,3},{3,0},{4,5},{5,6},{6,7},{7,4},{8,9},{9,10},{10,1... | collective-permute-start | bytes 393224 | tf_op jit(solution)/shard_map/ppermute | solution.py:175
  152.9 38.5 %collective-permute-start.4 = (bf16[128,512]{1,0:T(8,128)(2,1)S(1)}, bf16[128,512]{1,0:T(8,128)(2,1)S(1)}, u32[]{:S(2)}, u32[]{:S(2)}) collective-permute-start(bf16[128,512]{1,0:T(8,128)(2,1)S(1)} %get-tuple-element.69), channel_id=1, source_target_pairs={{0,2},{1,3},{2,0},{3,1},{4,6},{5,7},{6,4},{7,5},{8,10},{9,11},{10,... | collective-permute-start | bytes 393224 | tf_op jit(solution)/shard_map/ppermute | solution.py:175
  156.0 35.4 %collective-permute-start.5 = (bf16[128,512]{1,0:T(8,128)(2,1)S(1)}, bf16[128,512]{1,0:T(8,128)(2,1)S(1)}, u32[]{:S(2)}, u32[]{:S(2)}) collective-permute-start(bf16[128,512]{1,0:T(8,128)(2,1)S(1)} %get-tuple-element.68), channel_id=1, source_target_pairs={{0,3},{1,0},{2,1},{3,2},{4,7},{5,4},{6,5},{7,6},{8,11},{9,8},{10,9... | collective-permute-start | bytes 393224 | tf_op jit(solution)/shard_map/ppermute | solution.py:175
  161.3 13.0 %collective-permute-start.8 = (f32[520,128]{1,0:T(8,128)S(1)}, f32[520,128]{1,0:T(8,128)S(1)}, u32[]{:S(2)}, u32[]{:S(2)}) collective-permute-start(f32[520,128]{1,0:T(8,128)S(1)} %select_maximum_fusion.1), channel_id=1, source_target_pairs={{4,12},{8,16},{12,20},{16,24},{20,28},{5,13},{9,17},{13,21},{17,25... | collective-permute-start | bytes 798728 | tf_op jit(solution)/shard_map/ppermute | solution.py:192
  175.2 20.0 %collective-permute-start.9 = (f32[520,128]{1,0:T(8,128)S(1)}, f32[520,128]{1,0:T(8,128)S(1)}, u32[]{:S(2)}, u32[]{:S(2)}) collective-permute-start(f32[520,128]{1,0:T(8,128)S(1)} %select_maximum_fusion), channel_id=1, source_target_pairs={{4,20},{8,24},{12,28},{5,21},{9,25},{13,29},{6,22},{10,26},{14,30}... | collective-permute-start | bytes 798728 | tf_op jit(solution)/shard_map/ppermute | solution.py:192
  191.4 3.8 %copy-start.9 = (bf16[128,2048]{1,0:T(8,128)(2,1)}, bf16[128,2048]{1,0:T(8,128)(2,1)S(1)}, u32[]{:S(2)}) copy-start(bf16[128,2048]{1,0:T(8,128)(2,1)S(1)} %constant_dynamic-update-slice_fusion.2) | copy-start | bytes 1572868
  207.6 8.1 %collective-permute-start.10 = (bf16[128,512]{1,0:T(8,128)(2,1)}, bf16[128,512]{1,0:T(8,128)(2,1)}, u32[]{:S(2)}, u32[]{:S(2)}) collective-permute-start(bf16[128,512]{1,0:T(8,128)(2,1)} %bitcast.213), channel_id=1, source_target_pairs={{0,1},{1,2},{2,3},{3,0},{4,5},{5,6},{6,7},{7,4},{8,9},{9,10},{10,1... | collective-permute-start | bytes 393224 | tf_op jit(solution)/shard_map/ppermute | solution.py:175
  210.3 8.2 %collective-permute-start.11 = (bf16[128,512]{1,0:T(8,128)(2,1)}, bf16[128,512]{1,0:T(8,128)(2,1)S(1)}, u32[]{:S(2)}, u32[]{:S(2)}) collective-permute-start(bf16[128,512]{1,0:T(8,128)(2,1)} %bitcast.212), channel_id=1, source_target_pairs={{0,2},{1,3},{2,0},{3,1},{4,6},{5,7},{6,4},{7,5},{8,10},{9,11},{10,... | collective-permute-start | bytes 393224 | tf_op jit(solution)/shard_map/ppermute | solution.py:175
  215.4 5.2 %collective-permute-start.12 = (bf16[128,512]{1,0:T(8,128)(2,1)}, bf16[128,512]{1,0:T(8,128)(2,1)S(1)}, u32[]{:S(2)}, u32[]{:S(2)}) collective-permute-start(bf16[128,512]{1,0:T(8,128)(2,1)} %bitcast.211), channel_id=1, source_target_pairs={{0,3},{1,0},{2,1},{3,2},{4,7},{5,4},{6,5},{7,6},{8,11},{9,8},{10,9... | collective-permute-start | bytes 393224 | tf_op jit(solution)/shard_map/ppermute | solution.py:175
  220.6 0.8 copy-start.8

commit v12 on v11

--- a/solution.py
+++ b/solution.py
@@ -204,8 +204,8 @@
         reach *= 2
     before = window[0]
 
-    far = jnp.stack(leads)[:, :, None, None] * before[None]
-    total_out = near + growth * jnp.einsum("bthd,bhde->bthe", q32, far, precision=highest)
+    far_scale = growth * jnp.stack(leads)[:, None, :, None]
+    total_out = near + far_scale * jnp.einsum("bthd,hde->bthe", q32, before, precision=highest)
     normed = total_out * lax.rsqrt(jnp.mean(total_out * total_out, axis=3, keepdims=True) + 1e-06)
     att_q = normed.astype(jnp.bfloat16).reshape(n_sy, count, qw)
     attended = send_home(att_q, heads * hd)

time: 223 us -> 218 us (0.978)
  starting transfers between devices: 70.2 us -> 58.7 us
  local copies, waits for them, and re-layouts: 47.1 us -> 58 us
  waiting for transfers between devices: 65.2 us -> 60.4 us
    all_to_all x1, waiting for transfers between devices: 0.01 us -> 37.4 us  [body(): back = lax.all_to_all(outgoing, seq_axes, 0, 0, tiled=True)]
    ppermute x3, waiting for transfers between devices: 32.1 us -> 2.87 us  [body(): lax.ppermute(piece, 'sy', [(i, (i + by) % n_sy) for i in range(n_sy)])]
    ppermute x4, starting transfers between devices: 34.7 us -> 21.8 us  [shifted(): got_value, got_span = unpack(lax.ppermute(packed, 'sz', pairs))]
    all_to_all x1, waiting for transfers between devices: 22.2 us -> 12.3 us  [body(): lax.all_to_all(send.reshape(n_experts, SLOTS, width), seq_axes, 0, 0, til...]
    reshape x0 -> x4, local copies, waits for them, and re-layouts: none -> 6.47 us  [unpack(): packed[:state_rows].reshape(quarter, hd, hd)]
    ppermute x4, waiting for transfers between devices: 6.66 us -> 3.76 us  [shifted(): got_value, got_span = unpack(lax.ppermute(packed, 'sz', pairs))]
    dynamic_update_slice x8, local copies, waits for them, and re-layouts: 1.93 us -> 4.77 us  [send_home(): lax.dynamic_update_slice(assembled, piece, (0, (yi - by) % n_sy * qw))]
    unnamed x33 -> x41, local copies, waits for them, and re-layouts: 6.96 us -> 7.49 us
  transfers between devices with their start and end apart: 15 -> 15, of which waited for: 9 -> 8; matrix products, arithmetic and copies ran while one was open for 26% -> 34% of each run, Pallas kernels for 0% -> 0%
where the time goes in v12:
time: 218 us; the launch traced here: 216 us
  waiting for transfers between devices  60.4 us (28%)
  starting transfers between devices  58.7 us (27%)
  local copies, waits for them, and re-layouts  58 us (27%)
  matrix products  24.9 us (11%)
  other arithmetic  12.8 us (6%)
    all_to_all x1, waiting for transfers between devices, body(): back = lax.all_to_all(outgoing, seq_axes, 0, 0, tiled=True)  37.4 us
    ppermute x4, starting transfers between devices, shifted(): got_value, got_span = unpack(lax.ppermute(packed, 'sz', pairs))  21.8 us
    ppermute x6, starting transfers between devices, send_home(): lax.ppermute(piece, 'sy', [(i, (i + by) % n_sy) for i in range(n_sy)])  13.3 us
    all_to_all x1, waiting for transfers between devices, body(): lax.all_to_all(send.reshape(n_experts, SLOTS, width), seq_axes, 0, 0, til...  12.3 us
    all_to_all x1, starting transfers between devices, body(): lax.all_to_all(send.reshape(n_experts, SLOTS, width), seq_axes, 0, 0, til...  11.5 us
    unnamed x41, local copies, waits for them, and re-layouts  7.49 us
    all_to_all x1, starting transfers between devices, body(): back = lax.all_to_all(outgoing, seq_axes, 0, 0, tiled=True)  6.52 us
    reshape x4, local copies, waits for them, and re-layouts, unpack(): packed[:state_rows].reshape(quarter, hd, hd)  6.47 us
  transfers between devices with their start and end apart: 15, of which 8 were waited for; matrix products, arithmetic and copies ran while one was open for 34% of the time, Pallas kernels for 0%

profile of v12, /device:TPU:36, one launch (start us, length us, event | category | flops | bytes accessed | tf_op | source)
XLA Modules:
  0.0 216.1 jit_solution(10011821227570245187)
XLA Ops:
  3.0 3.1 %convolution_convert_fusion = bf16[512,2048]{1,0:T(8,128)(2,1)} fusion(bf16[512,128]{1,0:T(8,128)(2,1)S(1)} %fusion.53, bf16[128,2048]{1,0:T(8,128)(2,1)} %param.16), kind=kOutput, calls=%fused_computation.7 | convolution fusion | flops 269484032 | bytes 2752512 | tf_op jit(solution)/shard_map/dot_general | solution.py:63
  6.1 11.5 %all-to-all-start = ((bf16[32,16,2048]{2,1,0:T(8,128)(2,1)}), bf16[32,16,2048]{2,1,0:T(8,128)(2,1)}, u32[]{:S(2)}, u32[]{:S(2)}) async-start(bf16[32,16,2048]{2,1,0:T(8,128)(2,1)} %bitcast.202), calls=%async_computation | async-start | bytes 4194304 | tf_op jit(solution)/shard_map/all_to_all | solution.py:95
  22.8 2.0 copy.158
  24.8 2.0 copy.159
  28.7 5.6 %concatenate.21 = bf16[4,272,512]{1,2,0:T(8,128)(2,1)} concatenate(bf16[4,128,512]{1,2,0:T(8,128)(2,1)} %bitcast.208, bf16[4,128,512]{1,2,0:T(8,128)(2,1)} %bitcast.209, bf16[4,1,512]{1,2,0:T(8,128)(2,1)} %copy.162, bf16[4,1,512]{1,2,0:T(8,128)(2,1)} %copy.163, bf16[4,1,512]{1,2,0:T(8,128)(2,1)} %copy.164, bf16[4,3,512]{1,2,0:T(8,128)(2,1)} %broadcast_in_dim.18, ...), dimensions={1} | concatenate | bytes 2228224 | tf_op jit(solution)/shard_map/concatenate | solution.py:78
  38.9 2.7 %collective-permute-start.1 = (bf16[1,272,512]{1,2,0:T(8,128)(2,1)}, bf16[1,272,512]{1,2,0:T(8,128)(2,1)}, u32[]{:S(2)}, u32[]{:S(2)}) collective-permute-start(bf16[1,272,512]{1,2,0:T(8,128)(2,1)} %get-tuple-element.57), channel_id=1, source_target_pairs={{0,2},{1,3},{2,0},{3,1},{4,6},{5,7},{6,4},{7,5},{8,10},{9,11},{10,... | collective-permute-start | bytes 835592 | tf_op jit(solution)/shard_map/ppermute | solution.py:93
  43.0 6.2 %reshape_squeeze.3 = bf16[768,4,512]{2,1,0:T(4,128)(2,1)} reshape(bf16[1,768,2048]{2,1,0:T(8,128)(2,1)} %param.21) | data formatting | bytes 6291456 | tf_op jit(solution)/shard_map/reshape;squeeze | solution.py:111
  50.4 2.9 %collective-permute-done = bf16[1,272,512]{1,2,0:T(8,128)(2,1)} collective-permute-done((bf16[1,272,512]{1,2,0:T(8,128)(2,1)}, bf16[1,272,512]{1,2,0:T(8,128)(2,1)}, u32[]{:S(2)}, u32[]{:S(2)}) %collective-permute-start) | collective-permute-done | bytes 278560 | tf_op jit(solution)/shard_map/ppermute | solution.py:93
  53.2 1.8 constant_dynamic-update-slice_fusion.7
  55.0 12.3 %all-to-all-done = bf16[32,16,2048]{2,1,0:T(8,128)(2,1)} async-done(((bf16[32,16,2048]{2,1,0:T(8,128)(2,1)}), bf16[32,16,2048]{2,1,0:T(8,128)(2,1)}, u32[]{:S(2)}, u32[]{:S(2)}) %all-to-all-start) | async-done | bytes 2097184 | tf_op jit(solution)/shard_map/all_to_all | solution.py:95
  67.3 3.5 %fusion.4 = f32[512,768]{1,0:T(8,128)S(1)} fusion(bf16[512,2048]{1,0:T(8,128)(2,1)} %bitcast.15, bf16[1,2048,768]{2,1,0:T(8,128)(2,1)S(1)} %copy-done), kind=kOutput, calls=%fused_computation.4 | convolution fusion | flops 1610612736 | bytes 6815744 | tf_op jit(solution)/shard_map/dot_general | solution.py:12
  70.9 3.8 %multiply_convert_fusion = bf16[512,768]{1,0:T(8,128)(2,1)S(1)} fusion(f32[512,768]{1,0:T(8,128)S(1)} %fusion.4, bf16[512,2048]{1,0:T(8,128)(2,1)} %bitcast.15, bf16[1,2048,768]{2,1,0:T(8,128)(2,1)S(1)} %copy-done.18, f32[768]{0:T(1024)S(1)} %multiply_reduce_fusion.1), kind=kOutput, calls=%fused_computation.9 | convolution fusion | flops 1613758464 | bytes 7605248 | tf_op jit(solution)/shard_map/dot_general | solution.py:13
  74.7 3.2 %fusion.7 = bf16[8,64,4,512]{3,1,2,0:T(8,128)(2,1)} fusion(bf16[8,64,768,1]{2,1,3,0:T(8,128)(2,1)S(1)} %bitcast.227, bf16[768,4,512]{2,1,0:T(4,128)(2,1)S(1)} %copy-done.5), kind=kOutput, calls=%fused_computation.8 | convolution fusion | flops 1611661312 | bytes 6029312 | tf_op jit(solution)/shard_map/zrk,kjc->zjrc/dot_general | solution.py:108
  77.9 6.5 %all-to-all-start.1 = ((bf16[32,64,512]{2,1,0:T(8,128)(2,1)}), bf16[32,64,512]{2,1,0:T(8,128)(2,1)}, u32[]{:S(2)}, u32[]{:S(2)}) async-start(bf16[32,64,512]{2,1,0:T(8,128)(2,1)} %bitcast.211), calls=%async_computation.1 | async-start | bytes 4194304 | tf_op jit(solution)/shard_map/all_to_all | solution.py:115
  84.5 1.8 constant_dynamic-update-slice_fusion.6
  87.1 2.2 %slice_convert_fusion = (f32[4,3,512]{1,2,0:T(8,128)S(1)}, bf16[4,3,512]{1,2,0:T(8,128)(2,1)}) fusion(bf16[4,272,512]{1,2,0:T(8,128)(2,1)} %constant_dynamic-update-slice_fusion.5), kind=kLoop, calls=%fused_computation.49 | loop fusion | flops 6144 | bytes 61440 | tf_op jit(solution)/shard_map/convert_element_type | solution.py:99
  93.5 2.3 %fusion.83 = (bf16[4,128,512]{1,2,0:T(8,128)(2,1)}, bf16[4,128,512]{1,2,0:T(8,128)(2,1)}) fusion(bf16[4,272,512]{1,2,0:T(8,128)(2,1)} %constant_dynamic-update-slice_fusion.5), kind=kLoop, calls=%fused_computation.208 | loop fusion | bytes 2097152 | tf_op jit(solution)/shard_map/slice | solution.py:98
  95.8 37.4 %all-to-all-done.1 = bf16[32,64,512]{2,1,0:T(8,128)(2,1)} async-done(((bf16[32,64,512]{2,1,0:T(8,128)(2,1)}), bf16[32,64,512]{2,1,0:T(8,128)(2,1)}, u32[]{:S(2)}, u32[]{:S(2)}) %all-to-all-start.1) | async-done | bytes 2097184 | tf_op jit(solution)/shard_map/all_to_all | solution.py:115
  133.2 2.8 %copy.170 = bf16[32,64,512]{2,0,1:T(8,128)(2,1)S(1)} copy(bf16[32,64,512]{2,1,0:T(8,128)(2,1)} %all-to-all-done.1) | data formatting | bytes 4194304 | tf_op jit(solution)/shard_map/all_to_all | solution.py:115
  138.8 4.0 %collective-permute-start.6 = (f32[520,128]{1,0:T(8,128)S(1)}, f32[520,128]{1,0:T(8,128)S(1)}, u32[]{:S(2)}, u32[]{:S(2)}) collective-permute-start(f32[520,128]{1,0:T(8,128)S(1)} %select_maximum_fusion.2), channel_id=1, source_target_pairs={{0,4},{4,8},{8,12},{12,16},{16,20},{20,24},{24,28},{1,5},{5,9},{9,... | collective-permute-start | bytes 798728 | tf_op jit(solution)/shard_map/ppermute | solution.py:192
  142.8 2.6 %collective-permute-start.7 = (f32[520,128]{1,0:T(8,128)S(1)}, f32[520,128]{1,0:T(8,128)S(1)}, u32[]{:S(2)}, u32[]{:S(2)}) collective-permute-start(f32[520,128]{1,0:T(8,128)S(1)} %select_maximum_fusion.2), channel_id=1, source_target_pairs={{0,8},{4,12},{8,16},{12,20},{16,24},{20,28},{1,9},{5,13},{9,17},{1... | collective-permute-start | bytes 798728 | tf_op jit(solution)/shard_map/ppermute | solution.py:192
  148.1 2.6 %collective-permute-start.5 = (bf16[128,512]{1,0:T(8,128)(2,1)}, bf16[128,512]{1,0:T(8,128)(2,1)S(1)}, u32[]{:S(2)}, u32[]{:S(2)}) collective-permute-start(bf16[128,512]{1,0:T(8,128)(2,1)} %get-tuple-element.68), channel_id=1, source_target_pairs={{0,3},{1,0},{2,1},{3,2},{4,7},{5,4},{6,5},{7,6},{8,11},{9,8},{10,9... | collective-permute-start | bytes 393224 | tf_op jit(solution)/shard_map/ppermute | solution.py:175
  150.9 2.1 fusion.18
  153.8 2.9 %collective-permute-done.7 = f32[520,128]{1,0:T(8,128)S(1)} collective-permute-done((f32[520,128]{1,0:T(8,128)S(1)}, f32[520,128]{1,0:T(8,128)S(1)}, u32[]{:S(2)}, u32[]{:S(2)}) %collective-permute-start.7) | collective-permute-done | bytes 266272 | tf_op jit(solution)/shard_map/ppermute | solution.py:192
  158.9 6.1 %collective-permute-start.8 = (f32[520,128]{1,0:T(8,128)}, f32[520,128]{1,0:T(8,128)}, u32[]{:S(2)}, u32[]{:S(2)}) collective-permute-start(f32[520,128]{1,0:T(8,128)} %select_maximum_fusion.1), channel_id=1, source_target_pairs={{4,12},{8,16},{12,20},{16,24},{20,28},{5,13},{9,17},{13,21},{17,25... | collective-permute-start | bytes 798728 | tf_op jit(solution)/shard_map/ppermute | solution.py:192
  165.0 3.6 %fusion.17 = f32[4,128,4,128]{1,3,2,0:T(8,128)} fusion(f32[4,128,4,128]{1,3,2,0:T(8,128)} %fusion.18, bf16[4,128,4,128]{1,3,2,0:T(8,128)(2,1)} %bitcast.203, bf16[4,128,4,128]{1,3,2,0:T(8,128)(2,1)} %bitcast.206, f32[4,4,128]{2,1,0:T(4,128)S(1)} %reduce_window_sum.11, pred[128,128]{1,0:T(8,128)(4,1)} %iota_compare_fusion.4, bf16[4,128,512]{2,1,0:T(8,128)(2,1)} %copy-done.1), kind=kOutput, calls=%fused_computation.19 | convolution fusion | flops 135790592 | bytes 3694592 | tf_op jit(solution)/shard_map/bhts,bshd->bthd/dot_general | solution.py:144
  173.0 9.1 %collective-permute-start.9 = (f32[520,128]{1,0:T(8,128)}, f32[520,128]{1,0:T(8,128)}, u32[]{:S(2)}, u32[]{:S(2)}) collective-permute-start(f32[520,128]{1,0:T(8,128)} %select_maximum_fusion), channel_id=1, source_target_pairs={{4,20},{8,24},{12,28},{5,21},{9,25},{13,29},{6,22},{10,26},{14,30}... | collective-permute-start | bytes 798728 | tf_op jit(solution)/shard_map/ppermute | solution.py:192
  188.8 1.8 copy.180
  194.1 2.4 %multiply_reduce_fusion = (f32[4,128,4]{1,2,0:T(4,128)S(1)}, f32[4,128,4,128]{1,3,2,0:T(8,128)S(1)}) fusion(f32[4,128,4,128]{1,3,2,0:T(8,128)} %fusion.17, bf16[4,128,4,128]{1,3,2,0:T(8,128)(2,1)} %bitcast.204, f32[4,128,128]{1,2,0:T(8,128)} %copy.182, f32[4,128,128]{1,2,0:T(8,128)S(1)} %copy.181, f32[4,128,128]{1,2,0:T(8,128)} %copy.180, ...), kind=kOutput, calls=%fused_computation.37 | convolution fusion | flops 404092928 | bytes 3686448 | tf_op jit(solution)/shard_map/bthd,hde->bthe/dot_general | solution.py:208
  200.0 4.0 %collective-permute-start.10 = (bf16[128,512]{1,0:T(8,128)(2,1)}, bf16[128,512]{1,0:T(8,128)(2,1)}, u32[]{:S(2)}, u32[]{:S(2)}) collective-permute-start(bf16[128,512]{1,0:T(8,128)(2,1)} %bitcast.218), channel_id=1, source_target_pairs={{0,1},{1,2},{2,3},{3,0},{4,5},{5,6},{6,7},{7,4},{8,9},{9,10},{10,1... | collective-permute-start | bytes 393224 | tf_op jit(solution)/shard_map/ppermute | solution.py:175
  204.8 4.6 %collective-permute-start.11 = (bf16[128,512]{1,0:T(8,128)(2,1)}, bf16[128,512]{1,0:T(8,128)(2,1)S(1)}, u32[]{:S(2)}, u32[]{:S(2)}) collective-permute-start(bf16[128,512]{1,0:T(8,128)(2,1)} %bitcast.217), channel_id=1, source_target_pairs={{0,2},{1,3},{2,0},{3,1},{4,6},{5,7},{6,4},{7,5},{8,10},{9,11},{10,... | collective-permute-start | bytes 393224 | tf_op jit(solution)/shard_map/ppermute | solution.py:175
  211.8 2.8 %collective-permute-done.11 = bf16[128,512]{1,0:T(8,128)(2,1)S(1)} collective-permute-done((bf16[128,512]{1,0:T(8,128)(2,1)}, bf16[128,512]{1,0:T(8,128)(2,1)S(1)}, u32[]{:S(2)}, u32[]{:S(2)}) %collective-permute-start.11) | collective-permute-done | bytes 131104 | tf_op jit(solution)/shard_map/ppermute | solution.py:175
  (145 shorter events, 52.8 us)
Async XLA Ops:
  0.6 66.7 %copy-start = (bf16[1,2048,768]{2,1,0:T(8,128)(2,1)S(1)}, bf16[1,2048,768]{2,1,0:T(8,128)(2,1)}, u32[]{:S(2)}) copy-start(bf16[1,2048,768]{2,1,0:T(8,128)(2,1)} %param.19) | copy-start | bytes 9437188
  6.1 11.6 %copy-start.10 = (bf16[2048,32]{0,1:T(8,128)(2,1)S(1)}, bf16[2048,32]{0,1:T(8,128)(2,1)}, u32[]{:S(2)}) copy-start(bf16[2048,32]{0,1:T(8,128)(2,1)} %param.18) | copy-start | bytes 393220
  6.1 12.9 %copy-start.11 = (s32[128,2]{0,1:T(2,128)S(1)}, s32[128,2]{0,1:T(2,128)}, u32[]{:S(2)}) copy-start(s32[128,2]{0,1:T(2,128)} %param.17) | copy-start | bytes 3076
  6.1 13.5 %copy-start.12 = (f32[16,128]{1,0:T(8,128)S(1)}, f32[16,128]{1,0:T(8,128)}, u32[]{:S(2)}) copy-start(f32[16,128]{1,0:T(8,128)} %param.25) | copy-start | bytes 24580
  6.1 61.3 %all-to-all-start = ((bf16[32,16,2048]{2,1,0:T(8,128)(2,1)}), bf16[32,16,2048]{2,1,0:T(8,128)(2,1)}, u32[]{:S(2)}, u32[]{:S(2)}) async-start(bf16[32,16,2048]{2,1,0:T(8,128)(2,1)} %bitcast.202), calls=%async_computation | async-start | bytes 4194304 | tf_op jit(solution)/shard_map/all_to_all | solution.py:95
  34.3 2.0 copy-start.3
  37.4 15.8 %collective-permute-start = (bf16[1,272,512]{1,2,0:T(8,128)(2,1)}, bf16[1,272,512]{1,2,0:T(8,128)(2,1)}, u32[]{:S(2)}, u32[]{:S(2)}) collective-permute-start(bf16[1,272,512]{1,2,0:T(8,128)(2,1)} %get-tuple-element.58), channel_id=1, source_target_pairs={{0,1},{1,2},{2,3},{3,0},{4,5},{5,6},{6,7},{7,4},{8,9},{9,10},{10,1... | collective-permute-start | bytes 835592 | tf_op jit(solution)/shard_map/ppermute | solution.py:93
  38.9 45.5 %collective-permute-start.1 = (bf16[1,272,512]{1,2,0:T(8,128)(2,1)}, bf16[1,272,512]{1,2,0:T(8,128)(2,1)}, u32[]{:S(2)}, u32[]{:S(2)}) collective-permute-start(bf16[1,272,512]{1,2,0:T(8,128)(2,1)} %get-tuple-element.57), channel_id=1, source_target_pairs={{0,2},{1,3},{2,0},{3,1},{4,6},{5,7},{6,4},{7,5},{8,10},{9,11},{10,... | collective-permute-start | bytes 835592 | tf_op jit(solution)/shard_map/ppermute | solution.py:93
  41.6 44.7 %collective-permute-start.2 = (bf16[1,272,512]{1,2,0:T(8,128)(2,1)}, bf16[1,272,512]{1,2,0:T(8,128)(2,1)S(1)}, u32[]{:S(2)}, u32[]{:S(2)}) collective-permute-start(bf16[1,272,512]{1,2,0:T(8,128)(2,1)} %get-tuple-element.56), channel_id=1, source_target_pairs={{0,3},{1,0},{2,1},{3,2},{4,7},{5,4},{6,5},{7,6},{8,11},{9,8},{10,9... | collective-permute-start | bytes 835592 | tf_op jit(solution)/shard_map/ppermute | solution.py:93
  43.0 6.7 %copy-start.16 = (s32[1,768]{1,0:T(1,128)S(1)}, s32[1,768]{1,0:T(1,128)}, u32[]{:S(2)}) copy-start(s32[1,768]{1,0:T(1,128)} %param.22) | copy-start | bytes 9220
  67.3 3.5 %copy-start.18 = (bf16[1,2048,768]{2,1,0:T(8,128)(2,1)S(1)}, bf16[1,2048,768]{2,1,0:T(8,128)(2,1)}, u32[]{:S(2)}) copy-start(bf16[1,2048,768]{2,1,0:T(8,128)(2,1)} %param.20) | copy-start | bytes 9437188
  70.9 3.8 %copy-start.5 = (bf16[768,4,512]{2,1,0:T(4,128)(2,1)S(1)}, bf16[768,4,512]{2,1,0:T(4,128)(2,1)}, u32[]{:S(2)}) copy-start(bf16[768,4,512]{2,1,0:T(4,128)(2,1)} %reshape_squeeze.3) | copy-start | bytes 9437188
  77.9 55.3 %all-to-all-start.1 = ((bf16[32,64,512]{2,1,0:T(8,128)(2,1)}), bf16[32,64,512]{2,1,0:T(8,128)(2,1)}, u32[]{:S(2)}, u32[]{:S(2)}) async-start(bf16[32,64,512]{2,1,0:T(8,128)(2,1)} %bitcast.211), calls=%async_computation.1 | async-start | bytes 4194304 | tf_op jit(solution)/shard_map/all_to_all | solution.py:115
  136.5 1.0 copy-start.4
  137.1 13.7 %copy-start.1 = (bf16[4,128,512]{2,1,0:T(8,128)(2,1)}, bf16[4,128,512]{2,1,0:T(8,128)(2,1)S(1)}, u32[]{:S(2)}) copy-start(bf16[4,128,512]{2,1,0:T(8,128)(2,1)S(1)} %fusion.19) | copy-start | bytes 1572868
  138.4 12.5 %copy-start.2 = (bf16[4,128,512]{1,2,0:T(8,128)(2,1)S(1)}, bf16[4,128,512]{1,2,0:T(8,128)(2,1)}, u32[]{:S(2)}) copy-start(bf16[4,128,512]{1,2,0:T(8,128)(2,1)} %get-tuple-element.53) | copy-start | bytes 1572868
  138.4 12.5 %copy-start.17 = (f32[4]{0:T(128)S(1)}, f32[4]{0:T(128)}, u32[]{:S(2)}) copy-start(f32[4]{0:T(128)} %pad.29.clone) | copy-start | bytes 52
  138.8 15.0 %collective-permute-start.6 = (f32[520,128]{1,0:T(8,128)S(1)}, f32[520,128]{1,0:T(8,128)S(1)}, u32[]{:S(2)}, u32[]{:S(2)}) collective-permute-start(f32[520,128]{1,0:T(8,128)S(1)} %select_maximum_fusion.2), channel_id=1, source_target_pairs={{0,4},{4,8},{8,12},{12,16},{16,20},{20,24},{24,28},{1,5},{5,9},{9,... | collective-permute-start | bytes 798728 | tf_op jit(solution)/shard_map/ppermute | solution.py:192
  142.8 13.9 %collective-permute-start.7 = (f32[520,128]{1,0:T(8,128)S(1)}, f32[520,128]{1,0:T(8,128)S(1)}, u32[]{:S(2)}, u32[]{:S(2)}) collective-permute-start(f32[520,128]{1,0:T(8,128)S(1)} %select_maximum_fusion.2), channel_id=1, source_target_pairs={{0,8},{4,12},{8,16},{12,20},{16,24},{20,28},{1,9},{5,13},{9,17},{1... | collective-permute-start | bytes 798728 | tf_op jit(solution)/shard_map/ppermute | solution.py:192
  146.2 35.9 %collective-permute-start.3 = (bf16[128,512]{1,0:T(8,128)(2,1)}, bf16[128,512]{1,0:T(8,128)(2,1)}, u32[]{:S(2)}, u32[]{:S(2)}) collective-permute-start(bf16[128,512]{1,0:T(8,128)(2,1)} %get-tuple-element.70), channel_id=1, source_target_pairs={{0,1},{1,2},{2,3},{3,0},{4,5},{5,6},{6,7},{7,4},{8,9},{9,10},{10,1... | collective-permute-start | bytes 393224 | tf_op jit(solution)/shard_map/ppermute | solution.py:175
  146.9 36.8 %collective-permute-start.4 = (bf16[128,512]{1,0:T(8,128)(2,1)}, bf16[128,512]{1,0:T(8,128)(2,1)}, u32[]{:S(2)}, u32[]{:S(2)}) collective-permute-start(bf16[128,512]{1,0:T(8,128)(2,1)} %get-tuple-element.69), channel_id=1, source_target_pairs={{0,2},{1,3},{2,0},{3,1},{4,6},{5,7},{6,4},{7,5},{8,10},{9,11},{10,... | collective-permute-start | bytes 393224 | tf_op jit(solution)/shard_map/ppermute | solution.py:175
  148.1 37.1 %collective-permute-start.5 = (bf16[128,512]{1,0:T(8,128)(2,1)}, bf16[128,512]{1,0:T(8,128)(2,1)S(1)}, u32[]{:S(2)}, u32[]{:S(2)}) collective-permute-start(bf16[128,512]{1,0:T(8,128)(2,1)} %get-tuple-element.68), channel_id=1, source_target_pairs={{0,3},{1,0},{2,1},{3,2},{4,7},{5,4},{6,5},{7,6},{8,11},{9,8},{10,9... | collective-permute-start | bytes 393224 | tf_op jit(solution)/shard_map/ppermute | solution.py:175
  150.8 8.1 %copy-start.7 = (bf16[128,2048]{1,0:T(8,128)(2,1)}, bf16[128,2048]{1,0:T(8,128)(2,1)S(1)}, u32[]{:S(2)}) copy-start(bf16[128,2048]{1,0:T(8,128)(2,1)S(1)} %bitcast_dynamic-update-slice_fusion.1) | copy-start | bytes 1572868
  153.8 3.5 %copy-start.8 = (f32[520,128]{1,0:T(8,128)}, f32[520,128]{1,0:T(8,128)S(1)}, u32[]{:S(2)}) copy-start(f32[520,128]{1,0:T(8,128)S(1)} %collective-permute-done.6) | copy-start | bytes 798724
  156.7 1.5 copy-start.9
  156.7 1.5 copy-start.15
  158.9 9.7 %collective-permute-start.8 = (f32[520,128]{1,0:T(8,128)}, f32[520,128]{1,0:T(8,128)}, u32[]{:S(2)}, u32[]{:S(2)}) collective-permute-start(f32[520,128]{1,0:T(8,128)} %select_maximum_fusion.1), channel_id=1, source_target_pairs={{4,12},{8,16},{12,20},{16,24},{20,28},{5,13},{9,17},{13,21},{17,25... | collective-permute-start | bytes 798728 | tf_op jit(solution)/shard_map/ppermute | solution.py:192
  169.8 22.5 %copy-start.13 = (f32[4]{0:T(128)}, f32[4]{0:T(128)S(1)}, u32[]{:S(2)}) copy-start(f32[4]{0:T(128)S(1)} %get-tuple-element.41) | copy-start | bytes 52
  173.0 17.6 %collective-permute-start.9 = (f32[520,128]{1,0:T(8,128)}, f32[520,128]{1,0:T(8,128)}, u32[]{:S(2)}, u32[]{:S(2)}) collective-permute-start(f32[520,128]{1,0:T(8,128)} %select_maximum_fusion), channel_id=1, source_target_pairs={{4,20},{8,24},{12,28},{5,21},{9,25},{13,29},{6,22},{10,26},{14,30}... | collective-permute-start | bytes 798728 | tf_op jit(solution)/shard_map/ppermute | solution.py:192
  200.0 10.9 %collective-permute-start.10 = (bf16[128,512]{1,0:T(8,128)(2,1)}, bf16[128,512]{1,0:T(8,128)(2,1)}, u32[]{:S(2)}, u32[]{:S(2)}) collective-permute-start(bf16[128,512]{1,0:T(8,128)(2,1)} %bitcast.218), channel_id=1, source_target_pairs={{0,1},{1,2},{2,3},{3,0},{4,5},{5,6},{6,7},{7,4},{8,9},{9,10},{10,1... | collective-permute-start | bytes 393224 | tf_op jit(solution)/shard_map/ppermute | solution.py:175
  204.8 9.8 %collective-permute-start.11 = (bf16[128,512]{1,0:T(8,128)(2,1)}, bf16[128,512]{1,0:T(8,128)(2,1)S(1)}, u32[]{:S(2)}, u32[]{:S(2)}) collective-permute-start(bf16[128,512]{1,0:T(8,128)(2,1)} %bitcast.217), channel_id=1, source_target_pairs={{0,2},{1,3},{2,0},{3,1},{4,6},{5,7},{6,4},{7,5},{8,10},{9,11},{10,... | collective-permute-start | bytes 393224 | tf_op jit(solution)/shard_map/ppermute | solution.py:175
  210.1 5.2 %collective-permute-start.12 = (bf16[128,512]{1,0:T(8,128)(2,1)}, bf16[128,512]{1,0:T(8,128)(2,1)S(1)}, u32[]{:S(2)}, u32[]{:S(2)}) collective-permute-start(bf16[128,512]{1,0:T(8,128)(2,1)} %bitcast.216), channel_id=1, source_target_pairs={{0,3},{1,0},{2,1},{3,2},{4,7},{5,4},{6,5},{7,6},{8,11},{9,8},{10,9... | collective-permute-start | bytes 393224 | tf_op jit(solution)/shard_map/ppermute | solution.py:175
  (2 other events, 1.3 us)
